TPU v7x, 512 devices: a whole 4x8x8 slice. The times are simulated.
512 devices in a mesh: ta: 32 (over y, x), pb: 16 (over z, core).
Axes of the slice: x: 4, y: 8, z: 8, core: 2. Of those that a mesh axis runs over, the one named last changes fastest.
Arguments:
- particles: float32 [2, 2097152], P(None, ('ta', 'pb')), may hold values from -6 to 6
- weights: bfloat16 [2097152], P(('ta', 'pb')), may hold values from 0.5 to 2
- cell_index: int32 [2097152], P(('ta', 'pb')), may hold values from 0 to 9215
- target_group: int32 [2097152, 1], P(('ta', 'pb')), may hold values from 0 to 31; in each aligned block of 4096 rows (0 to 4095, 4096 to 8191, ...) at most 256 rows name the same one
- target_slice: int32 [2097152], P(('ta', 'pb')), may hold values from 0 to 3
- laser_x: float32 [96], replicated, may hold values from 0.3 to 1.5
- laser_y: float32 [96], replicated, may hold values from 0.3 to 1.5
- mode_x: float32 [96], replicated, may hold values from 0.3 to 1.5
- mode_y: float32 [96], replicated, may hold values from 0.3 to 1.5
- along_coeff: float32 [96, 96], replicated, may hold values from 0.2 to 2
- across_coeff: float32 [96, 96], replicated, may hold values from 0.1 to 1
Outputs:
- arrivals: float32 [2, 4194304], P(None, ('ta', 'pb'))
- radiation: float32 [2, 128], P(None, 'ta')
Inputs may be any that keep to these rules, and one draw needn't show every extreme that they name: `target_group`: in the rows of one device at most 256 rows name the same group, and in every draw some group is named by exactly 256 rows of some device.
All inputs are finite; a program needn't handle non-finite values.
Results may differ from a plain program's by a relative error of at most 0.0009.
Values sent between devices are 32-bit elements; how exact they have to be, the bound alone decides.
No kernel may reach another device: no remote copies, remote signals or barrier semaphores. Data moves between devices by JAX's collectives and lax.ppermute only.
A program may use at most 64 MiB of HBM per device.

v0:
```python
import math

import jax
import jax.numpy as jnp
from jax import lax
from jax.sharding import PartitionSpec as P

SL_DEV = 4
PS_DEV = 1024
HARM = 48
PERIODS = 2


DISPERSION = 3.0
LASER_GAIN = 1.0
KICK_GAIN = 0.5
SLIP_GAIN = 0.05


def with_halo(x, sides, width):
    for axis, dim in sides:
        peers, length = (lax.axis_size(axis), x.shape[dim])
        up = [(i, (i + 1) % peers) for i in range(peers - 1)]
        down = [(j, i) for i, j in up]
        last = lax.slice_in_dim(x, length - width, length, axis=dim)
        leading = lax.slice_in_dim(x, 0, width, axis=dim)
        before = lax.ppermute(last, axis, up)
        after = lax.ppermute(leading, axis, down)
        x = jnp.concatenate([before, x, after], axis=dim)
    return x


def shifted(value, axis, steps):
    count = lax.axis_size(axis)
    leading, last = (max(0, -steps), min(count, count - steps))
    return lax.ppermute(value, axis, [(source, source + steps) for source in range(leading, last)])


def lookup(values_table, positions):
    matches = positions[None, :] == jnp.arange(values_table.shape[0], dtype=jnp.int32)[:, None]
    return jnp.sum(jnp.where(matches, values_table[:, None], 0.0), axis=0)


def arrival_slots(destination, groups):
    count = destination.shape[0]
    block_size = math.gcd(count, 512)
    turn_count = count // block_size
    onehot = (destination[:, None] == jnp.arange(groups, dtype=jnp.int32)[None, :]).astype(
        jnp.bfloat16
    )
    onehot = onehot.reshape(turn_count, block_size, groups)
    earlier = (jnp.arange(block_size)[:, None] > jnp.arange(block_size)[None, :]).astype(
        jnp.bfloat16
    )

    def count_step(counted, onehot_rows):
        before = (
            jnp.dot(earlier, onehot_rows, preferred_element_type=jnp.float32) + counted[None, :]
        )
        rows_f = onehot_rows.astype(jnp.float32)
        return (counted + jnp.sum(rows_f, axis=0), jnp.sum(before * rows_f, axis=1))

    _, arrival = lax.scan(count_step, jnp.zeros((groups,), jnp.float32), onehot)
    return arrival.reshape(count).astype(jnp.int32)


def deposit(arrived_weight, got_slice, got_cell, slice_count, grid_x, grid_y):
    slot_count = arrived_weight.shape[0]
    block_size = math.gcd(slot_count, 2048)
    turn_count = slot_count // block_size
    block_items = (
        arrived_weight.reshape(turn_count, block_size),
        got_slice.reshape(turn_count, block_size),
        got_cell.reshape(turn_count, block_size),
    )

    def deposit_step(running, items):
        block_weight, block_slice, block_cell = items
        on_slice = block_slice[None, :] == jnp.arange(slice_count, dtype=jnp.int32)[:, None]
        on_row = (block_cell // grid_y)[None, :] == jnp.arange(grid_x, dtype=jnp.int32)[:, None]
        left = jnp.where(
            on_slice[:, None, :] & on_row[None, :, :],
            block_weight[None, None, :],
            jnp.zeros((), jnp.bfloat16),
        )
        left = left.reshape(slice_count * grid_x, block_size)
        right = (
            (block_cell % grid_y)[:, None] == jnp.arange(grid_y, dtype=jnp.int32)[None, :]
        ).astype(jnp.bfloat16)
        return (running + jnp.dot(left, right, preferred_element_type=jnp.float32), None)

    running, _ = lax.scan(
        deposit_step, jnp.zeros((slice_count * grid_x, grid_y), jnp.float32), block_items
    )
    return running.reshape(slice_count, grid_x * grid_y)


def stencil(extended, sideways, coeff_long, coeff_cross, grid_y):
    centre = sideways[:, grid_y:-grid_y]
    along_diff = extended[2:] - extended[:-2]
    across = sideways[:, 2 * grid_y :] + sideways[:, : -2 * grid_y]
    column = jnp.arange(centre.shape[1], dtype=jnp.int32) % grid_y
    upper_y = jnp.where(column < grid_y - 1, jnp.pad(centre, ((0, 0), (0, 1)))[:, 1:], 0.0)
    lower_y = jnp.where(column > 0, jnp.pad(centre, ((0, 0), (1, 0)))[:, :-1], 0.0)
    return coeff_long[None, :] * along_diff + coeff_cross[None, :] * (
        4.0 * centre - across - upper_y - lower_y
    )


def body(
    particles,
    weights,
    cell_index,
    target_group,
    target_slice,
    laser_x,
    laser_y,
    mode_x,
    mode_y,
    along_coeff,
    across_coeff,
):
    groups = lax.axis_size("ta")
    splits = lax.axis_size("pb")
    grid_x = laser_x.shape[0]
    grid_y = laser_y.shape[0]
    cell_count = grid_x * grid_y
    per_device = particles.shape[1]
    capacity = 2 * per_device // groups
    slot_count = groups * capacity
    row_x = cell_index // grid_y
    row_y = cell_index % grid_y
    energy = particles[1] + LASER_GAIN * lookup(laser_x, row_x) * lookup(laser_y, row_y) * jnp.sin(
        particles[0]
    )
    phases = particles[0] + DISPERSION * energy
    destination = target_group[:, 0]
    position = destination * capacity + arrival_slots(destination, groups)
    send_float = (
        jnp.zeros((3, slot_count), jnp.float32)
        .at[:, position]
        .set(jnp.stack([phases, energy, weights.astype(jnp.float32)]))
    )
    send_index = (
        jnp.zeros((1, slot_count), jnp.int32)
        .at[0, position]
        .set(target_slice * cell_count + cell_index)
    )
    got_float, got_index = (
        lax.all_to_all(
            send_float.reshape(3, groups, capacity), "ta", split_axis=1, concat_axis=1, tiled=True
        ),
        lax.all_to_all(
            send_index.reshape(1, groups, capacity), "ta", split_axis=1, concat_axis=1, tiled=True
        ),
    )
    got_float = got_float.reshape(3, slot_count)
    combined = got_index.reshape(slot_count)
    arrived_weight = got_float[2]
    got_slice = combined // cell_count
    got_cell = combined % cell_count
    partial_value = deposit(
        arrived_weight.astype(jnp.bfloat16), got_slice, got_cell, SL_DEV, grid_x, grid_y
    )
    long_flat = along_coeff.reshape(cell_count)
    cross_flat = across_coeff.reshape(cell_count)
    summed = lax.psum(partial_value, "pb")
    extended = with_halo(summed, (("ta", 0),), 1)
    sideways = jnp.pad(extended[1:-1], ((0, 0), (grid_y, grid_y)))
    force_map = stencil(extended, sideways, long_flat, cross_flat, grid_y)
    kicked = got_float[1] + jnp.take(force_map.reshape(-1), combined)
    got_phase = got_float[0]
    profile = lookup(mode_x, got_cell // grid_y) * lookup(mode_y, got_cell % grid_y)
    weighted = arrived_weight * profile
    select = (got_slice[None, :] == jnp.arange(SL_DEV, dtype=jnp.int32)[:, None]).astype(
        jnp.float32
    )
    couple = 1.0 / math.sqrt(splits * PS_DEV)
    radiation = jnp.zeros((2, SL_DEV), jnp.float32)
    for period in range(PERIODS):
        harmonic_phase = HARM * got_phase
        cosine = jnp.cos(harmonic_phase)
        sine_part = jnp.sin(harmonic_phase)
        local_sums = jnp.stack(
            [
                jnp.sum(select * (weighted * cosine)[None, :], axis=1),
                jnp.sum(select * (-weighted * sine_part)[None, :], axis=1),
            ]
        )
        bunching = lax.psum(local_sums, "pb")
        radiation = radiation + couple * bunching
        real_here = jnp.sum(select * radiation[0][:, None], axis=0)
        imag_here = jnp.sum(select * radiation[1][:, None], axis=0)
        kicked = kicked + KICK_GAIN * profile * (real_here * cosine - imag_here * sine_part)
        got_phase = got_phase + SLIP_GAIN * kicked
        incoming = shifted(radiation[:, -1:], "ta", 1)
        radiation = jnp.concatenate([incoming, radiation[:, :-1]], axis=1)
    filled = arrived_weight > 0
    result = jnp.stack([jnp.where(filled, got_phase, 0.0), jnp.where(filled, kicked, 0.0)])
    return (result, radiation)


def solution(mesh):
    return jax.shard_map(
        body,
        mesh=mesh,
        in_specs=(
            P(None, ("ta", "pb")),
            P(("ta", "pb")),
            P(("ta", "pb")),
            P(("ta", "pb"), None),
            P(("ta", "pb")),
            P(),
            P(),
            P(),
            P(),
            P(),
            P(),
        ),
        out_specs=(P(None, ("ta", "pb")), P(None, "ta")),
        check_vma=False,
    )
```

profile of v0, /device:TPU:32, one launch (start us, length us, event | category | flops | bytes accessed | tf_op | source)
XLA Modules:
  0.0 320.8 jit_solution(3291533808186617567)
XLA Ops:
  7.8 1.4 reduce.17
  9.3 4.0 %while.26 = (s32[]{:T(128)}, f32[32]{0:T(128)S(1)}, f32[8,512]{1,0:T(8,128)S(1)}, bf16[8,512,32]{1,2,0:T(8,128)(2,1)S(1)}, s32[]{:T(128)}, /*index=5*/s32[]{:T(128)}) while((s32[]{:T(128)}, f32[32]{0:T(128)S(1)}, f32[8,512]{1,0:T(8,128)S(1)}, bf16[8,512,32]{1,2,0:T(8,128)(2,1)S(1)}, s32[]{:T(128)}, /*index=5*/s32[]{:T(128)}) %tuple.81), condition=%wide.region_3.4_spmd.clone, body=%wide.region_0.3_spmd.clone.sunk | while | flops 17399332 | bytes 106719 | solution.py:63
  13.7 16.1 %scatter_custom_fusion.1 = s32[8192]{0:T(1024)} fusion(s32[4096]{0:T(1024)S(1)} %broadcast_select_fusion.2, s32[4096]{0:T(1024)S(1)} %get-tuple-element.186, s32[]{:T(128)} %constant.147.clone.1), kind=kCustom, calls=%fused_computation.109 | custom fusion | bytes 32772
  29.8 9.8 %all-to-all-start.1 = ((s32[1,32,256]{2,0,1:T(1,128)}), s32[1,32,256]{2,0,1:T(1,128)S(1)}, u32[]{:S(2)}, u32[]{:S(2)}) async-start(s32[1,32,256]{2,0,1:T(1,128)} %bitcast.8), calls=%async_computation.1 | async-start | bytes 65536 | tf_op jit(solution)/shard_map/all_to_all | solution.py:153
  39.7 0.5 select_reduce_fusion.2
  40.8 0.6 copy.23
  41.4 12.8 %scatter_custom_fusion = f32[3,8192]{0,1:T(8,128)} fusion(s32[4096]{0:T(1024)S(1)} %bitcast.101, f32[4096,3]{1,0:T(8,128)S(1)} %copy.23, f32[]{:T(128)} %constant.145.clone.1), kind=kCustom, calls=%fused_computation.31 | custom fusion | bytes 98308 | tf_op jit(solution)/shard_map/scatter | solution.py:142
  54.2 3.5 %copy.24 = f32[3,32,256]{2,0,1:T(4,128)} copy(f32[3,32,256]{0,2,1:T(8,128)} %bitcast.82) | data formatting | bytes 196608 | tf_op jit(solution)/shard_map/reshape | solution.py:151
  57.9 9.8 %all-to-all-start = ((f32[3,32,256]{2,0,1:T(4,128)}), f32[3,32,256]{2,0,1:T(4,128)S(1)}, u32[]{:S(2)}, u32[]{:S(2)}) async-start(f32[3,32,256]{2,0,1:T(4,128)} %copy.24), calls=%async_computation | async-start | bytes 262144 | tf_op jit(solution)/shard_map/all_to_all | solution.py:150
  68.4 1.0 select_reduce_fusion
  69.4 4.2 %all-to-all-done = f32[3,32,256]{2,0,1:T(4,128)S(1)} async-done(((f32[3,32,256]{2,0,1:T(4,128)}), f32[3,32,256]{2,0,1:T(4,128)S(1)}, u32[]{:S(2)}, u32[]{:S(2)}) %all-to-all-start) | async-done | bytes 98336 | tf_op jit(solution)/shard_map/all_to_all | solution.py:150
  74.2 30.3 %psum.22 = f32[2,4]{1,0:T(2,128)S(1)} all-reduce(f32[2,4]{1,0:T(2,128)S(1)} %pad_maximum_fusion.3), channel_id=1, replica_groups=mesh['ta'=32,'pb'=16] {'pb'}, use_global_device_ids=true, to_apply=%region_15.16 | all-reduce | flops 8 | bytes 64 | tf_op jit(solution)/shard_map/psum | solution.py:190
  104.6 8.0 %while.27 = (s32[]{:T(128)}, f32[384,96]{0,1:T(8,128)S(1)}, s32[4,2048]{1,0:T(4,128)S(1)}, s32[4,2048]{1,0:T(4,128)S(1)}, bf16[4,2048]{1,0:T(4,128)(2,1)S(1)}, /*index=5*/s32[]{:T(128)}, s32[]{:T(128)}) while((s32[]{:T(128)}, f32[384,96]{0,1:T(8,128)S(1)}, s32[4,2048]{1,0:T(4,128)S(1)}, s32[4,2048]{1,0:T(4,128)S(1)}, ...), condition=%wide.region_9.10_spmd.clone, body=%wide.region_8.9_spmd.clone.sunk | while | flops 153069568 | bytes 5517415 | solution.py:92
  105.6 1.0 convolution_add_fusion.3
  107.6 1.0 convolution_add_fusion.3
  109.6 1.0 convolution_add_fusion.3
  111.6 1.0 convolution_add_fusion.3
  112.8 0.8 reshape.556
  113.7 2.5 collective-permute-start.2
  116.2 101.6 %all-reduce.6.cloned.1.call-done = f32[4,9216]{1,0:T(4,128)} async-done(((f32[4,9216]{1,0:T(4,128)}), f32[4,9216]{1,0:T(4,128)}) %all-reduce.6.cloned.1.call-update) | async-done | bytes 147472 | tf_op jit(solution)/shard_map/psum | solution.py:167
  217.9 1.0 fusion.37
  218.9 3.4 %collective-permute-start.1 = (f32[1,9216]{1,0:T(1,128)S(1)}, f32[1,9216]{1,0:T(1,128)S(1)}, u32[]{:S(2)}, u32[]{:S(2)}) collective-permute-start(f32[1,9216]{1,0:T(1,128)S(1)} %get-tuple-element.177), channel_id=1, source_target_pairs={{0,16},{16,32},{32,48},{48,64},{64,80},{80,96},{96,112},{112,128},... | collective-permute-start | bytes 110600 | tf_op jit(solution)/shard_map/ppermute | solution.py:27
  222.3 6.0 %collective-permute-start = (f32[1,9216]{1,0:T(1,128)S(1)}, f32[1,9216]{1,0:T(1,128)S(1)}, u32[]{:S(2)}, u32[]{:S(2)}) collective-permute-start(f32[1,9216]{1,0:T(1,128)S(1)} %get-tuple-element.176), channel_id=1, source_target_pairs={{16,0},{32,16},{48,32},{64,48},{80,64},{96,80},{112,96},{128,112},... | collective-permute-start | bytes 110600 | tf_op jit(solution)/shard_map/ppermute | solution.py:28
  228.5 1.2 collective-permute-done
  229.7 2.0 fusion.19
  231.8 45.5 %gather_fusion = f32[8192]{0:T(1024)S(1)} fusion(f32[36864]{0:T(1024)S(1)} %bitcast.81, s32[8192]{0:T(1024)S(1)} %broadcast_clamp_fusion), kind=kCustom, calls=%fused_computation | custom fusion | bytes 98304 | tf_op jit(solution)/shard_map/jit(_take)/gather | solution.py:171
  278.0 23.5 %psum.23 = f32[2,4]{1,0:T(2,128)S(1)} all-reduce(f32[2,4]{1,0:T(2,128)S(1)} %pad_maximum_fusion.4), channel_id=1, replica_groups=mesh['ta'=32,'pb'=16] {'pb'}, use_global_device_ids=true, to_apply=%region_20.21 | all-reduce | flops 8 | bytes 64 | tf_op jit(solution)/shard_map/psum | solution.py:190
  301.9 2.2 add_select_fusion.8
  304.3 1.9 collective-permute-start.3
  306.2 0.7 pad_maximum_fusion.2
  306.9 6.5 %collective-permute-done.3 = f32[2,1]{1,0:T(2,128)S(1)} collective-permute-done((f32[2,1]{1,0:T(2,128)S(1)}, f32[2,1]{1,0:T(2,128)S(1)}, u32[]{:S(2)}, u32[]{:S(2)}) %collective-permute-start.3) | collective-permute-done | bytes 40 | tf_op jit(solution)/shard_map/ppermute | solution.py:36
  313.4 0.6 pad_maximum_fusion.5
  (143 shorter events, 11.9 us)
Async XLA Ops:
  7.2 6.2 %copy-start.12 = (s32[2]{0:T(128)S(1)}, s32[2]{0:T(128)}, u32[]{:S(2)}) copy-start(s32[2]{0:T(128)} %constant.174) | copy-start | bytes 28
  7.2 6.3 %copy-start.11 = (s32[2]{0:T(128)S(1)}, s32[2]{0:T(128)}, u32[]{:S(2)}) copy-start(s32[2]{0:T(128)} %constant.171) | copy-start | bytes 28
  7.2 6.1 %copy-start = (s32[4096,1]{0,1:T(1,128)S(1)}, s32[4096,1]{0,1:T(1,128)}, u32[]{:S(2)}) copy-start(s32[4096,1]{0,1:T(1,128)} %param.18) | copy-start | bytes 49156
  7.2 6.4 %copy-start.4 = (s32[4096]{0:T(1024)S(1)}, s32[4096]{0:T(1024)}, u32[]{:S(2)}) copy-start(s32[4096]{0:T(1024)} %param.17) | copy-start | bytes 49156
  7.2 6.4 %copy-start.5 = (s32[4096]{0:T(1024)S(1)}, s32[4096]{0:T(1024)}, u32[]{:S(2)}) copy-start(s32[4096]{0:T(1024)} %param.19) | copy-start | bytes 49156
  7.2 32.4 %copy-start.6 = (bf16[4096]{0:T(1024)(128)(2,1)S(1)}, bf16[4096]{0:T(1024)(128)(2,1)}, u32[]{:S(2)}) copy-start(bf16[4096]{0:T(1024)(128)(2,1)} %param.16) | copy-start | bytes 24580
  7.2 32.4 %copy-start.7 = (f32[96]{0:T(128)S(1)}, f32[96]{0:T(128)}, u32[]{:S(2)}) copy-start(f32[96]{0:T(128)} %param.21) | copy-start | bytes 1156
  7.2 32.4 %copy-start.8 = (f32[96]{0:T(128)S(1)}, f32[96]{0:T(128)}, u32[]{:S(2)}) copy-start(f32[96]{0:T(128)} %param.20) | copy-start | bytes 1156
  7.3 33.0 %copy-start.3 = (f32[2,4096]{1,0:T(2,128)S(1)}, f32[2,4096]{1,0:T(2,128)}, u32[]{:S(2)}) copy-start(f32[2,4096]{1,0:T(2,128)} %param.15) | copy-start | bytes 98308
  29.8 28.1 %all-to-all-start.1 = ((s32[1,32,256]{2,0,1:T(1,128)}), s32[1,32,256]{2,0,1:T(1,128)S(1)}, u32[]{:S(2)}, u32[]{:S(2)}) async-start(s32[1,32,256]{2,0,1:T(1,128)} %bitcast.8), calls=%async_computation.1 | async-start | bytes 65536 | tf_op jit(solution)/shard_map/all_to_all | solution.py:153
  54.2 3.5 %copy-start.1 = (f32[96,96]{1,0:T(8,128)S(1)}, f32[96,96]{1,0:T(8,128)}, u32[]{:S(2)}) copy-start(f32[96,96]{1,0:T(8,128)} %param.25) | copy-start | bytes 110596
  54.2 3.6 %copy-start.2 = (f32[96,96]{1,0:T(8,128)S(1)}, f32[96,96]{1,0:T(8,128)}, u32[]{:S(2)}) copy-start(f32[96,96]{1,0:T(8,128)} %param.24) | copy-start | bytes 110596
  54.2 14.2 %copy-start.9 = (f32[96]{0:T(128)S(1)}, f32[96]{0:T(128)}, u32[]{:S(2)}) copy-start(f32[96]{0:T(128)} %param.23) | copy-start | bytes 1156
  54.2 14.2 %copy-start.10 = (f32[96]{0:T(128)S(1)}, f32[96]{0:T(128)}, u32[]{:S(2)}) copy-start(f32[96]{0:T(128)} %param.22) | copy-start | bytes 1156
  57.9 15.7 %all-to-all-start = ((f32[3,32,256]{2,0,1:T(4,128)}), f32[3,32,256]{2,0,1:T(4,128)S(1)}, u32[]{:S(2)}, u32[]{:S(2)}) async-start(f32[3,32,256]{2,0,1:T(4,128)} %copy.24), calls=%async_computation | async-start | bytes 262144 | tf_op jit(solution)/shard_map/all_to_all | solution.py:150
  67.7 150.2 %all-reduce.6.cloned.1.call-start = ((), (), s32[]{:S(2)}) async-start(), calls=%async_computation.2 | async-start | bytes 294912 | tf_op jit(solution)/shard_map/psum | solution.py:167
  113.7 187.8 %collective-permute-start.2 = (f32[2,1]{1,0:T(2,128)S(1)}, f32[2,1]{1,0:T(2,128)S(1)}, u32[]{:S(2)}, u32[]{:S(2)}) collective-permute-start(f32[2,1]{1,0:T(2,128)S(1)} %slice.85), channel_id=1, source_target_pairs={{0,16},{16,32},{32,48},{48,64},{64,80},{80,96},{96,112},{112,128},... | collective-permute-start | bytes 32 | tf_op jit(solution)/shard_map/ppermute | solution.py:36
  218.9 9.6 %collective-permute-start.1 = (f32[1,9216]{1,0:T(1,128)S(1)}, f32[1,9216]{1,0:T(1,128)S(1)}, u32[]{:S(2)}, u32[]{:S(2)}) collective-permute-start(f32[1,9216]{1,0:T(1,128)S(1)} %get-tuple-element.177), channel_id=1, source_target_pairs={{0,16},{16,32},{32,48},{48,64},{64,80},{80,96},{96,112},{112,128},... | collective-permute-start | bytes 110600 | tf_op jit(solution)/shard_map/ppermute | solution.py:27
  222.3 7.4 %collective-permute-start = (f32[1,9216]{1,0:T(1,128)S(1)}, f32[1,9216]{1,0:T(1,128)S(1)}, u32[]{:S(2)}, u32[]{:S(2)}) collective-permute-start(f32[1,9216]{1,0:T(1,128)S(1)} %get-tuple-element.176), channel_id=1, source_target_pairs={{16,0},{32,16},{48,32},{64,48},{80,64},{96,80},{112,96},{128,112},... | collective-permute-start | bytes 110600 | tf_op jit(solution)/shard_map/ppermute | solution.py:28
  304.3 9.1 %collective-permute-start.3 = (f32[2,1]{1,0:T(2,128)S(1)}, f32[2,1]{1,0:T(2,128)S(1)}, u32[]{:S(2)}, u32[]{:S(2)}) collective-permute-start(f32[2,1]{1,0:T(2,128)S(1)} %slice.89), channel_id=1, source_target_pairs={{0,16},{16,32},{32,48},{48,64},{64,80},{80,96},{96,112},{112,128},... | collective-permute-start | bytes 32 | tf_op jit(solution)/shard_map/ppermute | solution.py:36
Sparse Core Ops, SparseCore 0:
  113.8 104.0 all-reduce.5
where the time goes:
time: 321 us
  waiting for transfers between devices  114 us (36%)
  local copies, waits for them, and re-layouts  82.4 us (26%)
  blocking collectives  53.8 us (17%)
  starting transfers between devices  33.4 us (10%)
  other arithmetic  16.3 us (5%)
  between operations  14.6 us (5%)
  matrix products  6.37 us (2%)
    psum x1, waiting for transfers between devices, body(): summed = lax.psum(partial_value, 'pb')  102 us
    psum x2, blocking collectives, body(): bunching = lax.psum(local_sums, 'pb')  53.8 us
    gather x1, local copies, waits for them, and re-layouts, body(): kicked = got_float[1] + jnp.take(force_map.reshape(-1), combined)  45.5 us
    unnamed x30, local copies, waits for them, and re-layouts  16.7 us
    scatter x1, local copies, waits for them, and re-layouts, body(): send_float = jnp.zeros((3, slot_count), jnp.float32).at[:, position].set(...  12.8 us
    all_to_all x1, starting transfers between devices, body(): lax.all_to_all(send_index.reshape(1, groups, capacity), 'ta', split_axis=...  9.83 us
    all_to_all x1, starting transfers between devices, body(): lax.all_to_all(send_float.reshape(3, groups, capacity), 'ta', split_axis=...  9.79 us
    ppermute x2, waiting for transfers between devices, shifted(): lax.ppermute(value, axis, [(source, source + steps) for source in range(l...  6.48 us
  transfers between devices with their start and end apart: 7, of which 4 were waited for; matrix products, arithmetic and copies ran while one was open for 22% of the time, Pallas kernels for 0%

commit v1 on v0

v1 whole, which is shorter than its diff:
```python
import math

import jax
import jax.numpy as jnp
from jax import lax
from jax.sharding import PartitionSpec as P

SL_DEV = 4
PS_DEV = 1024
HARM = 48
PERIODS = 2


DISPERSION = 3.0
LASER_GAIN = 1.0
KICK_GAIN = 0.5
SLIP_GAIN = 0.05


def shifted(value, axis, steps):
    count = lax.axis_size(axis)
    leading, last = (max(0, -steps), min(count, count - steps))
    return lax.ppermute(value, axis, [(source, source + steps) for source in range(leading, last)])


def lookup(values_table, positions):
    matches = positions[None, :] == jnp.arange(values_table.shape[0], dtype=jnp.int32)[:, None]
    return jnp.sum(jnp.where(matches, values_table[:, None], 0.0), axis=0)


def split3(x):
    hi = lax.reduce_precision(x, exponent_bits=8, mantissa_bits=7)
    rest = x - hi
    mid = lax.reduce_precision(rest, exponent_bits=8, mantissa_bits=7)
    lo = rest - mid
    return [part.astype(jnp.bfloat16) for part in (hi, mid, lo)]


def arrival_slots(destination, groups):
    count = destination.shape[0]
    block_size = math.gcd(count, 512)
    turn_count = count // block_size
    onehot = (destination[:, None] == jnp.arange(groups, dtype=jnp.int32)[None, :]).astype(
        jnp.bfloat16
    )
    onehot = onehot.reshape(turn_count, block_size, groups)
    earlier = (jnp.arange(block_size)[:, None] > jnp.arange(block_size)[None, :]).astype(
        jnp.bfloat16
    )

    def count_step(counted, onehot_rows):
        before = (
            jnp.dot(earlier, onehot_rows, preferred_element_type=jnp.float32) + counted[None, :]
        )
        rows_f = onehot_rows.astype(jnp.float32)
        return (counted + jnp.sum(rows_f, axis=0), jnp.sum(before * rows_f, axis=1))

    _, arrival = lax.scan(count_step, jnp.zeros((groups,), jnp.float32), onehot)
    return arrival.reshape(count).astype(jnp.int32)


def deposit_rows(weight_bf16, row_key, col, targets, grid_y):
    left = jnp.where(
        row_key[None, :] == targets[:, None], weight_bf16[None, :], jnp.zeros((), jnp.bfloat16)
    )
    right = (col[:, None] == jnp.arange(grid_y, dtype=jnp.int32)[None, :]).astype(jnp.bfloat16)
    return jnp.dot(left, right, preferred_element_type=jnp.float32)


def pb_sum(flat, axis):
    count = lax.axis_size(axis)
    chunks = flat.reshape(count, -1)
    mine = jnp.sum(lax.all_to_all(chunks, axis, 0, 0, tiled=True), axis=0)
    every = lax.all_to_all(jnp.broadcast_to(mine[None], chunks.shape), axis, 0, 0, tiled=True)
    return every.reshape(-1)


def pb_sum_small(value, axis):
    count = lax.axis_size(axis)
    spread = jnp.broadcast_to(value[None], (count,) + value.shape)
    return jnp.sum(lax.all_to_all(spread, axis, 0, 0, tiled=True), axis=0)


def stencil(extended, sideways, coeff_long, coeff_cross, grid_y):
    centre = sideways[:, grid_y:-grid_y]
    along_diff = extended[2:] - extended[:-2]
    across = sideways[:, 2 * grid_y :] + sideways[:, : -2 * grid_y]
    column = jnp.arange(centre.shape[1], dtype=jnp.int32) % grid_y
    upper_y = jnp.where(column < grid_y - 1, jnp.pad(centre, ((0, 0), (0, 1)))[:, 1:], 0.0)
    lower_y = jnp.where(column > 0, jnp.pad(centre, ((0, 0), (1, 0)))[:, :-1], 0.0)
    return coeff_long[None, :] * along_diff + coeff_cross[None, :] * (
        4.0 * centre - across - upper_y - lower_y
    )


def body(
    particles,
    weights,
    cell_index,
    target_group,
    target_slice,
    laser_x,
    laser_y,
    mode_x,
    mode_y,
    along_coeff,
    across_coeff,
):
    groups = lax.axis_size("ta")
    splits = lax.axis_size("pb")
    grid_x = laser_x.shape[0]
    grid_y = laser_y.shape[0]
    cell_count = grid_x * grid_y
    per_device = particles.shape[1]
    capacity = 2 * per_device // groups
    slot_count = groups * capacity
    row_x = cell_index // grid_y
    row_y = cell_index % grid_y
    energy = particles[1] + LASER_GAIN * lookup(laser_x, row_x) * lookup(laser_y, row_y) * jnp.sin(
        particles[0]
    )
    phases = particles[0] + DISPERSION * energy
    destination = target_group[:, 0]
    arrival = arrival_slots(destination, groups)

    values = jnp.stack(
        [
            phases,
            energy,
            weights.astype(jnp.float32),
            (target_slice * cell_count + cell_index).astype(jnp.float32),
        ]
    )
    value_count = values.shape[0]
    to_group = destination[None, :] == jnp.arange(groups, dtype=jnp.int32)[:, None]
    parts = split3(values)
    left = jnp.concatenate(
        [
            jnp.where(to_group[None], part[:, None, :], jnp.zeros((), jnp.bfloat16)).reshape(
                value_count * groups, per_device
            )
            for part in parts
        ]
    )
    to_slot = (arrival[:, None] == jnp.arange(capacity, dtype=jnp.int32)[None, :]).astype(
        jnp.bfloat16
    )
    placed = jnp.dot(left, to_slot, preferred_element_type=jnp.float32)
    rows = value_count * groups
    send = (placed[:rows] + placed[rows : 2 * rows]) + placed[2 * rows :]
    got = lax.all_to_all(
        send.reshape(value_count, groups, capacity), "ta", split_axis=1, concat_axis=1, tiled=True
    ).reshape(value_count, slot_count)

    got_phase = got[0]
    got_energy = got[1]
    arrived_weight = got[2]
    combined = got[3].astype(jnp.int32)
    got_slice = combined // cell_count
    got_cell = combined % cell_count
    got_x = got_cell // grid_y
    got_y = got_cell % grid_y
    row_key = got_slice * grid_x + got_x
    weight_bf16 = arrived_weight.astype(jnp.bfloat16)

    edge_targets = jnp.concatenate(
        [
            jnp.arange(grid_x, dtype=jnp.int32),
            jnp.arange(grid_x, dtype=jnp.int32) + (SL_DEV - 1) * grid_x,
        ]
    )
    edges = deposit_rows(weight_bf16, row_key, got_y, edge_targets, grid_y).reshape(2, cell_count)
    below = shifted(edges[1:2], "ta", 1)
    above = shifted(edges[0:1], "ta", -1)
    middle_targets = jnp.arange(grid_x, (SL_DEV - 1) * grid_x, dtype=jnp.int32)
    middle = deposit_rows(weight_bf16, row_key, got_y, middle_targets, grid_y).reshape(
        SL_DEV - 2, cell_count
    )

    profile = lookup(mode_x, got_x) * lookup(mode_y, got_y)
    weighted = arrived_weight * profile
    select = (got_slice[None, :] == jnp.arange(SL_DEV, dtype=jnp.int32)[:, None]).astype(
        jnp.float32
    )

    def local_bunching(phase):
        harmonic_phase = HARM * phase
        cosine = jnp.cos(harmonic_phase)
        sine_part = jnp.sin(harmonic_phase)
        sums = jnp.stack(
            [
                jnp.sum(select * (weighted * cosine)[None, :], axis=1),
                jnp.sum(select * (-weighted * sine_part)[None, :], axis=1),
            ]
        )
        return cosine, sine_part, sums

    cosine0, sine0, sums0 = local_bunching(got_phase)
    stacked = jnp.concatenate(
        [below.reshape(-1), edges[0], middle.reshape(-1), edges[1], above.reshape(-1), sums0.reshape(-1)]
    )
    width = splits * 8
    padded_len = -(-stacked.shape[0] // width) * width
    stacked = jnp.pad(stacked, (0, padded_len - stacked.shape[0]))
    summed = pb_sum(stacked, "pb")
    extended = summed[: (SL_DEV + 2) * cell_count].reshape(SL_DEV + 2, cell_count)
    bunching0 = summed[(SL_DEV + 2) * cell_count : (SL_DEV + 2) * cell_count + 2 * SL_DEV].reshape(
        2, SL_DEV
    )

    long_flat = along_coeff.reshape(cell_count)
    cross_flat = across_coeff.reshape(cell_count)
    sideways = jnp.pad(extended[1:-1], ((0, 0), (grid_y, grid_y)))
    force_map = stencil(extended, sideways, long_flat, cross_flat, grid_y)

    force_rows = force_map.reshape(SL_DEV * grid_x, grid_y)
    force_parts = jnp.concatenate(split3(force_rows), axis=1)
    pick_row = (row_key[:, None] == jnp.arange(SL_DEV * grid_x, dtype=jnp.int32)[None, :]).astype(
        jnp.bfloat16
    )
    picked = jnp.dot(pick_row, force_parts, preferred_element_type=jnp.float32)
    picked = (picked[:, :grid_y] + picked[:, grid_y : 2 * grid_y]) + picked[:, 2 * grid_y :]
    pick_col = got_y[:, None] == jnp.arange(grid_y, dtype=jnp.int32)[None, :]
    kicked = got_energy + jnp.sum(jnp.where(pick_col, picked, 0.0), axis=1)

    couple = 1.0 / math.sqrt(splits * PS_DEV)
    radiation = jnp.zeros((2, SL_DEV), jnp.float32)
    for period in range(PERIODS):
        if period == 0:
            cosine, sine_part, bunching = cosine0, sine0, bunching0
        else:
            cosine, sine_part, local_sums = local_bunching(got_phase)
            bunching = pb_sum_small(local_sums, "pb")
        radiation = radiation + couple * bunching
        real_here = jnp.sum(select * radiation[0][:, None], axis=0)
        imag_here = jnp.sum(select * radiation[1][:, None], axis=0)
        kicked = kicked + KICK_GAIN * profile * (real_here * cosine - imag_here * sine_part)
        got_phase = got_phase + SLIP_GAIN * kicked
        incoming = shifted(radiation[:, -1:], "ta", 1)
        radiation = jnp.concatenate([incoming, radiation[:, :-1]], axis=1)
    filled = arrived_weight > 0
    result = jnp.stack([jnp.where(filled, got_phase, 0.0), jnp.where(filled, kicked, 0.0)])
    return (result, radiation)


def solution(mesh):
    return jax.shard_map(
        body,
        mesh=mesh,
        in_specs=(
            P(None, ("ta", "pb")),
            P(("ta", "pb")),
            P(("ta", "pb")),
            P(("ta", "pb"), None),
            P(("ta", "pb")),
            P(),
            P(),
            P(),
            P(),
            P(),
            P(),
        ),
        out_specs=(P(None, ("ta", "pb")), P(None, "ta")),
        check_vma=False,
    )
```

time: 321 us -> 119 us (0.37)
  the two profiles are of different devices: /device:TPU:32 before, /device:TPU:8 now
where the time goes in v1:
time: 119 us; the launch traced here: 118 us
  waiting for transfers between devices  30.7 us (26%)
  starting transfers between devices  29.2 us (25%)
  blocking collectives  20.7 us (17%)
  other arithmetic  16.4 us (14%)
  matrix products  10.5 us (9%)
  local copies, waits for them, and re-layouts  8.85 us (7%)
    all_to_all x1, blocking collectives, pb_sum(): mine = jnp.sum(lax.all_to_all(chunks, axis, 0, 0, tiled=True), axis=0)  20.7 us
    ppermute x4, starting transfers between devices, shifted(): lax.ppermute(value, axis, [(source, source + steps) for source in range(l...  11.8 us
    all_to_all x1, starting transfers between devices, body(): lax.all_to_all(send.reshape(value_count, groups, capacity), 'ta', split_a...  10.2 us
    all_to_all x1, waiting for transfers between devices, pb_sum(): lax.all_to_all(jnp.broadcast_to(mine[None], chunks.shape), axis, 0, 0, ti...  9.88 us
    all_to_all x1, waiting for transfers between devices, body(): lax.all_to_all(send.reshape(value_count, groups, capacity), 'ta', split_a...  9.54 us
    ppermute x4, waiting for transfers between devices, shifted(): lax.ppermute(value, axis, [(source, source + steps) for source in range(l...  5.69 us
    all_to_all x1, waiting for transfers between devices, pb_sum_small(): return jnp.sum(lax.all_to_all(spread, axis, 0, 0, tiled=True), axis=0)  5.62 us
    dot_general x1, matrix products, body(): picked = jnp.dot(pick_row, force_parts, preferred_element_type=jnp.float32)  4.05 us
  transfers between devices with their start and end apart: 7, of which 6 were waited for; matrix products, arithmetic and copies ran while one was open for 3% of the time, Pallas kernels for 0%

profile of v1, /device:TPU:8, one launch (start us, length us, event | category | flops | bytes accessed | tf_op | source)
XLA Modules:
  0.0 117.8 jit_solution(6044724486221007281)
XLA Ops:
  0.7 0.8 iota_compare_fusion.13
  1.5 0.7 stack.47
  2.7 1.4 %reduce.8 = s32[4096]{0:T(1024)S(1)} reduce(s32[4096,1]{0,1:T(1,128)} %param.16, s32[]{:T(128)} %broadcast.452), dimensions={1}, to_apply=%param.16.reduce_sub_computation.3 | reduce | bytes 32772 | tf_op args[3]
  4.1 4.0 %while.13 = (s32[]{:T(128)}, f32[32]{0:T(128)S(1)}, f32[8,512]{1,0:T(8,128)S(1)}, bf16[8,512,32]{1,2,0:T(8,128)(2,1)S(1)}, s32[]{:T(128)}, /*index=5*/s32[]{:T(128)}) while((s32[]{:T(128)}, f32[32]{0:T(128)S(1)}, f32[8,512]{1,0:T(8,128)S(1)}, bf16[8,512,32]{1,2,0:T(8,128)(2,1)S(1)}, s32[]{:T(128)}, /*index=5*/s32[]{:T(128)}) %tuple.59), condition=%wide.region_5.6_spmd.clone, body=%wide.region_2.5_spmd.clone.sunk | while | flops 17399332 | bytes 106719 | solution.py:58
  8.2 0.8 add_select_fusion.6
  8.9 1.2 %select_reduce_fusion.2 = (f32[4096]{0:T(1024)S(1)}, f32[4096]{0:T(1024)S(1)}) fusion(f32[96]{0:T(128)} %param.19, s32[4096]{0:T(1024)S(1)} %get-tuple-element.98, f32[96]{0:T(128)} %param.18, s32[4096]{0:T(1024)S(1)} %get-tuple-element.100), kind=kLoop, calls=%fused_computation.46 | loop fusion | flops 2351104 | bytes 66304 | tf_op jit(solution)/shard_map/reduce_sum | solution.py:28
  11.1 1.2 %fusion.12 = f32[384,256]{1,0:T(8,128)S(1)} fusion(bf16[128,4096]{1,0:T(8,128)(2,1)S(1)} %bitcast.63, bf16[128,4096]{1,0:T(8,128)(2,1)S(1)} %bitcast.62, bf16[128,4096]{1,0:T(8,128)(2,1)S(1)} %bitcast.61, s32[4096]{0:T(1024)S(1)} %bitcast.90), kind=kOutput, calls=%fused_computation.18 | convolution fusion | flops 815792128 | bytes 3555328 | tf_op jit(solution)/shard_map/dot_general | solution.py:148
  12.3 0.7 copy.16
  13.0 10.2 %all-to-all-start = ((f32[4,32,256]{2,0,1:T(4,128)}), f32[4,32,256]{2,0,1:T(4,128)S(1)}, u32[]{:S(2)}, u32[]{:S(2)}) async-start(f32[4,32,256]{2,0,1:T(4,128)} %copy.16), calls=%async_computation | async-start | bytes 262144 | tf_op jit(solution)/shard_map/all_to_all | solution.py:151
  23.3 9.5 %all-to-all-done = f32[4,32,256]{2,0,1:T(4,128)S(1)} async-done(((f32[4,32,256]{2,0,1:T(4,128)}), f32[4,32,256]{2,0,1:T(4,128)S(1)}, u32[]{:S(2)}, u32[]{:S(2)}) %all-to-all-start) | async-done | bytes 131104 | tf_op jit(solution)/shard_map/all_to_all | solution.py:151
  33.4 1.5 %fusion.13 = f32[192,96]{1,0:T(8,128)S(1)} fusion(s32[8192]{0:T(1024)S(1)} %get-tuple-element.72, s32[192]{0:T(256)S(1)} %pad_add_fusion, bf16[8192]{0:T(1024)(128)(2,1)S(1)} %convert_element_type.107, s32[8192]{0:T(1024)S(1)} %get-tuple-element.97), kind=kOutput, calls=%fused_computation.19 | convolution fusion | flops 305922048 | bytes 156416 | tf_op jit(solution)/shard_map/dot_general | solution.py:67
  35.4 0.6 select_reduce_fusion
  36.0 2.5 %collective-permute-start = (f32[1,9216]{1,0:T(1,128)S(1)}, f32[1,9216]{1,0:T(1,128)S(1)}, u32[]{:S(2)}, u32[]{:S(2)}) collective-permute-start(f32[1,9216]{1,0:T(1,128)S(1)} %slice.130), channel_id=1, source_target_pairs={{0,16},{16,32},{32,48},{48,64},{64,80},{80,96},{96,112},{112,128},... | collective-permute-start | bytes 110600 | tf_op jit(solution)/shard_map/ppermute | solution.py:23
  38.5 1.5 %fusion.14 = f32[192,96]{1,0:T(8,128)S(1)} fusion(s32[8192]{0:T(1024)S(1)} %get-tuple-element.72, s32[192]{0:T(256)S(1)} %iota_add_fusion, bf16[8192]{0:T(1024)(128)(2,1)S(1)} %convert_element_type.107, s32[8192]{0:T(1024)S(1)} %get-tuple-element.97), kind=kOutput, calls=%fused_computation.20 | convolution fusion | flops 305922048 | bytes 156416 | tf_op jit(solution)/shard_map/dot_general | solution.py:67
  40.1 5.5 %collective-permute-start.1 = (f32[1,9216]{1,0:T(1,128)S(1)}, f32[1,9216]{1,0:T(1,128)S(1)}, u32[]{:S(2)}, u32[]{:S(2)}) collective-permute-start(f32[1,9216]{1,0:T(1,128)S(1)} %slice.132), channel_id=1, source_target_pairs={{16,0},{32,16},{48,32},{64,48},{80,64},{96,80},{112,96},{128,112},... | collective-permute-start | bytes 110600 | tf_op jit(solution)/shard_map/ppermute | solution.py:23
  47.5 20.7 %all_to_all.25 = f32[16,1,3464]{2,1,0:T(1,128)S(1)} all-to-all(f32[16,1,3464]{2,1,0:T(1,128)S(1)} %all_to_all.17), channel_id=1, replica_groups=mesh['ta'=32,'pb'=16] {'pb'}, dimensions={0} | all-to-all | bytes 443392 | tf_op jit(solution)/shard_map/all_to_all | solution.py:73
  68.4 0.8 broadcast_in_dim.191
  69.2 3.7 %all-to-all-start.2 = ((f32[16,1,3464]{2,1,0:T(1,128)}), f32[16,1,3464]{2,1,0:T(1,128)S(1)}, u32[]{:S(2)}, u32[]{:S(2)}) async-start(f32[16,1,3464]{2,1,0:T(1,128)} %broadcast_in_dim.191), calls=%async_computation.2 | async-start | bytes 458752 | tf_op jit(solution)/shard_map/all_to_all | solution.py:74
  73.2 9.9 %all-to-all-done.2 = f32[16,1,3464]{2,1,0:T(1,128)S(1)} async-done(((f32[16,1,3464]{2,1,0:T(1,128)}), f32[16,1,3464]{2,1,0:T(1,128)S(1)}, u32[]{:S(2)}, u32[]{:S(2)}) %all-to-all-start.2) | async-done | bytes 221728 | tf_op jit(solution)/shard_map/all_to_all | solution.py:74
  83.6 3.9 %slice.144 = f32[13856,4]{1,0:T(8,128)} reshape(f32[16,3464]{1,0:T(8,128)S(1)} %reduce.3) | data formatting | bytes 443392 | tf_op jit(solution)/shard_map/slice | solution.py:207
  87.6 0.7 slice_multiply_fusion
  89.1 4.1 %fusion.10 = f32[8192,288]{0,1:T(8,128)S(1)} fusion(s32[8192]{0:T(1024)S(1)} %get-tuple-element.72, bf16[384,96]{1,0:T(8,128)(2,1)S(1)} %get-tuple-element.79, bf16[384,96]{1,0:T(8,128)(2,1)S(1)} %get-tuple-element.80, bf16[384,96]{1,0:T(8,128)(2,1)S(1)} %get-tuple-element.78), kind=kOutput, calls=%fused_computation.13 | convolution fusion | flops 1815748608 | bytes 9691136 | tf_op jit(solution)/shard_map/dot_general | solution.py:221
  93.2 0.9 fusion.16
  94.9 0.6 broadcast_in_dim.196
  95.5 3.5 %all-to-all-start.3 = ((f32[16,2,4]{2,1,0:T(2,128)}), f32[16,2,4]{2,1,0:T(2,128)S(1)}, u32[]{:S(2)}, u32[]{:S(2)}) async-start(f32[16,2,4]{2,1,0:T(2,128)} %broadcast_in_dim.196), calls=%async_computation.3 | async-start | bytes 32768 | tf_op jit(solution)/shard_map/all_to_all | solution.py:81
  99.1 1.9 %collective-permute-start.2 = (f32[2,1]{1,0:T(2,128)S(1)}, f32[2,1]{1,0:T(2,128)S(1)}, u32[]{:S(2)}, u32[]{:S(2)}) collective-permute-start(f32[2,1]{1,0:T(2,128)S(1)} %slice.148), channel_id=1, source_target_pairs={{0,16},{16,32},{32,48},{48,64},{64,80},{80,96},{96,112},{112,128},... | collective-permute-start | bytes 32 | tf_op jit(solution)/shard_map/ppermute | solution.py:23
  101.0 5.6 %all-to-all-done.3 = f32[16,2,4]{2,1,0:T(2,128)S(1)} async-done(((f32[16,2,4]{2,1,0:T(2,128)}), f32[16,2,4]{2,1,0:T(2,128)S(1)}, u32[]{:S(2)}, u32[]{:S(2)}) %all-to-all-start.3) | async-done | bytes 544 | tf_op jit(solution)/shard_map/all_to_all | solution.py:81
  107.3 2.2 %add_select_fusion.5 = (f32[1,8192]{1,0:T(1,128)S(1)}, f32[1,8192]{1,0:T(1,128)S(1)}) fusion(pred[1,8192]{1,0:T(4,128)(4,1)S(1)} %bitcast.70, f32[1,8192]{1,0:T(1,128)S(1)} %bitcast.67, f32[1,8192]{1,0:T(1,128)S(1)} %bitcast.82, f32[1,8192]{1,0:T(1,128)S(1)} %bitcast.81, f32[1,8192]{1,0:T(1,128)S(1)} %bitcast.80, f32[1,8192]{1,0:T(1,128)S(1)} %bitcast.75, ...), kind=kLoop, calls=%fused_computation.106 | loop fusion | flops 147456 | bytes 335872 | tf_op jit(solution)/shard_map/jit(_where)/select_n | solution.py:242
  109.6 1.9 %collective-permute-start.3 = (f32[2,1]{1,0:T(2,128)S(1)}, f32[2,1]{1,0:T(2,128)S(1)}, u32[]{:S(2)}, u32[]{:S(2)}) collective-permute-start(f32[2,1]{1,0:T(2,128)S(1)} %slice.152), channel_id=1, source_target_pairs={{0,16},{16,32},{32,48},{48,64},{64,80},{80,96},{96,112},{112,128},... | collective-permute-start | bytes 32 | tf_op jit(solution)/shard_map/ppermute | solution.py:23
  111.5 0.7 pad_maximum_fusion.1
  112.2 5.0 %collective-permute-done.3 = f32[2,1]{1,0:T(2,128)S(1)} collective-permute-done((f32[2,1]{1,0:T(2,128)S(1)}, f32[2,1]{1,0:T(2,128)S(1)}, u32[]{:S(2)}, u32[]{:S(2)}) %collective-permute-start.3) | collective-permute-done | bytes 40 | tf_op jit(solution)/shard_map/ppermute | solution.py:23
  117.2 0.6 pad_maximum_fusion.4
  (112 shorter events, 11.7 us)
Async XLA Ops:
  0.6 9.5 %copy-start.2 = (f32[2,4096]{1,0:T(2,128)S(1)}, f32[2,4096]{1,0:T(2,128)}, u32[]{:S(2)}) copy-start(f32[2,4096]{1,0:T(2,128)} %param.13) | copy-start | bytes 98308
  13.0 19.8 %all-to-all-start = ((f32[4,32,256]{2,0,1:T(4,128)}), f32[4,32,256]{2,0,1:T(4,128)S(1)}, u32[]{:S(2)}, u32[]{:S(2)}) async-start(f32[4,32,256]{2,0,1:T(4,128)} %copy.16), calls=%async_computation | async-start | bytes 262144 | tf_op jit(solution)/shard_map/all_to_all | solution.py:151
  33.4 2.0 %copy-start.3 = (f32[96]{0:T(128)S(1)}, f32[96]{0:T(128)}, u32[]{:S(2)}) copy-start(f32[96]{0:T(128)} %param.21) | copy-start | bytes 1156
  36.0 9.6 %copy-start.4 = (f32[96]{0:T(128)S(1)}, f32[96]{0:T(128)}, u32[]{:S(2)}) copy-start(f32[96]{0:T(128)} %param.20) | copy-start | bytes 1156
  36.0 10.8 %collective-permute-start = (f32[1,9216]{1,0:T(1,128)S(1)}, f32[1,9216]{1,0:T(1,128)S(1)}, u32[]{:S(2)}, u32[]{:S(2)}) collective-permute-start(f32[1,9216]{1,0:T(1,128)S(1)} %slice.130), channel_id=1, source_target_pairs={{0,16},{16,32},{32,48},{48,64},{64,80},{80,96},{96,112},{112,128},... | collective-permute-start | bytes 110600 | tf_op jit(solution)/shard_map/ppermute | solution.py:23
  40.0 33.0 %copy-start = (f32[96,96]{1,0:T(8,128)S(1)}, f32[96,96]{1,0:T(8,128)}, u32[]{:S(2)}) copy-start(f32[96,96]{1,0:T(8,128)} %param.23) | copy-start | bytes 110596
  40.0 33.1 %copy-start.1 = (f32[96,96]{1,0:T(8,128)S(1)}, f32[96,96]{1,0:T(8,128)}, u32[]{:S(2)}) copy-start(f32[96,96]{1,0:T(8,128)} %param.22) | copy-start | bytes 110596
  40.1 7.1 %collective-permute-start.1 = (f32[1,9216]{1,0:T(1,128)S(1)}, f32[1,9216]{1,0:T(1,128)S(1)}, u32[]{:S(2)}, u32[]{:S(2)}) collective-permute-start(f32[1,9216]{1,0:T(1,128)S(1)} %slice.132), channel_id=1, source_target_pairs={{16,0},{32,16},{48,32},{64,48},{80,64},{96,80},{112,96},{128,112},... | collective-permute-start | bytes 110600 | tf_op jit(solution)/shard_map/ppermute | solution.py:23
  69.2 13.8 %all-to-all-start.2 = ((f32[16,1,3464]{2,1,0:T(1,128)}), f32[16,1,3464]{2,1,0:T(1,128)S(1)}, u32[]{:S(2)}, u32[]{:S(2)}) async-start(f32[16,1,3464]{2,1,0:T(1,128)} %broadcast_in_dim.191), calls=%async_computation.2 | async-start | bytes 458752 | tf_op jit(solution)/shard_map/all_to_all | solution.py:74
  95.5 11.1 %all-to-all-start.3 = ((f32[16,2,4]{2,1,0:T(2,128)}), f32[16,2,4]{2,1,0:T(2,128)S(1)}, u32[]{:S(2)}, u32[]{:S(2)}) async-start(f32[16,2,4]{2,1,0:T(2,128)} %broadcast_in_dim.196), calls=%async_computation.3 | async-start | bytes 32768 | tf_op jit(solution)/shard_map/all_to_all | solution.py:81
  99.1 7.9 %collective-permute-start.2 = (f32[2,1]{1,0:T(2,128)S(1)}, f32[2,1]{1,0:T(2,128)S(1)}, u32[]{:S(2)}, u32[]{:S(2)}) collective-permute-start(f32[2,1]{1,0:T(2,128)S(1)} %slice.148), channel_id=1, source_target_pairs={{0,16},{16,32},{32,48},{48,64},{64,80},{80,96},{96,112},{112,128},... | collective-permute-start | bytes 32 | tf_op jit(solution)/shard_map/ppermute | solution.py:23
  109.6 7.6 %collective-permute-start.3 = (f32[2,1]{1,0:T(2,128)S(1)}, f32[2,1]{1,0:T(2,128)S(1)}, u32[]{:S(2)}, u32[]{:S(2)}) collective-permute-start(f32[2,1]{1,0:T(2,128)S(1)} %slice.152), channel_id=1, source_target_pairs={{0,16},{16,32},{32,48},{48,64},{64,80},{80,96},{96,112},{112,128},... | collective-permute-start | bytes 32 | tf_op jit(solution)/shard_map/ppermute | solution.py:23

commit v2 on v1

--- a/solution.py
+++ b/solution.py
@@ -47,15 +47,11 @@
     earlier = (jnp.arange(block_size)[:, None] > jnp.arange(block_size)[None, :]).astype(
         jnp.bfloat16
     )
-
-    def count_step(counted, onehot_rows):
-        before = (
-            jnp.dot(earlier, onehot_rows, preferred_element_type=jnp.float32) + counted[None, :]
-        )
-        rows_f = onehot_rows.astype(jnp.float32)
-        return (counted + jnp.sum(rows_f, axis=0), jnp.sum(before * rows_f, axis=1))
-
-    _, arrival = lax.scan(count_step, jnp.zeros((groups,), jnp.float32), onehot)
+    within = jnp.einsum("ij,tjg->tig", earlier, onehot, preferred_element_type=jnp.float32)
+    rows_f = onehot.astype(jnp.float32)
+    per_turn = jnp.sum(rows_f, axis=1)
+    offsets = jnp.cumsum(per_turn, axis=0) - per_turn
+    arrival = jnp.sum((within + offsets[:, None, :]) * rows_f, axis=2)
     return arrival.reshape(count).astype(jnp.int32)
 
 
@@ -67,12 +63,12 @@
     return jnp.dot(left, right, preferred_element_type=jnp.float32)
 
 
-def pb_sum(flat, axis):
+def pb_sum(rows, axis):
     count = lax.axis_size(axis)
-    chunks = flat.reshape(count, -1)
+    chunks = rows.reshape((count, -1) + rows.shape[1:])
     mine = jnp.sum(lax.all_to_all(chunks, axis, 0, 0, tiled=True), axis=0)
     every = lax.all_to_all(jnp.broadcast_to(mine[None], chunks.shape), axis, 0, 0, tiled=True)
-    return every.reshape(-1)
+    return every.reshape(rows.shape)
 
 
 def pb_sum_small(value, axis):
@@ -81,14 +77,15 @@
     return jnp.sum(lax.all_to_all(spread, axis, 0, 0, tiled=True), axis=0)
 
 
-def stencil(extended, sideways, coeff_long, coeff_cross, grid_y):
-    centre = sideways[:, grid_y:-grid_y]
+def stencil(extended, coeff_long, coeff_cross):
+    centre = extended[1:-1]
     along_diff = extended[2:] - extended[:-2]
-    across = sideways[:, 2 * grid_y :] + sideways[:, : -2 * grid_y]
-    column = jnp.arange(centre.shape[1], dtype=jnp.int32) % grid_y
-    upper_y = jnp.where(column < grid_y - 1, jnp.pad(centre, ((0, 0), (0, 1)))[:, 1:], 0.0)
-    lower_y = jnp.where(column > 0, jnp.pad(centre, ((0, 0), (1, 0)))[:, :-1], 0.0)
-    return coeff_long[None, :] * along_diff + coeff_cross[None, :] * (
+    padded_x = jnp.pad(centre, ((0, 0), (1, 1), (0, 0)))
+    across = padded_x[:, 2:, :] + padded_x[:, :-2, :]
+    padded_y = jnp.pad(centre, ((0, 0), (0, 0), (1, 1)))
+    upper_y = padded_y[:, :, 2:]
+    lower_y = padded_y[:, :, :-2]
+    return coeff_long[None] * along_diff + coeff_cross[None] * (
         4.0 * centre - across - upper_y - lower_y
     )
 
@@ -120,7 +117,7 @@
         particles[0]
     )
     phases = particles[0] + DISPERSION * energy
-    destination = target_group[:, 0]
+    destination = target_group.reshape(-1)
     arrival = arrival_slots(destination, groups)
 
     values = jnp.stack(
@@ -169,13 +166,11 @@
             jnp.arange(grid_x, dtype=jnp.int32) + (SL_DEV - 1) * grid_x,
         ]
     )
-    edges = deposit_rows(weight_bf16, row_key, got_y, edge_targets, grid_y).reshape(2, cell_count)
-    below = shifted(edges[1:2], "ta", 1)
-    above = shifted(edges[0:1], "ta", -1)
+    edges = deposit_rows(weight_bf16, row_key, got_y, edge_targets, grid_y)
+    below = shifted(edges[grid_x:], "ta", 1)
+    above = shifted(edges[:grid_x], "ta", -1)
     middle_targets = jnp.arange(grid_x, (SL_DEV - 1) * grid_x, dtype=jnp.int32)
-    middle = deposit_rows(weight_bf16, row_key, got_y, middle_targets, grid_y).reshape(
-        SL_DEV - 2, cell_count
-    )
+    middle = deposit_rows(weight_bf16, row_key, got_y, middle_targets, grid_y)
 
     profile = lookup(mode_x, got_x) * lookup(mode_y, got_y)
     weighted = arrived_weight * profile
@@ -196,30 +191,26 @@
         return cosine, sine_part, sums
 
     cosine0, sine0, sums0 = local_bunching(got_phase)
-    stacked = jnp.concatenate(
-        [below.reshape(-1), edges[0], middle.reshape(-1), edges[1], above.reshape(-1), sums0.reshape(-1)]
-    )
-    width = splits * 8
-    padded_len = -(-stacked.shape[0] // width) * width
-    stacked = jnp.pad(stacked, (0, padded_len - stacked.shape[0]))
+    sums_row = jnp.pad(sums0.reshape(1, 2 * SL_DEV), ((0, 7), (0, grid_y - 2 * SL_DEV)))
+    stacked = jnp.concatenate([below, edges[:grid_x], middle, edges[grid_x:], above, sums_row])
+    chunk_rows = -(-stacked.shape[0] // (splits * 8)) * 8
+    stacked = jnp.pad(stacked, ((0, chunk_rows * splits - stacked.shape[0]), (0, 0)))
     summed = pb_sum(stacked, "pb")
-    extended = summed[: (SL_DEV + 2) * cell_count].reshape(SL_DEV + 2, cell_count)
-    bunching0 = summed[(SL_DEV + 2) * cell_count : (SL_DEV + 2) * cell_count + 2 * SL_DEV].reshape(
-        2, SL_DEV
-    )
-
-    long_flat = along_coeff.reshape(cell_count)
-    cross_flat = across_coeff.reshape(cell_count)
-    sideways = jnp.pad(extended[1:-1], ((0, 0), (grid_y, grid_y)))
-    force_map = stencil(extended, sideways, long_flat, cross_flat, grid_y)
+    density_rows = (SL_DEV + 2) * grid_x
+    extended = summed[:density_rows].reshape(SL_DEV + 2, grid_x, grid_y)
+    bunching0 = summed[density_rows, : 2 * SL_DEV].reshape(2, SL_DEV)
+    force_map = stencil(extended, along_coeff, across_coeff)
 
     force_rows = force_map.reshape(SL_DEV * grid_x, grid_y)
-    force_parts = jnp.concatenate(split3(force_rows), axis=1)
+    force_hi = lax.reduce_precision(force_rows, exponent_bits=8, mantissa_bits=7)
+    force_parts = jnp.concatenate(
+        [force_hi.astype(jnp.bfloat16), (force_rows - force_hi).astype(jnp.bfloat16)], axis=1
+    )
     pick_row = (row_key[:, None] == jnp.arange(SL_DEV * grid_x, dtype=jnp.int32)[None, :]).astype(
         jnp.bfloat16
     )
     picked = jnp.dot(pick_row, force_parts, preferred_element_type=jnp.float32)
-    picked = (picked[:, :grid_y] + picked[:, grid_y : 2 * grid_y]) + picked[:, 2 * grid_y :]
+    picked = picked[:, :grid_y] + picked[:, grid_y:]
     pick_col = got_y[:, None] == jnp.arange(grid_y, dtype=jnp.int32)[None, :]
     kicked = got_energy + jnp.sum(jnp.where(pick_col, picked, 0.0), axis=1)
 

time: 119 us -> 112 us (0.941)
  blocking collectives: 20.7 us -> 38.4 us
  waiting for transfers between devices: 30.7 us -> 21 us
  local copies, waits for them, and re-layouts: 8.85 us -> 2.8 us
  starting transfers between devices: 29.2 us -> 25.8 us
  matrix products: 10.5 us -> 7.93 us
  other arithmetic: 16.4 us -> 14.5 us
    all_to_all x0 -> x1, blocking collectives: none -> 15.8 us  [pb_sum(): lax.all_to_all(jnp.broadcast_to(mine[None], chunks.shape), axis, 0, 0, ti...]
    all_to_all x1 -> x0, waiting for transfers between devices: 9.88 us -> none  [pb_sum(): lax.all_to_all(jnp.broadcast_to(mine[None], chunks.shape), axis, 0, 0, ti...]
    slice x5 -> x1, local copies, waits for them, and re-layouts: 4.18 us -> 0.08 us  [body(): edges[:grid_x]]
    all_to_all x1 -> x0, starting transfers between devices: 3.71 us -> none  [pb_sum(): lax.all_to_all(jnp.broadcast_to(mine[None], chunks.shape), axis, 0, 0, ti...]
    all_to_all x1, blocking collectives: 20.7 us -> 22.6 us  [pb_sum(): mine = jnp.sum(lax.all_to_all(chunks, axis, 0, 0, tiled=True), axis=0)]
    dot_general x8 -> x1, matrix products: 2.22 us -> 0.37 us  [arrival_slots(): jnp.einsum('ij,tjg->tig', earlier, onehot, preferred_element_type=jnp.flo...]
  transfers between devices with their start and end apart: 7 -> 6, of which waited for: 6 -> 5; matrix products, arithmetic and copies ran while one was open for 3% -> 3% of each run, Pallas kernels for 0% -> 0%
where the time goes in v2:
time: 112 us; the launch traced here: 111 us
  blocking collectives  38.4 us (34%)
  starting transfers between devices  25.8 us (23%)
  waiting for transfers between devices  21 us (19%)
  other arithmetic  14.5 us (13%)
  matrix products  7.93 us (7%)
  local copies, waits for them, and re-layouts  2.8 us (2%)
    all_to_all x1, blocking collectives, pb_sum(): mine = jnp.sum(lax.all_to_all(chunks, axis, 0, 0, tiled=True), axis=0)  22.6 us
    all_to_all x1, blocking collectives, pb_sum(): lax.all_to_all(jnp.broadcast_to(mine[None], chunks.shape), axis, 0, 0, ti...  15.8 us
    ppermute x4, starting transfers between devices, shifted(): lax.ppermute(value, axis, [(source, source + steps) for source in range(l...  12 us
    all_to_all x1, starting transfers between devices, body(): lax.all_to_all(send.reshape(value_count, groups, capacity), 'ta', split_a...  10.2 us
    all_to_all x1, waiting for transfers between devices, body(): lax.all_to_all(send.reshape(value_count, groups, capacity), 'ta', split_a...  9.54 us
    ppermute x4, waiting for transfers between devices, shifted(): lax.ppermute(value, axis, [(source, source + steps) for source in range(l...  5.91 us
    all_to_all x1, waiting for transfers between devices, pb_sum_small(): return jnp.sum(lax.all_to_all(spread, axis, 0, 0, tiled=True), axis=0)  5.56 us
    all_to_all x1, starting transfers between devices, pb_sum_small(): return jnp.sum(lax.all_to_all(spread, axis, 0, 0, tiled=True), axis=0)  3.58 us
  transfers between devices with their start and end apart: 6, of which 5 were waited for; matrix products, arithmetic and copies ran while one was open for 3% of the time, Pallas kernels for 0%

profile of v2, /device:TPU:8, one launch (start us, length us, event | category | flops | bytes accessed | tf_op | source)
XLA Modules:
  0.0 111.4 jit_solution(9623844434657155003)
XLA Ops:
  0.6 0.8 iota_compare_fusion.14
  1.4 0.7 stack.47
  2.1 0.5 broadcast.456
  2.6 1.4 %reduce.9 = s32[4096]{0:T(1024)S(1)} reduce(s32[4096,1]{0,1:T(1,128)} %param.14, s32[]{:T(128)} %broadcast.456), dimensions={1}, to_apply=%param.14.reduce_sub_computation.3 | reduce | bytes 32772 | tf_op args[3]
  4.6 0.8 add_select_fusion.5
  5.4 1.2 %select_reduce_fusion.2 = (f32[4096]{0:T(1024)S(1)}, f32[4096]{0:T(1024)S(1)}) fusion(f32[96]{0:T(128)} %param.17, s32[4096]{0:T(1024)S(1)} %get-tuple-element.44, f32[96]{0:T(128)} %param.16, s32[4096]{0:T(1024)S(1)} %get-tuple-element.46), kind=kLoop, calls=%fused_computation.33 | loop fusion | flops 2351104 | bytes 66304 | tf_op jit(solution)/shard_map/reduce_sum | solution.py:28
  6.6 1.3 %multiply_add_fusion.4 = (f32[1,4096]{1,0:T(1,128)S(1)}, f32[1,4096]{1,0:T(1,128)S(1)}) fusion(f32[2,4096]{1,0:T(2,128)} %param.11, f32[1,4096]{1,0:T(1,128)S(1)} %bitcast.84), kind=kLoop, calls=%fused_computation.114 | loop fusion | flops 16384 | bytes 81920 | tf_op jit(solution)/shard_map/add | solution.py:119
  8.4 1.2 %fusion.2 = f32[384,256]{1,0:T(8,128)S(1)} fusion(bf16[128,4096]{1,0:T(8,128)(2,1)S(1)} %bitcast.61, bf16[128,4096]{1,0:T(8,128)(2,1)S(1)} %bitcast.60, bf16[128,4096]{1,0:T(8,128)(2,1)S(1)} %bitcast.59, s32[4096]{0:T(1024)S(1)} %bitcast.87), kind=kOutput, calls=%fused_computation.6 | convolution fusion | flops 815792128 | bytes 3555328 | tf_op jit(solution)/shard_map/dot_general | solution.py:145
  9.6 0.7 copy.25
  10.4 10.2 %all-to-all-start = ((f32[4,32,256]{2,0,1:T(4,128)}), f32[4,32,256]{2,0,1:T(4,128)S(1)}, u32[]{:S(2)}, u32[]{:S(2)}) async-start(f32[4,32,256]{2,0,1:T(4,128)} %copy.25), calls=%async_computation | async-start | bytes 262144 | tf_op jit(solution)/shard_map/all_to_all | solution.py:148
  20.6 9.5 %all-to-all-done = f32[4,32,256]{2,0,1:T(4,128)S(1)} async-done(((f32[4,32,256]{2,0,1:T(4,128)}), f32[4,32,256]{2,0,1:T(4,128)S(1)}, u32[]{:S(2)}, u32[]{:S(2)}) %all-to-all-start) | async-done | bytes 131104 | tf_op jit(solution)/shard_map/all_to_all | solution.py:148
  30.7 0.6 select_reduce_fusion
  31.3 1.5 %fusion.3 = f32[192,96]{0,1:T(8,128)S(1)} fusion(s32[8192]{0:T(1024)S(1)} %get-tuple-element.17, s32[192]{0:T(256)S(1)} %pad_add_fusion, bf16[8192]{0:T(1024)(128)(2,1)S(1)} %convert_element_type.102, s32[8192]{0:T(1024)S(1)} %get-tuple-element.43), kind=kOutput, calls=%fused_computation.7 | convolution fusion | flops 305922048 | bytes 156416 | tf_op jit(solution)/shard_map/dot_general | solution.py:63
  32.9 2.6 %collective-permute-start = (f32[96,96]{0,1:T(8,128)S(1)}, f32[96,96]{0,1:T(8,128)S(1)}, u32[]{:S(2)}, u32[]{:S(2)}) collective-permute-start(f32[96,96]{0,1:T(8,128)S(1)} %get-tuple-element.38), channel_id=1, source_target_pairs={{0,16},{16,32},{32,48},{48,64},{64,80},{80,96},{96,112},{112,128},... | collective-permute-start | bytes 110600 | tf_op jit(solution)/shard_map/ppermute | solution.py:23
  35.5 1.5 %fusion.4 = f32[192,96]{0,1:T(8,128)S(1)} fusion(s32[8192]{0:T(1024)S(1)} %get-tuple-element.17, s32[192]{0:T(256)S(1)} %iota_add_fusion, bf16[8192]{0:T(1024)(128)(2,1)S(1)} %convert_element_type.102, s32[8192]{0:T(1024)S(1)} %get-tuple-element.43), kind=kOutput, calls=%fused_computation.8 | convolution fusion | flops 305922048 | bytes 156416 | tf_op jit(solution)/shard_map/dot_general | solution.py:63
  37.0 5.6 %collective-permute-start.1 = (f32[96,96]{0,1:T(8,128)S(1)}, f32[96,96]{0,1:T(8,128)S(1)}, u32[]{:S(2)}, u32[]{:S(2)}) collective-permute-start(f32[96,96]{0,1:T(8,128)S(1)} %get-tuple-element.37), channel_id=1, source_target_pairs={{16,0},{32,16},{48,32},{64,48},{80,64},{96,80},{112,96},{128,112},... | collective-permute-start | bytes 110600 | tf_op jit(solution)/shard_map/ppermute | solution.py:23
  42.6 0.6 select_reduce_fusion.1
  43.8 0.6 collective-permute-done.1
  44.7 22.6 %all_to_all.20 = f32[16,40,96]{2,1,0:T(8,128)S(1)} all-to-all(f32[16,40,96]{2,1,0:T(8,128)S(1)} %bitcast.58), channel_id=1, replica_groups=mesh['ta'=32,'pb'=16] {'pb'}, dimensions={0} | all-to-all | bytes 491520 | tf_op jit(solution)/shard_map/all_to_all | solution.py:69
  67.4 15.8 %all_to_all.21 = f32[16,40,96]{2,1,0:T(8,128)S(1)} all-to-all(f32[16,40,96]{2,1,0:T(8,128)S(1)} %broadcast_in_dim.169), channel_id=1, replica_groups=mesh['ta'=32,'pb'=16] {'pb'}, dimensions={0} | all-to-all | bytes 491520 | tf_op jit(solution)/shard_map/all_to_all | solution.py:70
  83.5 3.3 %fusion = f32[8192,192]{0,1:T(8,128)S(1)} fusion(s32[8192]{0:T(1024)S(1)} %get-tuple-element.17, bf16[384,96]{1,0:T(8,128)(2,1)S(1)} %get-tuple-element.26, bf16[384,96]{1,0:T(8,128)(2,1)S(1)} %get-tuple-element.25), kind=kOutput, calls=%fused_computation.1 | convolution fusion | flops 1211400192 | bytes 6471680 | tf_op jit(solution)/shard_map/dot_general | solution.py:212
  86.8 0.6 fusion.6
  88.3 0.6 broadcast_in_dim.171
  88.9 3.6 %all-to-all-start.3 = ((f32[16,2,4]{2,1,0:T(2,128)}), f32[16,2,4]{2,1,0:T(2,128)S(1)}, u32[]{:S(2)}, u32[]{:S(2)}) async-start(f32[16,2,4]{2,1,0:T(2,128)} %broadcast_in_dim.171), calls=%async_computation.3 | async-start | bytes 32768 | tf_op jit(solution)/shard_map/all_to_all | solution.py:77
  92.7 1.9 %collective-permute-start.2 = (f32[2,1]{1,0:T(2,128)S(1)}, f32[2,1]{1,0:T(2,128)S(1)}, u32[]{:S(2)}, u32[]{:S(2)}) collective-permute-start(f32[2,1]{1,0:T(2,128)S(1)} %slice.129), channel_id=1, source_target_pairs={{0,16},{16,32},{32,48},{48,64},{64,80},{80,96},{96,112},{112,128},... | collective-permute-start | bytes 32 | tf_op jit(solution)/shard_map/ppermute | solution.py:23
  94.6 5.6 %all-to-all-done.3 = f32[16,2,4]{2,1,0:T(2,128)S(1)} async-done(((f32[16,2,4]{2,1,0:T(2,128)}), f32[16,2,4]{2,1,0:T(2,128)S(1)}, u32[]{:S(2)}, u32[]{:S(2)}) %all-to-all-start.3) | async-done | bytes 544 | tf_op jit(solution)/shard_map/all_to_all | solution.py:77
  100.2 0.4 collective-permute-done.2
  101.0 2.2 %add_select_fusion.4 = (f32[1,8192]{1,0:T(1,128)S(1)}, f32[1,8192]{1,0:T(1,128)S(1)}) fusion(pred[1,8192]{1,0:T(4,128)(4,1)S(1)} %bitcast.70, f32[1,8192]{1,0:T(1,128)S(1)} %bitcast.65, f32[1,8192]{1,0:T(1,128)S(1)} %bitcast.82, f32[1,8192]{1,0:T(1,128)S(1)} %bitcast.81, f32[1,8192]{1,0:T(1,128)S(1)} %bitcast.80, f32[1,8192]{1,0:T(1,128)S(1)} %bitcast.75, ...), kind=kLoop, calls=%fused_computation.90 | loop fusion | flops 147456 | bytes 335872 | tf_op jit(solution)/shard_map/jit(_where)/select_n | solution.py:233
  103.2 1.9 %collective-permute-start.3 = (f32[2,1]{1,0:T(2,128)S(1)}, f32[2,1]{1,0:T(2,128)S(1)}, u32[]{:S(2)}, u32[]{:S(2)}) collective-permute-start(f32[2,1]{1,0:T(2,128)S(1)} %slice.133), channel_id=1, source_target_pairs={{0,16},{16,32},{32,48},{48,64},{64,80},{80,96},{96,112},{112,128},... | collective-permute-start | bytes 32 | tf_op jit(solution)/shard_map/ppermute | solution.py:23
  105.1 0.7 pad_maximum_fusion.1
  105.8 5.0 %collective-permute-done.3 = f32[2,1]{1,0:T(2,128)S(1)} collective-permute-done((f32[2,1]{1,0:T(2,128)S(1)}, f32[2,1]{1,0:T(2,128)S(1)}, u32[]{:S(2)}, u32[]{:S(2)}) %collective-permute-start.3) | collective-permute-done | bytes 40 | tf_op jit(solution)/shard_map/ppermute | solution.py:23
  110.8 0.6 pad_maximum_fusion.4
  (60 shorter events, 4.5 us)
Async XLA Ops:
  8.3 22.4 %copy-start.2 = (f32[96]{0:T(128)S(1)}, f32[96]{0:T(128)}, u32[]{:S(2)}) copy-start(f32[96]{0:T(128)} %param.19) | copy-start | bytes 1156
  10.4 19.8 %all-to-all-start = ((f32[4,32,256]{2,0,1:T(4,128)}), f32[4,32,256]{2,0,1:T(4,128)S(1)}, u32[]{:S(2)}, u32[]{:S(2)}) async-start(f32[4,32,256]{2,0,1:T(4,128)} %copy.25), calls=%async_computation | async-start | bytes 262144 | tf_op jit(solution)/shard_map/all_to_all | solution.py:148
  32.9 9.8 %copy-start.3 = (f32[96]{0:T(128)S(1)}, f32[96]{0:T(128)}, u32[]{:S(2)}) copy-start(f32[96]{0:T(128)} %param.18) | copy-start | bytes 1156
  32.9 10.9 %collective-permute-start = (f32[96,96]{0,1:T(8,128)S(1)}, f32[96,96]{0,1:T(8,128)S(1)}, u32[]{:S(2)}, u32[]{:S(2)}) collective-permute-start(f32[96,96]{0,1:T(8,128)S(1)} %get-tuple-element.38), channel_id=1, source_target_pairs={{0,16},{16,32},{32,48},{48,64},{64,80},{80,96},{96,112},{112,128},... | collective-permute-start | bytes 110600 | tf_op jit(solution)/shard_map/ppermute | solution.py:23
  37.0 46.3 %copy-start = (f32[96,96]{1,0:T(8,128)S(1)}, f32[96,96]{1,0:T(8,128)}, u32[]{:S(2)}) copy-start(f32[96,96]{1,0:T(8,128)} %param.21) | copy-start | bytes 110596
  37.0 46.3 %copy-start.1 = (f32[96,96]{1,0:T(8,128)S(1)}, f32[96,96]{1,0:T(8,128)}, u32[]{:S(2)}) copy-start(f32[96,96]{1,0:T(8,128)} %param.20) | copy-start | bytes 110596
  37.0 7.3 %collective-permute-start.1 = (f32[96,96]{0,1:T(8,128)S(1)}, f32[96,96]{0,1:T(8,128)S(1)}, u32[]{:S(2)}, u32[]{:S(2)}) collective-permute-start(f32[96,96]{0,1:T(8,128)S(1)} %get-tuple-element.37), channel_id=1, source_target_pairs={{16,0},{32,16},{48,32},{64,48},{80,64},{96,80},{112,96},{128,112},... | collective-permute-start | bytes 110600 | tf_op jit(solution)/shard_map/ppermute | solution.py:23
  88.9 11.2 %all-to-all-start.3 = ((f32[16,2,4]{2,1,0:T(2,128)}), f32[16,2,4]{2,1,0:T(2,128)S(1)}, u32[]{:S(2)}, u32[]{:S(2)}) async-start(f32[16,2,4]{2,1,0:T(2,128)} %broadcast_in_dim.171), calls=%async_computation.3 | async-start | bytes 32768 | tf_op jit(solution)/shard_map/all_to_all | solution.py:77
  92.7 7.9 %collective-permute-start.2 = (f32[2,1]{1,0:T(2,128)S(1)}, f32[2,1]{1,0:T(2,128)S(1)}, u32[]{:S(2)}, u32[]{:S(2)}) collective-permute-start(f32[2,1]{1,0:T(2,128)S(1)} %slice.129), channel_id=1, source_target_pairs={{0,16},{16,32},{32,48},{48,64},{64,80},{80,96},{96,112},{112,128},... | collective-permute-start | bytes 32 | tf_op jit(solution)/shard_map/ppermute | solution.py:23
  103.2 7.6 %collective-permute-start.3 = (f32[2,1]{1,0:T(2,128)S(1)}, f32[2,1]{1,0:T(2,128)S(1)}, u32[]{:S(2)}, u32[]{:S(2)}) collective-permute-start(f32[2,1]{1,0:T(2,128)S(1)} %slice.133), channel_id=1, source_target_pairs={{0,16},{16,32},{32,48},{48,64},{64,80},{80,96},{96,112},{112,128},... | collective-permute-start | bytes 32 | tf_op jit(solution)/shard_map/ppermute | solution.py:23

commit v3 on v2

--- a/solution.py
+++ b/solution.py
@@ -36,22 +36,19 @@
     return [part.astype(jnp.bfloat16) for part in (hi, mid, lo)]
 
 
-def arrival_slots(destination, groups):
-    count = destination.shape[0]
+def arrival_slots(to_group):
+    groups, count = to_group.shape
     block_size = math.gcd(count, 512)
     turn_count = count // block_size
-    onehot = (destination[:, None] == jnp.arange(groups, dtype=jnp.int32)[None, :]).astype(
-        jnp.bfloat16
-    )
-    onehot = onehot.reshape(turn_count, block_size, groups)
+    onehot = to_group.astype(jnp.bfloat16).reshape(groups, turn_count, block_size)
     earlier = (jnp.arange(block_size)[:, None] > jnp.arange(block_size)[None, :]).astype(
         jnp.bfloat16
     )
-    within = jnp.einsum("ij,tjg->tig", earlier, onehot, preferred_element_type=jnp.float32)
+    within = jnp.einsum("gtj,ij->gti", onehot, earlier, preferred_element_type=jnp.float32)
     rows_f = onehot.astype(jnp.float32)
-    per_turn = jnp.sum(rows_f, axis=1)
-    offsets = jnp.cumsum(per_turn, axis=0) - per_turn
-    arrival = jnp.sum((within + offsets[:, None, :]) * rows_f, axis=2)
+    per_turn = jnp.sum(rows_f, axis=2)
+    offsets = jnp.cumsum(per_turn, axis=1) - per_turn
+    arrival = jnp.sum((within + offsets[:, :, None]) * rows_f, axis=0)
     return arrival.reshape(count).astype(jnp.int32)
 
 
@@ -117,8 +114,9 @@
         particles[0]
     )
     phases = particles[0] + DISPERSION * energy
-    destination = target_group.reshape(-1)
-    arrival = arrival_slots(destination, groups)
+    destination = target_group.reshape(1, per_device)
+    to_group = destination == jnp.arange(groups, dtype=jnp.int32)[:, None]
+    arrival = arrival_slots(to_group)
 
     values = jnp.stack(
         [
@@ -129,7 +127,6 @@
         ]
     )
     value_count = values.shape[0]
-    to_group = destination[None, :] == jnp.arange(groups, dtype=jnp.int32)[:, None]
     parts = split3(values)
     left = jnp.concatenate(
         [

time: 112 us -> 112 us (level)
  no operation moved by 1% of the time
where the time goes in v3:
time: 112 us
  blocking collectives  38.4 us (34%)
  starting transfers between devices  25.8 us (23%)
  waiting for transfers between devices  21 us (19%)
  other arithmetic  14.6 us (13%)
  matrix products  7.92 us (7%)
  local copies, waits for them, and re-layouts  2.8 us (2%)
    all_to_all x1, blocking collectives, pb_sum(): mine = jnp.sum(lax.all_to_all(chunks, axis, 0, 0, tiled=True), axis=0)  22.6 us
    all_to_all x1, blocking collectives, pb_sum(): lax.all_to_all(jnp.broadcast_to(mine[None], chunks.shape), axis, 0, 0, ti...  15.8 us
    ppermute x4, starting transfers between devices, shifted(): lax.ppermute(value, axis, [(source, source + steps) for source in range(l...  12 us
    all_to_all x1, starting transfers between devices, body(): lax.all_to_all(send.reshape(value_count, groups, capacity), 'ta', split_a...  10.2 us
    all_to_all x1, waiting for transfers between devices, body(): lax.all_to_all(send.reshape(value_count, groups, capacity), 'ta', split_a...  9.54 us
    ppermute x4, waiting for transfers between devices, shifted(): lax.ppermute(value, axis, [(source, source + steps) for source in range(l...  5.91 us
    all_to_all x1, waiting for transfers between devices, pb_sum_small(): return jnp.sum(lax.all_to_all(spread, axis, 0, 0, tiled=True), axis=0)  5.56 us
    all_to_all x1, starting transfers between devices, pb_sum_small(): return jnp.sum(lax.all_to_all(spread, axis, 0, 0, tiled=True), axis=0)  3.58 us
  transfers between devices with their start and end apart: 6, of which 5 were waited for; matrix products, arithmetic and copies ran while one was open for 3% of the time, Pallas kernels for 0%

profile of v3, /device:TPU:8, one launch (start us, length us, event | category | flops | bytes accessed | tf_op | source)
XLA Modules:
  0.0 111.5 jit_solution(458427621943660586)
XLA Ops:
  0.6 0.8 iota_compare_fusion.14
  1.4 0.7 stack.47
  2.1 0.5 broadcast.455
  2.6 1.4 %reduce.9 = s32[4096]{0:T(1024)S(1)} reduce(s32[4096,1]{0,1:T(1,128)} %param.14, s32[]{:T(128)} %broadcast.455), dimensions={1}, to_apply=%param.14.reduce_sub_computation.3 | reduce | bytes 32772 | tf_op args[3]
  4.8 0.8 add_select_fusion.5
  5.5 1.2 %select_reduce_fusion.2 = (f32[4096]{0:T(1024)S(1)}, f32[4096]{0:T(1024)S(1)}) fusion(f32[96]{0:T(128)} %param.17, s32[4096]{0:T(1024)S(1)} %get-tuple-element.44, f32[96]{0:T(128)} %param.16, s32[4096]{0:T(1024)S(1)} %get-tuple-element.46), kind=kLoop, calls=%fused_computation.33 | loop fusion | flops 2351104 | bytes 66304 | tf_op jit(solution)/shard_map/reduce_sum | solution.py:28
  6.8 1.3 %multiply_add_fusion.4 = (f32[1,4096]{1,0:T(1,128)S(1)}, f32[1,4096]{1,0:T(1,128)S(1)}) fusion(f32[2,4096]{1,0:T(2,128)} %param.11, f32[1,4096]{1,0:T(1,128)S(1)} %bitcast.78), kind=kLoop, calls=%fused_computation.113 | loop fusion | flops 16384 | bytes 81920 | tf_op jit(solution)/shard_map/add | solution.py:116
  8.5 1.2 %fusion.2 = f32[384,256]{1,0:T(8,128)S(1)} fusion(bf16[128,4096]{1,0:T(8,128)(2,1)S(1)} %bitcast.55, bf16[128,4096]{1,0:T(8,128)(2,1)S(1)} %bitcast.54, bf16[128,4096]{1,0:T(8,128)(2,1)S(1)} %bitcast.53, s32[4096]{0:T(1024)S(1)} %bitcast.81), kind=kOutput, calls=%fused_computation.6 | convolution fusion | flops 815792128 | bytes 3555328 | tf_op jit(solution)/shard_map/dot_general | solution.py:142
  9.7 0.7 copy.25
  10.5 10.2 %all-to-all-start = ((f32[4,32,256]{2,0,1:T(4,128)}), f32[4,32,256]{2,0,1:T(4,128)S(1)}, u32[]{:S(2)}, u32[]{:S(2)}) async-start(f32[4,32,256]{2,0,1:T(4,128)} %copy.25), calls=%async_computation | async-start | bytes 262144 | tf_op jit(solution)/shard_map/all_to_all | solution.py:145
  20.8 9.5 %all-to-all-done = f32[4,32,256]{2,0,1:T(4,128)S(1)} async-done(((f32[4,32,256]{2,0,1:T(4,128)}), f32[4,32,256]{2,0,1:T(4,128)S(1)}, u32[]{:S(2)}, u32[]{:S(2)}) %all-to-all-start) | async-done | bytes 131104 | tf_op jit(solution)/shard_map/all_to_all | solution.py:145
  30.8 0.6 select_reduce_fusion
  31.4 1.5 %fusion.3 = f32[192,96]{0,1:T(8,128)S(1)} fusion(s32[8192]{0:T(1024)S(1)} %get-tuple-element.17, s32[192]{0:T(256)S(1)} %pad_add_fusion, bf16[8192]{0:T(1024)(128)(2,1)S(1)} %convert_element_type.102, s32[8192]{0:T(1024)S(1)} %get-tuple-element.43), kind=kOutput, calls=%fused_computation.7 | convolution fusion | flops 305922048 | bytes 156416 | tf_op jit(solution)/shard_map/dot_general | solution.py:60
  33.0 2.6 %collective-permute-start = (f32[96,96]{0,1:T(8,128)S(1)}, f32[96,96]{0,1:T(8,128)S(1)}, u32[]{:S(2)}, u32[]{:S(2)}) collective-permute-start(f32[96,96]{0,1:T(8,128)S(1)} %get-tuple-element.38), channel_id=1, source_target_pairs={{0,16},{16,32},{32,48},{48,64},{64,80},{80,96},{96,112},{112,128},... | collective-permute-start | bytes 110600 | tf_op jit(solution)/shard_map/ppermute | solution.py:23
  35.6 1.5 %fusion.4 = f32[192,96]{0,1:T(8,128)S(1)} fusion(s32[8192]{0:T(1024)S(1)} %get-tuple-element.17, s32[192]{0:T(256)S(1)} %iota_add_fusion, bf16[8192]{0:T(1024)(128)(2,1)S(1)} %convert_element_type.102, s32[8192]{0:T(1024)S(1)} %get-tuple-element.43), kind=kOutput, calls=%fused_computation.8 | convolution fusion | flops 305922048 | bytes 156416 | tf_op jit(solution)/shard_map/dot_general | solution.py:60
  37.1 5.6 %collective-permute-start.1 = (f32[96,96]{0,1:T(8,128)S(1)}, f32[96,96]{0,1:T(8,128)S(1)}, u32[]{:S(2)}, u32[]{:S(2)}) collective-permute-start(f32[96,96]{0,1:T(8,128)S(1)} %get-tuple-element.37), channel_id=1, source_target_pairs={{16,0},{32,16},{48,32},{64,48},{80,64},{96,80},{112,96},{128,112},... | collective-permute-start | bytes 110600 | tf_op jit(solution)/shard_map/ppermute | solution.py:23
  42.8 0.6 select_reduce_fusion.1
  43.9 0.6 collective-permute-done.1
  44.8 22.6 %all_to_all.20 = f32[16,40,96]{2,1,0:T(8,128)S(1)} all-to-all(f32[16,40,96]{2,1,0:T(8,128)S(1)} %bitcast.52), channel_id=1, replica_groups=mesh['ta'=32,'pb'=16] {'pb'}, dimensions={0} | all-to-all | bytes 491520 | tf_op jit(solution)/shard_map/all_to_all | solution.py:66
  67.5 15.8 %all_to_all.21 = f32[16,40,96]{2,1,0:T(8,128)S(1)} all-to-all(f32[16,40,96]{2,1,0:T(8,128)S(1)} %broadcast_in_dim.168), channel_id=1, replica_groups=mesh['ta'=32,'pb'=16] {'pb'}, dimensions={0} | all-to-all | bytes 491520 | tf_op jit(solution)/shard_map/all_to_all | solution.py:67
  83.6 3.3 %fusion = f32[8192,192]{0,1:T(8,128)S(1)} fusion(s32[8192]{0:T(1024)S(1)} %get-tuple-element.17, bf16[384,96]{1,0:T(8,128)(2,1)S(1)} %get-tuple-element.26, bf16[384,96]{1,0:T(8,128)(2,1)S(1)} %get-tuple-element.25), kind=kOutput, calls=%fused_computation.1 | convolution fusion | flops 1211400192 | bytes 6471680 | tf_op jit(solution)/shard_map/dot_general | solution.py:209
  87.0 0.6 fusion.6
  88.4 0.6 broadcast_in_dim.170
  89.0 3.6 %all-to-all-start.3 = ((f32[16,2,4]{2,1,0:T(2,128)}), f32[16,2,4]{2,1,0:T(2,128)S(1)}, u32[]{:S(2)}, u32[]{:S(2)}) async-start(f32[16,2,4]{2,1,0:T(2,128)} %broadcast_in_dim.170), calls=%async_computation.3 | async-start | bytes 32768 | tf_op jit(solution)/shard_map/all_to_all | solution.py:74
  92.8 1.9 %collective-permute-start.2 = (f32[2,1]{1,0:T(2,128)S(1)}, f32[2,1]{1,0:T(2,128)S(1)}, u32[]{:S(2)}, u32[]{:S(2)}) collective-permute-start(f32[2,1]{1,0:T(2,128)S(1)} %slice.129), channel_id=1, source_target_pairs={{0,16},{16,32},{32,48},{48,64},{64,80},{80,96},{96,112},{112,128},... | collective-permute-start | bytes 32 | tf_op jit(solution)/shard_map/ppermute | solution.py:23
  94.7 5.6 %all-to-all-done.3 = f32[16,2,4]{2,1,0:T(2,128)S(1)} async-done(((f32[16,2,4]{2,1,0:T(2,128)}), f32[16,2,4]{2,1,0:T(2,128)S(1)}, u32[]{:S(2)}, u32[]{:S(2)}) %all-to-all-start.3) | async-done | bytes 544 | tf_op jit(solution)/shard_map/all_to_all | solution.py:74
  100.3 0.4 collective-permute-done.2
  101.1 2.2 %add_select_fusion.4 = (f32[1,8192]{1,0:T(1,128)S(1)}, f32[1,8192]{1,0:T(1,128)S(1)}) fusion(pred[1,8192]{1,0:T(4,128)(4,1)S(1)} %bitcast.64, f32[1,8192]{1,0:T(1,128)S(1)} %bitcast.59, f32[1,8192]{1,0:T(1,128)S(1)} %bitcast.76, f32[1,8192]{1,0:T(1,128)S(1)} %bitcast.75, f32[1,8192]{1,0:T(1,128)S(1)} %bitcast.74, f32[1,8192]{1,0:T(1,128)S(1)} %bitcast.69, ...), kind=kLoop, calls=%fused_computation.89 | loop fusion | flops 147456 | bytes 335872 | tf_op jit(solution)/shard_map/jit(_where)/select_n | solution.py:230
  103.3 1.9 %collective-permute-start.3 = (f32[2,1]{1,0:T(2,128)S(1)}, f32[2,1]{1,0:T(2,128)S(1)}, u32[]{:S(2)}, u32[]{:S(2)}) collective-permute-start(f32[2,1]{1,0:T(2,128)S(1)} %slice.133), channel_id=1, source_target_pairs={{0,16},{16,32},{32,48},{48,64},{64,80},{80,96},{96,112},{112,128},... | collective-permute-start | bytes 32 | tf_op jit(solution)/shard_map/ppermute | solution.py:23
  105.2 0.7 pad_maximum_fusion.1
  105.9 5.0 %collective-permute-done.3 = f32[2,1]{1,0:T(2,128)S(1)} collective-permute-done((f32[2,1]{1,0:T(2,128)S(1)}, f32[2,1]{1,0:T(2,128)S(1)}, u32[]{:S(2)}, u32[]{:S(2)}) %collective-permute-start.3) | collective-permute-done | bytes 40 | tf_op jit(solution)/shard_map/ppermute | solution.py:23
  110.9 0.6 pad_maximum_fusion.4
  (60 shorter events, 4.6 us)
Async XLA Ops:
  8.5 22.4 %copy-start.2 = (f32[96]{0:T(128)S(1)}, f32[96]{0:T(128)}, u32[]{:S(2)}) copy-start(f32[96]{0:T(128)} %param.19) | copy-start | bytes 1156
  10.5 19.8 %all-to-all-start = ((f32[4,32,256]{2,0,1:T(4,128)}), f32[4,32,256]{2,0,1:T(4,128)S(1)}, u32[]{:S(2)}, u32[]{:S(2)}) async-start(f32[4,32,256]{2,0,1:T(4,128)} %copy.25), calls=%async_computation | async-start | bytes 262144 | tf_op jit(solution)/shard_map/all_to_all | solution.py:145
  33.0 9.8 %copy-start.3 = (f32[96]{0:T(128)S(1)}, f32[96]{0:T(128)}, u32[]{:S(2)}) copy-start(f32[96]{0:T(128)} %param.18) | copy-start | bytes 1156
  33.0 10.9 %collective-permute-start = (f32[96,96]{0,1:T(8,128)S(1)}, f32[96,96]{0,1:T(8,128)S(1)}, u32[]{:S(2)}, u32[]{:S(2)}) collective-permute-start(f32[96,96]{0,1:T(8,128)S(1)} %get-tuple-element.38), channel_id=1, source_target_pairs={{0,16},{16,32},{32,48},{48,64},{64,80},{80,96},{96,112},{112,128},... | collective-permute-start | bytes 110600 | tf_op jit(solution)/shard_map/ppermute | solution.py:23
  37.1 46.3 %copy-start = (f32[96,96]{1,0:T(8,128)S(1)}, f32[96,96]{1,0:T(8,128)}, u32[]{:S(2)}) copy-start(f32[96,96]{1,0:T(8,128)} %param.21) | copy-start | bytes 110596
  37.1 46.3 %copy-start.1 = (f32[96,96]{1,0:T(8,128)S(1)}, f32[96,96]{1,0:T(8,128)}, u32[]{:S(2)}) copy-start(f32[96,96]{1,0:T(8,128)} %param.20) | copy-start | bytes 110596
  37.1 7.3 %collective-permute-start.1 = (f32[96,96]{0,1:T(8,128)S(1)}, f32[96,96]{0,1:T(8,128)S(1)}, u32[]{:S(2)}, u32[]{:S(2)}) collective-permute-start(f32[96,96]{0,1:T(8,128)S(1)} %get-tuple-element.37), channel_id=1, source_target_pairs={{16,0},{32,16},{48,32},{64,48},{80,64},{96,80},{112,96},{128,112},... | collective-permute-start | bytes 110600 | tf_op jit(solution)/shard_map/ppermute | solution.py:23
  89.0 11.2 %all-to-all-start.3 = ((f32[16,2,4]{2,1,0:T(2,128)}), f32[16,2,4]{2,1,0:T(2,128)S(1)}, u32[]{:S(2)}, u32[]{:S(2)}) async-start(f32[16,2,4]{2,1,0:T(2,128)} %broadcast_in_dim.170), calls=%async_computation.3 | async-start | bytes 32768 | tf_op jit(solution)/shard_map/all_to_all | solution.py:74
  92.8 7.9 %collective-permute-start.2 = (f32[2,1]{1,0:T(2,128)S(1)}, f32[2,1]{1,0:T(2,128)S(1)}, u32[]{:S(2)}, u32[]{:S(2)}) collective-permute-start(f32[2,1]{1,0:T(2,128)S(1)} %slice.129), channel_id=1, source_target_pairs={{0,16},{16,32},{32,48},{48,64},{64,80},{80,96},{96,112},{112,128},... | collective-permute-start | bytes 32 | tf_op jit(solution)/shard_map/ppermute | solution.py:23
  103.3 7.6 %collective-permute-start.3 = (f32[2,1]{1,0:T(2,128)S(1)}, f32[2,1]{1,0:T(2,128)S(1)}, u32[]{:S(2)}, u32[]{:S(2)}) collective-permute-start(f32[2,1]{1,0:T(2,128)S(1)} %slice.133), channel_id=1, source_target_pairs={{0,16},{16,32},{32,48},{48,64},{64,80},{80,96},{96,112},{112,128},... | collective-permute-start | bytes 32 | tf_op jit(solution)/shard_map/ppermute | solution.py:23

commit v4 on v3

--- a/solution.py
+++ b/solution.py
@@ -157,17 +157,10 @@
     row_key = got_slice * grid_x + got_x
     weight_bf16 = arrived_weight.astype(jnp.bfloat16)
 
-    edge_targets = jnp.concatenate(
-        [
-            jnp.arange(grid_x, dtype=jnp.int32),
-            jnp.arange(grid_x, dtype=jnp.int32) + (SL_DEV - 1) * grid_x,
-        ]
-    )
-    edges = deposit_rows(weight_bf16, row_key, got_y, edge_targets, grid_y)
-    below = shifted(edges[grid_x:], "ta", 1)
-    above = shifted(edges[:grid_x], "ta", -1)
-    middle_targets = jnp.arange(grid_x, (SL_DEV - 1) * grid_x, dtype=jnp.int32)
-    middle = deposit_rows(weight_bf16, row_key, got_y, middle_targets, grid_y)
+    density_rows = SL_DEV * grid_x
+    partial = deposit_rows(
+        weight_bf16, row_key, got_y, jnp.arange(density_rows, dtype=jnp.int32), grid_y
+    )
 
     profile = lookup(mode_x, got_x) * lookup(mode_y, got_y)
     weighted = arrived_weight * profile
@@ -189,14 +182,17 @@
 
     cosine0, sine0, sums0 = local_bunching(got_phase)
     sums_row = jnp.pad(sums0.reshape(1, 2 * SL_DEV), ((0, 7), (0, grid_y - 2 * SL_DEV)))
-    stacked = jnp.concatenate([below, edges[:grid_x], middle, edges[grid_x:], above, sums_row])
+    stacked = jnp.concatenate([partial, sums_row])
     chunk_rows = -(-stacked.shape[0] // (splits * 8)) * 8
     stacked = jnp.pad(stacked, ((0, chunk_rows * splits - stacked.shape[0]), (0, 0)))
     summed = pb_sum(stacked, "pb")
-    density_rows = (SL_DEV + 2) * grid_x
-    extended = summed[:density_rows].reshape(SL_DEV + 2, grid_x, grid_y)
+    density = summed[:density_rows].reshape(SL_DEV, grid_x, grid_y)
     bunching0 = summed[density_rows, : 2 * SL_DEV].reshape(2, SL_DEV)
-    force_map = stencil(extended, along_coeff, across_coeff)
+
+    below = shifted(density[SL_DEV - 1], "ta", 1)
+    above = shifted(density[0], "ta", -1)
+    empty = jnp.zeros((1, grid_x, grid_y), jnp.float32)
+    force_map = stencil(jnp.concatenate([empty, density, empty]), along_coeff, across_coeff)
 
     force_rows = force_map.reshape(SL_DEV * grid_x, grid_y)
     force_hi = lax.reduce_precision(force_rows, exponent_bits=8, mantissa_bits=7)
@@ -209,7 +205,24 @@
     picked = jnp.dot(pick_row, force_parts, preferred_element_type=jnp.float32)
     picked = picked[:, :grid_y] + picked[:, grid_y:]
     pick_col = got_y[:, None] == jnp.arange(grid_y, dtype=jnp.int32)[None, :]
-    kicked = got_energy + jnp.sum(jnp.where(pick_col, picked, 0.0), axis=1)
+    force_here = jnp.sum(jnp.where(pick_col, picked, 0.0), axis=1)
+    halo_force = jnp.concatenate([-along_coeff * below, along_coeff * above]).reshape(
+        2 * grid_x, grid_y
+    )
+    halo_hi = lax.reduce_precision(halo_force, exponent_bits=8, mantissa_bits=7)
+    halo_parts = jnp.concatenate(
+        [halo_hi.astype(jnp.bfloat16), (halo_force - halo_hi).astype(jnp.bfloat16)], axis=1
+    )
+    halo_key = jnp.where(
+        got_slice == 0, got_x, jnp.where(got_slice == SL_DEV - 1, got_x + grid_x, -1)
+    )
+    pick_halo = (halo_key[:, None] == jnp.arange(2 * grid_x, dtype=jnp.int32)[None, :]).astype(
+        jnp.bfloat16
+    )
+    halo_picked = jnp.dot(pick_halo, halo_parts, preferred_element_type=jnp.float32)
+    halo_picked = halo_picked[:, :grid_y] + halo_picked[:, grid_y:]
+    halo_here = jnp.sum(jnp.where(pick_col, halo_picked, 0.0), axis=1)
+    kicked = got_energy + (force_here + halo_here)
 
     couple = 1.0 / math.sqrt(splits * PS_DEV)
     radiation = jnp.zeros((2, SL_DEV), jnp.float32)

time: 112 us -> 108 us (0.964)
  the two profiles are of different devices: /device:TPU:8 before, /device:TPU:32 now
where the time goes in v4:
time: 108 us; the launch traced here: 107 us
  blocking collectives  51.2 us (47%)
  other arithmetic  15.4 us (14%)
  starting transfers between devices  14.6 us (14%)
  waiting for transfers between devices  14.3 us (13%)
  matrix products  8.5 us (8%)
  local copies, waits for them, and re-layouts  1.91 us (2%)
    all_to_all x1, blocking collectives, pb_sum(): mine = jnp.sum(lax.all_to_all(chunks, axis, 0, 0, tiled=True), axis=0)  21.4 us
    all_to_all x1, blocking collectives, body(): lax.all_to_all(send.reshape(value_count, groups, capacity), 'ta', split_a...  15.4 us
    all_to_all x1, blocking collectives, pb_sum(): lax.all_to_all(jnp.broadcast_to(mine[None], chunks.shape), axis, 0, 0, ti...  14.4 us
    ppermute x4, starting transfers between devices, shifted(): lax.ppermute(value, axis, [(source, source + steps) for source in range(l...  11.1 us
    ppermute x4, waiting for transfers between devices, shifted(): lax.ppermute(value, axis, [(source, source + steps) for source in range(l...  8.79 us
    all_to_all x1, waiting for transfers between devices, pb_sum_small(): return jnp.sum(lax.all_to_all(spread, axis, 0, 0, tiled=True), axis=0)  5.47 us
    all_to_all x1, starting transfers between devices, pb_sum_small(): return jnp.sum(lax.all_to_all(spread, axis, 0, 0, tiled=True), axis=0)  3.49 us
    dot_general x1, matrix products, body(): picked = jnp.dot(pick_row, force_parts, preferred_element_type=jnp.float32)  3.34 us
  transfers between devices with their start and end apart: 5, of which 4 were waited for; matrix products, arithmetic and copies ran while one was open for 6% of the time, Pallas kernels for 0%

profile of v4, /device:TPU:32, one launch (start us, length us, event | category | flops | bytes accessed | tf_op | source)
XLA Modules:
  0.0 106.9 jit_solution(4428064636269073621)
XLA Ops:
  0.6 0.5 broadcast.513
  1.1 1.4 %reduce.9 = s32[4096]{0:T(1024)S(1)} reduce(s32[4096,1]{0,1:T(1,128)} %param.14, s32[]{:T(128)} %broadcast.513), dimensions={1}, to_apply=%param.14.reduce_sub_computation.3 | reduce | bytes 32772 | tf_op args[3]
  2.9 0.4 fusion.23
  3.2 0.7 stack.47
  4.0 0.8 iota_compare_fusion.16
  4.7 0.8 add_select_fusion.5
  5.5 1.2 %select_reduce_fusion.2 = (f32[4096]{0:T(1024)S(1)}, f32[4096]{0:T(1024)S(1)}) fusion(f32[96]{0:T(128)} %param.17, s32[4096]{0:T(1024)S(1)} %get-tuple-element.50, f32[96]{0:T(128)} %param.16, s32[4096]{0:T(1024)S(1)} %get-tuple-element.52), kind=kLoop, calls=%fused_computation.32 | loop fusion | flops 2351104 | bytes 66304 | tf_op jit(solution)/shard_map/reduce_sum | solution.py:28
  6.8 1.3 %multiply_add_fusion.4 = (f32[1,4096]{1,0:T(1,128)S(1)}, f32[1,4096]{1,0:T(1,128)S(1)}) fusion(f32[2,4096]{1,0:T(2,128)} %param.11, f32[1,4096]{1,0:T(1,128)S(1)} %bitcast.78), kind=kLoop, calls=%fused_computation.126 | loop fusion | flops 16384 | bytes 81920 | tf_op jit(solution)/shard_map/add | solution.py:116
  8.1 0.3 broadcast_select_fusion.2
  8.5 1.2 %fusion.7 = f32[384,256]{1,0:T(8,128)S(1)} fusion(bf16[128,4096]{1,0:T(8,128)(2,1)S(1)} %bitcast.54, bf16[128,4096]{1,0:T(8,128)(2,1)S(1)} %bitcast.53, bf16[128,4096]{1,0:T(8,128)(2,1)S(1)} %bitcast.52, s32[4096]{0:T(1024)S(1)} %bitcast.83), kind=kOutput, calls=%fused_computation.10 | convolution fusion | flops 815792128 | bytes 3555328 | tf_op jit(solution)/shard_map/dot_general | solution.py:142
  9.9 15.4 %all_to_all.20 = f32[4,32,256]{2,0,1:T(4,128)S(1)} all-to-all(f32[4,32,256]{2,0,1:T(4,128)S(1)} %copy.25), channel_id=1, replica_groups=mesh['ta'=32,'pb'=16] {'ta'}, dimensions={1} | all-to-all | bytes 262144 | tf_op jit(solution)/shard_map/all_to_all | solution.py:145
  25.9 0.6 select_reduce_fusion.1
  26.5 0.6 select_reduce_fusion
  27.6 2.1 %fusion.2 = f32[384,96]{0,1:T(8,128)S(1)} fusion(s32[8192]{0:T(1024)S(1)} %get-tuple-element.47, bf16[8192]{0:T(1024)(128)(2,1)S(1)} %convert_element_type.111, s32[8192]{0:T(1024)S(1)} %get-tuple-element.49), kind=kOutput, calls=%fused_computation.4 | convolution fusion | flops 611057664 | bytes 229376 | tf_op jit(solution)/shard_map/dot_general | solution.py:60
  29.9 21.4 %all_to_all.21 = f32[16,32,96]{2,1,0:T(8,128)S(1)} all-to-all(f32[16,32,96]{2,1,0:T(8,128)S(1)} %bitcast.55), channel_id=1, replica_groups=mesh['ta'=32,'pb'=16] {'pb'}, dimensions={0} | all-to-all | bytes 393216 | tf_op jit(solution)/shard_map/all_to_all | solution.py:66
  51.3 14.4 %all_to_all.22 = f32[16,32,96]{2,1,0:T(8,128)S(1)} all-to-all(f32[16,32,96]{2,1,0:T(8,128)S(1)} %broadcast_in_dim.165), channel_id=1, replica_groups=mesh['ta'=32,'pb'=16] {'pb'}, dimensions={0} | all-to-all | bytes 393216 | tf_op jit(solution)/shard_map/all_to_all | solution.py:67
  66.1 5.2 %collective-permute-start.1 = (f32[96,96]{1,0:T(8,128)S(1)}, f32[96,96]{1,0:T(8,128)S(1)}, u32[]{:S(2)}, u32[]{:S(2)}) collective-permute-start(f32[96,96]{1,0:T(8,128)S(1)} %bitcast.82), channel_id=1, source_target_pairs={{16,0},{32,16},{48,32},{64,48},{80,64},{96,80},{112,96},{128,112},... | collective-permute-start | bytes 110600 | tf_op jit(solution)/shard_map/ppermute | solution.py:23
  71.3 2.1 %collective-permute-start = (f32[96,96]{1,0:T(8,128)S(1)}, f32[96,96]{1,0:T(8,128)S(1)}, u32[]{:S(2)}, u32[]{:S(2)}) collective-permute-start(f32[96,96]{1,0:T(8,128)S(1)} %bitcast.81), channel_id=1, source_target_pairs={{0,16},{16,32},{32,48},{48,64},{64,80},{80,96},{96,112},{112,128},... | collective-permute-start | bytes 110600 | tf_op jit(solution)/shard_map/ppermute | solution.py:23
  73.4 3.3 %fusion = f32[8192,192]{0,1:T(8,128)S(1)} fusion(s32[8192]{0:T(1024)S(1)} %get-tuple-element.47, bf16[384,96]{1,0:T(8,128)(2,1)S(1)} %get-tuple-element.29, bf16[384,96]{1,0:T(8,128)(2,1)S(1)} %get-tuple-element.28), kind=kOutput, calls=%fused_computation.2 | convolution fusion | flops 1211400192 | bytes 6471680 | tf_op jit(solution)/shard_map/dot_general | solution.py:205
  77.0 3.7 %collective-permute-done = f32[96,96]{1,0:T(8,128)S(1)} collective-permute-done((f32[96,96]{1,0:T(8,128)S(1)}, f32[96,96]{1,0:T(8,128)S(1)}, u32[]{:S(2)}, u32[]{:S(2)}) %collective-permute-start) | collective-permute-done | bytes 36896 | tf_op jit(solution)/shard_map/ppermute | solution.py:23
  80.8 1.5 %fusion.6 = f32[8192,192]{0,1:T(8,128)S(1)} fusion(s32[8192]{0:T(1024)S(1)} %get-tuple-element.18, bf16[192,96]{1,0:T(8,128)(2,1)S(1)} %get-tuple-element.41, bf16[192,96]{1,0:T(8,128)(2,1)S(1)} %get-tuple-element.40), kind=kOutput, calls=%fused_computation.8 | convolution fusion | flops 605700096 | bytes 6397952 | tf_op jit(solution)/shard_map/dot_general | solution.py:222
  82.2 1.4 %fusion.9 = (f32[8192]{0:T(1024)S(1)}, f32[8192]{0:T(1024)S(1)}) fusion(f32[8192,192]{0,1:T(8,128)S(1)} %fusion.6, s32[8192]{0:T(1024)S(1)} %get-tuple-element.49, f32[8192,192]{0,1:T(8,128)S(1)} %fusion), kind=kLoop, calls=%fused_computation.13 | loop fusion | flops 5488640 | bytes 12681216 | tf_op jit(solution)/shard_map/reduce_sum | solution.py:224
  84.3 0.6 broadcast_in_dim.167
  84.9 3.5 %all-to-all-start.3 = ((f32[16,2,4]{2,1,0:T(2,128)}), f32[16,2,4]{2,1,0:T(2,128)S(1)}, u32[]{:S(2)}, u32[]{:S(2)}) async-start(f32[16,2,4]{2,1,0:T(2,128)} %broadcast_in_dim.167), calls=%async_computation.3 | async-start | bytes 32768 | tf_op jit(solution)/shard_map/all_to_all | solution.py:74
  88.5 1.9 %collective-permute-start.2 = (f32[2,1]{1,0:T(2,128)S(1)}, f32[2,1]{1,0:T(2,128)S(1)}, u32[]{:S(2)}, u32[]{:S(2)}) collective-permute-start(f32[2,1]{1,0:T(2,128)S(1)} %slice.132), channel_id=1, source_target_pairs={{0,16},{16,32},{32,48},{48,64},{64,80},{80,96},{96,112},{112,128},... | collective-permute-start | bytes 32 | tf_op jit(solution)/shard_map/ppermute | solution.py:23
  90.5 5.5 %all-to-all-done.3 = f32[16,2,4]{2,1,0:T(2,128)S(1)} async-done(((f32[16,2,4]{2,1,0:T(2,128)}), f32[16,2,4]{2,1,0:T(2,128)S(1)}, u32[]{:S(2)}, u32[]{:S(2)}) %all-to-all-start.3) | async-done | bytes 544 | tf_op jit(solution)/shard_map/all_to_all | solution.py:74
  96.0 1.4 %collective-permute-done.2 = f32[2,1]{1,0:T(2,128)S(1)} collective-permute-done((f32[2,1]{1,0:T(2,128)S(1)}, f32[2,1]{1,0:T(2,128)S(1)}, u32[]{:S(2)}, u32[]{:S(2)}) %collective-permute-start.2) | collective-permute-done | bytes 40 | tf_op jit(solution)/shard_map/ppermute | solution.py:23
  97.5 1.9 %collective-permute-start.3 = (f32[2,1]{1,0:T(2,128)S(1)}, f32[2,1]{1,0:T(2,128)S(1)}, u32[]{:S(2)}, u32[]{:S(2)}) collective-permute-start(f32[2,1]{1,0:T(2,128)S(1)} %slice.136), channel_id=1, source_target_pairs={{0,16},{16,32},{32,48},{48,64},{64,80},{80,96},{96,112},{112,128},... | collective-permute-start | bytes 32 | tf_op jit(solution)/shard_map/ppermute | solution.py:23
  99.6 2.2 %add_select_fusion.4 = (f32[1,8192]{1,0:T(1,128)S(1)}, f32[1,8192]{1,0:T(1,128)S(1)}) fusion(pred[1,8192]{1,0:T(4,128)(4,1)S(1)} %bitcast.64, f32[1,8192]{1,0:T(1,128)S(1)} %bitcast.59, f32[1,8192]{1,0:T(1,128)S(1)} %bitcast.76, f32[1,8192]{1,0:T(1,128)S(1)} %bitcast.74, f32[1,8192]{1,0:T(1,128)S(1)} %bitcast.73, f32[1,8192]{1,0:T(1,128)S(1)} %bitcast.69, ...), kind=kLoop, calls=%fused_computation.101 | loop fusion | flops 147456 | bytes 335872 | tf_op jit(solution)/shard_map/jit(_where)/select_n | solution.py:243
  101.9 0.7 pad_maximum_fusion.2
  102.6 3.7 %collective-permute-done.3 = f32[2,1]{1,0:T(2,128)S(1)} collective-permute-done((f32[2,1]{1,0:T(2,128)S(1)}, f32[2,1]{1,0:T(2,128)S(1)}, u32[]{:S(2)}, u32[]{:S(2)}) %collective-permute-start.3) | collective-permute-done | bytes 40 | tf_op jit(solution)/shard_map/ppermute | solution.py:23
  106.3 0.6 pad_maximum_fusion.5
  (57 shorter events, 3.7 us)
Async XLA Ops:
  8.5 17.4 %copy-start.2 = (f32[96]{0:T(128)S(1)}, f32[96]{0:T(128)}, u32[]{:S(2)}) copy-start(f32[96]{0:T(128)} %param.18) | copy-start | bytes 1156
  8.5 18.0 %copy-start.3 = (f32[96]{0:T(128)S(1)}, f32[96]{0:T(128)}, u32[]{:S(2)}) copy-start(f32[96]{0:T(128)} %param.19) | copy-start | bytes 1156
  29.7 36.1 %copy-start = (f32[96,96]{1,0:T(8,128)S(1)}, f32[96,96]{1,0:T(8,128)}, u32[]{:S(2)}) copy-start(f32[96,96]{1,0:T(8,128)} %param.20) | copy-start | bytes 110596
  29.7 36.1 %copy-start.1 = (f32[96,96]{1,0:T(8,128)S(1)}, f32[96,96]{1,0:T(8,128)}, u32[]{:S(2)}) copy-start(f32[96,96]{1,0:T(8,128)} %param.21) | copy-start | bytes 110596
  66.1 10.9 %collective-permute-start.1 = (f32[96,96]{1,0:T(8,128)S(1)}, f32[96,96]{1,0:T(8,128)S(1)}, u32[]{:S(2)}, u32[]{:S(2)}) collective-permute-start(f32[96,96]{1,0:T(8,128)S(1)} %bitcast.82), channel_id=1, source_target_pairs={{16,0},{32,16},{48,32},{64,48},{80,64},{96,80},{112,96},{128,112},... | collective-permute-start | bytes 110600 | tf_op jit(solution)/shard_map/ppermute | solution.py:23
  71.3 9.4 %collective-permute-start = (f32[96,96]{1,0:T(8,128)S(1)}, f32[96,96]{1,0:T(8,128)S(1)}, u32[]{:S(2)}, u32[]{:S(2)}) collective-permute-start(f32[96,96]{1,0:T(8,128)S(1)} %bitcast.81), channel_id=1, source_target_pairs={{0,16},{16,32},{32,48},{48,64},{64,80},{80,96},{96,112},{112,128},... | collective-permute-start | bytes 110600 | tf_op jit(solution)/shard_map/ppermute | solution.py:23
  84.9 11.1 %all-to-all-start.3 = ((f32[16,2,4]{2,1,0:T(2,128)}), f32[16,2,4]{2,1,0:T(2,128)S(1)}, u32[]{:S(2)}, u32[]{:S(2)}) async-start(f32[16,2,4]{2,1,0:T(2,128)} %broadcast_in_dim.167), calls=%async_computation.3 | async-start | bytes 32768 | tf_op jit(solution)/shard_map/all_to_all | solution.py:74
  88.5 8.8 %collective-permute-start.2 = (f32[2,1]{1,0:T(2,128)S(1)}, f32[2,1]{1,0:T(2,128)S(1)}, u32[]{:S(2)}, u32[]{:S(2)}) collective-permute-start(f32[2,1]{1,0:T(2,128)S(1)} %slice.132), channel_id=1, source_target_pairs={{0,16},{16,32},{32,48},{48,64},{64,80},{80,96},{96,112},{112,128},... | collective-permute-start | bytes 32 | tf_op jit(solution)/shard_map/ppermute | solution.py:23
  97.5 8.8 %collective-permute-start.3 = (f32[2,1]{1,0:T(2,128)S(1)}, f32[2,1]{1,0:T(2,128)S(1)}, u32[]{:S(2)}, u32[]{:S(2)}) collective-permute-start(f32[2,1]{1,0:T(2,128)S(1)} %slice.136), channel_id=1, source_target_pairs={{0,16},{16,32},{32,48},{48,64},{64,80},{80,96},{96,112},{112,128},... | collective-permute-start | bytes 32 | tf_op jit(solution)/shard_map/ppermute | solution.py:23

commit v5 on v4

--- a/solution.py
+++ b/solution.py
@@ -56,8 +56,10 @@
     left = jnp.where(
         row_key[None, :] == targets[:, None], weight_bf16[None, :], jnp.zeros((), jnp.bfloat16)
     )
-    right = (col[:, None] == jnp.arange(grid_y, dtype=jnp.int32)[None, :]).astype(jnp.bfloat16)
-    return jnp.dot(left, right, preferred_element_type=jnp.float32)
+    right = (jnp.arange(grid_y, dtype=jnp.int32)[:, None] == col[None, :]).astype(jnp.bfloat16)
+    return lax.dot_general(
+        left, right, (((1,), (1,)), ((), ())), preferred_element_type=jnp.float32
+    )
 
 
 def pb_sum(rows, axis):
@@ -189,55 +191,55 @@
     density = summed[:density_rows].reshape(SL_DEV, grid_x, grid_y)
     bunching0 = summed[density_rows, : 2 * SL_DEV].reshape(2, SL_DEV)
 
-    below = shifted(density[SL_DEV - 1], "ta", 1)
+    couple = 1.0 / math.sqrt(splits * PS_DEV)
+    radiation0 = couple * bunching0
+    last_row = jnp.pad(radiation0[:, -1:].reshape(1, 2), ((0, 7), (0, grid_y - 2)))
+    halo_below = shifted(jnp.concatenate([density[SL_DEV - 1], last_row]), "ta", 1)
     above = shifted(density[0], "ta", -1)
     empty = jnp.zeros((1, grid_x, grid_y), jnp.float32)
     force_map = stencil(jnp.concatenate([empty, density, empty]), along_coeff, across_coeff)
 
-    force_rows = force_map.reshape(SL_DEV * grid_x, grid_y)
-    force_hi = lax.reduce_precision(force_rows, exponent_bits=8, mantissa_bits=7)
-    force_parts = jnp.concatenate(
-        [force_hi.astype(jnp.bfloat16), (force_rows - force_hi).astype(jnp.bfloat16)], axis=1
-    )
-    pick_row = (row_key[:, None] == jnp.arange(SL_DEV * grid_x, dtype=jnp.int32)[None, :]).astype(
-        jnp.bfloat16
-    )
-    picked = jnp.dot(pick_row, force_parts, preferred_element_type=jnp.float32)
-    picked = picked[:, :grid_y] + picked[:, grid_y:]
-    pick_col = got_y[:, None] == jnp.arange(grid_y, dtype=jnp.int32)[None, :]
-    force_here = jnp.sum(jnp.where(pick_col, picked, 0.0), axis=1)
-    halo_force = jnp.concatenate([-along_coeff * below, along_coeff * above]).reshape(
+    def pick(table, key, key_count):
+        table_hi = lax.reduce_precision(table, exponent_bits=8, mantissa_bits=7)
+        table_parts = jnp.concatenate(
+            [table_hi.astype(jnp.bfloat16), (table - table_hi).astype(jnp.bfloat16)], axis=1
+        ).T
+        pick_row = (jnp.arange(key_count, dtype=jnp.int32)[:, None] == key[None, :]).astype(
+            jnp.bfloat16
+        )
+        picked = jnp.dot(table_parts, pick_row, preferred_element_type=jnp.float32)
+        picked = picked[:grid_y] + picked[grid_y:]
+        return jnp.sum(jnp.where(pick_col, picked, 0.0), axis=0)
+
+    pick_col = jnp.arange(grid_y, dtype=jnp.int32)[:, None] == got_y[None, :]
+    force_here = pick(force_map.reshape(SL_DEV * grid_x, grid_y), row_key, SL_DEV * grid_x)
+    below_density = halo_below[:grid_x]
+    halo_force = jnp.concatenate([-along_coeff * below_density, along_coeff * above]).reshape(
         2 * grid_x, grid_y
-    )
-    halo_hi = lax.reduce_precision(halo_force, exponent_bits=8, mantissa_bits=7)
-    halo_parts = jnp.concatenate(
-        [halo_hi.astype(jnp.bfloat16), (halo_force - halo_hi).astype(jnp.bfloat16)], axis=1
     )
     halo_key = jnp.where(
         got_slice == 0, got_x, jnp.where(got_slice == SL_DEV - 1, got_x + grid_x, -1)
     )
-    pick_halo = (halo_key[:, None] == jnp.arange(2 * grid_x, dtype=jnp.int32)[None, :]).astype(
-        jnp.bfloat16
-    )
-    halo_picked = jnp.dot(pick_halo, halo_parts, preferred_element_type=jnp.float32)
-    halo_picked = halo_picked[:, :grid_y] + halo_picked[:, grid_y:]
-    halo_here = jnp.sum(jnp.where(pick_col, halo_picked, 0.0), axis=1)
+    halo_here = pick(halo_force, halo_key, 2 * grid_x)
     kicked = got_energy + (force_here + halo_here)
 
-    couple = 1.0 / math.sqrt(splits * PS_DEV)
     radiation = jnp.zeros((2, SL_DEV), jnp.float32)
     for period in range(PERIODS):
         if period == 0:
-            cosine, sine_part, bunching = cosine0, sine0, bunching0
+            cosine, sine_part = cosine0, sine0
+            radiation = radiation + radiation0
         else:
             cosine, sine_part, local_sums = local_bunching(got_phase)
             bunching = pb_sum_small(local_sums, "pb")
-        radiation = radiation + couple * bunching
+            radiation = radiation + couple * bunching
         real_here = jnp.sum(select * radiation[0][:, None], axis=0)
         imag_here = jnp.sum(select * radiation[1][:, None], axis=0)
         kicked = kicked + KICK_GAIN * profile * (real_here * cosine - imag_here * sine_part)
         got_phase = got_phase + SLIP_GAIN * kicked
-        incoming = shifted(radiation[:, -1:], "ta", 1)
+        if period == 0:
+            incoming = halo_below[grid_x, :2].reshape(2, 1)
+        else:
+            incoming = shifted(radiation[:, -1:], "ta", 1)
         radiation = jnp.concatenate([incoming, radiation[:, :-1]], axis=1)
     filled = arrived_weight > 0
     result = jnp.stack([jnp.where(filled, got_phase, 0.0), jnp.where(filled, kicked, 0.0)])

time: 108 us -> 106 us (0.981)
  the two profiles are of different devices: /device:TPU:32 before, /device:TPU:8 now
where the time goes in v5:
time: 106 us; the launch traced here: 105 us
  blocking collectives  55.3 us (52%)
  other arithmetic  15.4 us (15%)
  starting transfers between devices  13.5 us (13%)
  waiting for transfers between devices  9.96 us (9%)
  matrix products  8.04 us (8%)
  local copies, waits for them, and re-layouts  2.12 us (2%)
    all_to_all x1, blocking collectives, pb_sum(): mine = jnp.sum(lax.all_to_all(chunks, axis, 0, 0, tiled=True), axis=0)  21.4 us
    all_to_all x1, blocking collectives, body(): lax.all_to_all(send.reshape(value_count, groups, capacity), 'ta', split_a...  19.6 us
    all_to_all x1, blocking collectives, pb_sum(): lax.all_to_all(jnp.broadcast_to(mine[None], chunks.shape), axis, 0, 0, ti...  14.4 us
    ppermute x3, starting transfers between devices, shifted(): lax.ppermute(value, axis, [(source, source + steps) for source in range(l...  10 us
    all_to_all x1, waiting for transfers between devices, pb_sum_small(): return jnp.sum(lax.all_to_all(spread, axis, 0, 0, tiled=True), axis=0)  7.47 us
    dot_general x2, matrix products, pick(): picked = jnp.dot(table_parts, pick_row, preferred_element_type=jnp.float32)  4.36 us
    all_to_all x1, starting transfers between devices, pb_sum_small(): return jnp.sum(lax.all_to_all(spread, axis, 0, 0, tiled=True), axis=0)  3.49 us
    ppermute x3, waiting for transfers between devices, shifted(): lax.ppermute(value, axis, [(source, source + steps) for source in range(l...  2.49 us
  transfers between devices with their start and end apart: 4, of which 2 were waited for; matrix products, arithmetic and copies ran while one was open for 6% of the time, Pallas kernels for 0%

profile of v5, /device:TPU:8, one launch (start us, length us, event | category | flops | bytes accessed | tf_op | source)
XLA Modules:
  0.0 105.4 jit_solution(10640612867348210731)
XLA Ops:
  0.6 0.7 stack.47
  1.3 0.8 iota_compare_fusion.16
  2.1 0.5 broadcast.440
  2.6 1.4 %reduce.11 = s32[4096]{0:T(1024)S(1)} reduce(s32[4096,1]{0,1:T(1,128)} %param.14, s32[]{:T(128)} %broadcast.440), dimensions={1}, to_apply=%param.14.reduce_sub_computation.3 | reduce | bytes 32772 | tf_op args[3]
  4.4 0.4 fusion.23
  4.7 0.8 add_select_fusion.5
  5.5 1.2 %select_reduce_fusion.2 = (f32[4096]{0:T(1024)S(1)}, f32[4096]{0:T(1024)S(1)}) fusion(f32[96]{0:T(128)} %param.17, s32[4096]{0:T(1024)S(1)} %get-tuple-element.50, f32[96]{0:T(128)} %param.16, s32[4096]{0:T(1024)S(1)} %get-tuple-element.52), kind=kLoop, calls=%fused_computation.32 | loop fusion | flops 2351104 | bytes 66304 | tf_op jit(solution)/shard_map/reduce_sum | solution.py:28
  6.7 1.3 %multiply_add_fusion.4 = (f32[1,4096]{1,0:T(1,128)S(1)}, f32[1,4096]{1,0:T(1,128)S(1)}) fusion(f32[2,4096]{1,0:T(2,128)} %param.11, f32[1,4096]{1,0:T(1,128)S(1)} %bitcast.82), kind=kLoop, calls=%fused_computation.128 | loop fusion | flops 16384 | bytes 81920 | tf_op jit(solution)/shard_map/add | solution.py:118
  8.1 0.3 broadcast_select_fusion.2
  8.5 1.2 %fusion.7 = f32[384,256]{1,0:T(8,128)S(1)} fusion(bf16[128,4096]{1,0:T(8,128)(2,1)S(1)} %bitcast.57, bf16[128,4096]{1,0:T(8,128)(2,1)S(1)} %bitcast.56, bf16[128,4096]{1,0:T(8,128)(2,1)S(1)} %bitcast.55, s32[4096]{0:T(1024)S(1)} %bitcast.86), kind=kOutput, calls=%fused_computation.10 | convolution fusion | flops 815792128 | bytes 3555328 | tf_op jit(solution)/shard_map/dot_general | solution.py:144
  9.8 19.6 %all_to_all.20 = f32[4,32,256]{2,0,1:T(4,128)S(1)} all-to-all(f32[4,32,256]{2,0,1:T(4,128)S(1)} %copy.30), channel_id=1, replica_groups=mesh['ta'=32,'pb'=16] {'ta'}, dimensions={1} | all-to-all | bytes 262144 | tf_op jit(solution)/shard_map/all_to_all | solution.py:147
  30.1 0.6 select_reduce_fusion
  30.6 0.6 select_reduce_fusion.1
  31.8 2.1 %fusion.2 = f32[384,96]{0,1:T(8,128)S(1)} fusion(s32[8192]{0:T(1024)S(1)} %get-tuple-element.47, bf16[8192]{0:T(1024)(128)(2,1)S(1)} %convert_element_type.106, s32[8192]{0:T(1024)S(1)} %get-tuple-element.49), kind=kOutput, calls=%fused_computation.4 | convolution fusion | flops 611057664 | bytes 229376 | tf_op jit(solution)/shard_map/dot_general | solution.py:60
  34.1 21.4 %all_to_all.21 = f32[16,32,96]{2,1,0:T(8,128)S(1)} all-to-all(f32[16,32,96]{2,1,0:T(8,128)S(1)} %bitcast.58), channel_id=1, replica_groups=mesh['ta'=32,'pb'=16] {'pb'}, dimensions={0} | all-to-all | bytes 393216 | tf_op jit(solution)/shard_map/all_to_all | solution.py:68
  55.5 14.4 %all_to_all.22 = f32[16,32,96]{2,1,0:T(8,128)S(1)} all-to-all(f32[16,32,96]{2,1,0:T(8,128)S(1)} %broadcast_in_dim.163), channel_id=1, replica_groups=mesh['ta'=32,'pb'=16] {'pb'}, dimensions={0} | all-to-all | bytes 393216 | tf_op jit(solution)/shard_map/all_to_all | solution.py:69
  70.4 2.5 %collective-permute-start = (f32[104,96]{1,0:T(8,128)S(1)}, f32[104,96]{1,0:T(8,128)S(1)}, u32[]{:S(2)}, u32[]{:S(2)}) collective-permute-start(f32[104,96]{1,0:T(8,128)S(1)} %select_maximum_fusion.1), channel_id=1, source_target_pairs={{0,16},{16,32},{32,48},{48,64},{64,80},{80,96},{96,112},{112,128},... | collective-permute-start | bytes 119816 | tf_op jit(solution)/shard_map/ppermute | solution.py:23
  72.9 5.7 %collective-permute-start.1 = (f32[96,96]{1,0:T(8,128)S(1)}, f32[96,96]{1,0:T(8,128)S(1)}, u32[]{:S(2)}, u32[]{:S(2)}) collective-permute-start(f32[96,96]{1,0:T(8,128)S(1)} %bitcast.85), channel_id=1, source_target_pairs={{16,0},{32,16},{48,32},{64,48},{80,64},{96,80},{112,96},{128,112},... | collective-permute-start | bytes 110600 | tf_op jit(solution)/shard_map/ppermute | solution.py:23
  78.7 2.8 %fusion.1 = f32[192,8192]{1,0:T(8,128)S(1)} fusion(s32[8192]{0:T(1024)S(1)} %get-tuple-element.47, bf16[384,96]{1,0:T(8,128)(2,1)S(1)} %get-tuple-element.29, bf16[384,96]{1,0:T(8,128)(2,1)S(1)} %get-tuple-element.28), kind=kOutput, calls=%fused_computation.3 | convolution fusion | flops 1211400192 | bytes 6471680 | tf_op jit(solution)/shard_map/dot_general | solution.py:210
  81.5 0.2 select_reduce_fusion.9
  81.8 1.5 %fusion.6 = f32[192,8192]{1,0:T(8,128)S(1)} fusion(s32[8192]{0:T(1024)S(1)} %get-tuple-element.18, bf16[192,96]{1,0:T(8,128)(2,1)S(1)} %get-tuple-element.41, bf16[192,96]{1,0:T(8,128)(2,1)S(1)} %get-tuple-element.40), kind=kOutput, calls=%fused_computation.8 | convolution fusion | flops 605700096 | bytes 6397952 | tf_op jit(solution)/shard_map/dot_general | solution.py:210
  83.3 1.4 %fusion.9 = (f32[8192]{0:T(1024)S(1)}, f32[8192]{0:T(1024)S(1)}) fusion(f32[192,8192]{1,0:T(8,128)S(1)} %fusion.6, s32[8192]{0:T(1024)S(1)} %get-tuple-element.49, f32[192,8192]{1,0:T(8,128)S(1)} %fusion.1), kind=kLoop, calls=%fused_computation.13 | loop fusion | flops 5488640 | bytes 12681216 | tf_op jit(solution)/shard_map/reduce_sum | solution.py:212
  84.7 0.3 sine_multiply_fusion
  85.4 0.6 broadcast_in_dim.164
  86.0 3.5 %all-to-all-start.3 = ((f32[16,2,4]{2,1,0:T(2,128)}), f32[16,2,4]{2,1,0:T(2,128)S(1)}, u32[]{:S(2)}, u32[]{:S(2)}) async-start(f32[16,2,4]{2,1,0:T(2,128)} %broadcast_in_dim.164), calls=%async_computation.3 | async-start | bytes 32768 | tf_op jit(solution)/shard_map/all_to_all | solution.py:76
  89.6 7.5 %all-to-all-done.3 = f32[16,2,4]{2,1,0:T(2,128)S(1)} async-done(((f32[16,2,4]{2,1,0:T(2,128)}), f32[16,2,4]{2,1,0:T(2,128)S(1)}, u32[]{:S(2)}, u32[]{:S(2)}) %all-to-all-start.3) | async-done | bytes 544 | tf_op jit(solution)/shard_map/all_to_all | solution.py:76
  97.2 1.9 %collective-permute-start.2 = (f32[2,1]{1,0:T(2,128)S(1)}, f32[2,1]{1,0:T(2,128)S(1)}, u32[]{:S(2)}, u32[]{:S(2)}) collective-permute-start(f32[2,1]{1,0:T(2,128)S(1)} %slice.144), channel_id=1, source_target_pairs={{0,16},{16,32},{32,48},{48,64},{64,80},{80,96},{96,112},{112,128},... | collective-permute-start | bytes 32 | tf_op jit(solution)/shard_map/ppermute | solution.py:23
  99.2 0.2 select_reduce_fusion.5
  99.4 2.2 %add_select_fusion.4 = (f32[1,8192]{1,0:T(1,128)S(1)}, f32[1,8192]{1,0:T(1,128)S(1)}) fusion(pred[1,8192]{1,0:T(4,128)(4,1)S(1)} %bitcast.67, f32[1,8192]{1,0:T(1,128)S(1)} %bitcast.62, f32[1,8192]{1,0:T(1,128)S(1)} %bitcast.80, f32[1,8192]{1,0:T(1,128)S(1)} %bitcast.78, f32[1,8192]{1,0:T(1,128)S(1)} %bitcast.77, f32[1,8192]{1,0:T(1,128)S(1)} %bitcast.72, ...), kind=kLoop, calls=%fused_computation.103 | loop fusion | flops 147456 | bytes 335872 | tf_op jit(solution)/shard_map/jit(_where)/select_n | solution.py:245
  101.6 0.7 pad_maximum_fusion.2
  102.3 2.5 %collective-permute-done.2 = f32[2,1]{1,0:T(2,128)S(1)} collective-permute-done((f32[2,1]{1,0:T(2,128)S(1)}, f32[2,1]{1,0:T(2,128)S(1)}, u32[]{:S(2)}, u32[]{:S(2)}) %collective-permute-start.2) | collective-permute-done | bytes 40 | tf_op jit(solution)/shard_map/ppermute | solution.py:23
  104.8 0.6 pad_maximum_fusion.5
  (58 shorter events, 3.2 us)
Async XLA Ops:
  8.5 21.6 %copy-start.2 = (f32[96]{0:T(128)S(1)}, f32[96]{0:T(128)}, u32[]{:S(2)}) copy-start(f32[96]{0:T(128)} %param.19) | copy-start | bytes 1156
  8.5 22.2 %copy-start.3 = (f32[96]{0:T(128)S(1)}, f32[96]{0:T(128)}, u32[]{:S(2)}) copy-start(f32[96]{0:T(128)} %param.18) | copy-start | bytes 1156
  33.9 36.0 %copy-start = (f32[96,96]{1,0:T(8,128)S(1)}, f32[96,96]{1,0:T(8,128)}, u32[]{:S(2)}) copy-start(f32[96,96]{1,0:T(8,128)} %param.20) | copy-start | bytes 110596
  33.9 36.0 %copy-start.1 = (f32[96,96]{1,0:T(8,128)S(1)}, f32[96,96]{1,0:T(8,128)}, u32[]{:S(2)}) copy-start(f32[96,96]{1,0:T(8,128)} %param.21) | copy-start | bytes 110596
  70.4 11.3 %collective-permute-start = (f32[104,96]{1,0:T(8,128)S(1)}, f32[104,96]{1,0:T(8,128)S(1)}, u32[]{:S(2)}, u32[]{:S(2)}) collective-permute-start(f32[104,96]{1,0:T(8,128)S(1)} %select_maximum_fusion.1), channel_id=1, source_target_pairs={{0,16},{16,32},{32,48},{48,64},{64,80},{80,96},{96,112},{112,128},... | collective-permute-start | bytes 119816 | tf_op jit(solution)/shard_map/ppermute | solution.py:23
  72.9 8.8 %collective-permute-start.1 = (f32[96,96]{1,0:T(8,128)S(1)}, f32[96,96]{1,0:T(8,128)S(1)}, u32[]{:S(2)}, u32[]{:S(2)}) collective-permute-start(f32[96,96]{1,0:T(8,128)S(1)} %bitcast.85), channel_id=1, source_target_pairs={{16,0},{32,16},{48,32},{64,48},{80,64},{96,80},{112,96},{128,112},... | collective-permute-start | bytes 110600 | tf_op jit(solution)/shard_map/ppermute | solution.py:23
  86.0 11.1 %all-to-all-start.3 = ((f32[16,2,4]{2,1,0:T(2,128)}), f32[16,2,4]{2,1,0:T(2,128)S(1)}, u32[]{:S(2)}, u32[]{:S(2)}) async-start(f32[16,2,4]{2,1,0:T(2,128)} %broadcast_in_dim.164), calls=%async_computation.3 | async-start | bytes 32768 | tf_op jit(solution)/shard_map/all_to_all | solution.py:76
  97.2 7.6 %collective-permute-start.2 = (f32[2,1]{1,0:T(2,128)S(1)}, f32[2,1]{1,0:T(2,128)S(1)}, u32[]{:S(2)}, u32[]{:S(2)}) collective-permute-start(f32[2,1]{1,0:T(2,128)S(1)} %slice.144), channel_id=1, source_target_pairs={{0,16},{16,32},{32,48},{48,64},{64,80},{80,96},{96,112},{112,128},... | collective-permute-start | bytes 32 | tf_op jit(solution)/shard_map/ppermute | solution.py:23

commit v6 on v5

--- a/solution.py
+++ b/solution.py
@@ -120,30 +120,32 @@
     to_group = destination == jnp.arange(groups, dtype=jnp.int32)[:, None]
     arrival = arrival_slots(to_group)
 
-    values = jnp.stack(
+    index_value = (target_slice * cell_count + cell_index).astype(jnp.float32)
+    index_hi = lax.reduce_precision(index_value, exponent_bits=8, mantissa_bits=7)
+    pieces = jnp.stack(
+        split3(phases)
+        + split3(energy)
+        + [weights, index_hi.astype(jnp.bfloat16), (index_value - index_hi).astype(jnp.bfloat16)]
+    )
+    piece_count = pieces.shape[0]
+    left = jnp.where(to_group[None], pieces[:, None, :], jnp.zeros((), jnp.bfloat16)).reshape(
+        piece_count * groups, per_device
+    )
+    to_slot = (jnp.arange(capacity, dtype=jnp.int32)[:, None] == arrival[None, :]).astype(
+        jnp.bfloat16
+    )
+    placed = lax.dot_general(
+        left, to_slot, (((1,), (1,)), ((), ())), preferred_element_type=jnp.float32
+    ).reshape(piece_count, groups, capacity)
+    send = jnp.stack(
         [
-            phases,
-            energy,
-            weights.astype(jnp.float32),
-            (target_slice * cell_count + cell_index).astype(jnp.float32),
+            (placed[0] + placed[1]) + placed[2],
+            (placed[3] + placed[4]) + placed[5],
+            placed[6],
+            placed[7] + placed[8],
         ]
     )
-    value_count = values.shape[0]
-    parts = split3(values)
-    left = jnp.concatenate(
-        [
-            jnp.where(to_group[None], part[:, None, :], jnp.zeros((), jnp.bfloat16)).reshape(
-                value_count * groups, per_device
-            )
-            for part in parts
-        ]
-    )
-    to_slot = (arrival[:, None] == jnp.arange(capacity, dtype=jnp.int32)[None, :]).astype(
-        jnp.bfloat16
-    )
-    placed = jnp.dot(left, to_slot, preferred_element_type=jnp.float32)
-    rows = value_count * groups
-    send = (placed[:rows] + placed[rows : 2 * rows]) + placed[2 * rows :]
+    value_count = send.shape[0]
     got = lax.all_to_all(
         send.reshape(value_count, groups, capacity), "ta", split_axis=1, concat_axis=1, tiled=True
     ).reshape(value_count, slot_count)

time: 106 us -> 108 us (1.019)
    convert_element_type x1 -> x3, other arithmetic: 0.1 us -> 2.15 us  [split3(): return [part.astype(jnp.bfloat16) for part in (hi, mid, lo)]]
    add x2 -> x1, other arithmetic: 1.32 us -> 0.02 us  [body(): placed[0] + placed[1] + placed[2]]
where the time goes in v6:
time: 108 us; the launch traced here: 107 us
  blocking collectives  55.3 us (51%)
  other arithmetic  16.2 us (15%)
  starting transfers between devices  13.5 us (12%)
  waiting for transfers between devices  9.96 us (9%)
  matrix products  7.72 us (7%)
  local copies, waits for them, and re-layouts  3.07 us (3%)
    all_to_all x1, blocking collectives, pb_sum(): mine = jnp.sum(lax.all_to_all(chunks, axis, 0, 0, tiled=True), axis=0)  21.4 us
    all_to_all x1, blocking collectives, body(): lax.all_to_all(send.reshape(value_count, groups, capacity), 'ta', split_a...  19.6 us
    all_to_all x1, blocking collectives, pb_sum(): lax.all_to_all(jnp.broadcast_to(mine[None], chunks.shape), axis, 0, 0, ti...  14.4 us
    ppermute x3, starting transfers between devices, shifted(): lax.ppermute(value, axis, [(source, source + steps) for source in range(l...  10 us
    all_to_all x1, waiting for transfers between devices, pb_sum_small(): return jnp.sum(lax.all_to_all(spread, axis, 0, 0, tiled=True), axis=0)  7.47 us
    dot_general x2, matrix products, pick(): picked = jnp.dot(table_parts, pick_row, preferred_element_type=jnp.float32)  4.34 us
    all_to_all x1, starting transfers between devices, pb_sum_small(): return jnp.sum(lax.all_to_all(spread, axis, 0, 0, tiled=True), axis=0)  3.49 us
    ppermute x3, waiting for transfers between devices, shifted(): lax.ppermute(value, axis, [(source, source + steps) for source in range(l...  2.49 us
  transfers between devices with their start and end apart: 4, of which 2 were waited for; matrix products, arithmetic and copies ran while one was open for 6% of the time, Pallas kernels for 0%

profile of v6, /device:TPU:8, one launch (start us, length us, event | category | flops | bytes accessed | tf_op | source)
XLA Modules:
  0.0 106.9 jit_solution(11870395596172279425)
XLA Ops:
  0.6 0.7 add_select_fusion.5
  1.4 1.2 %select_reduce_fusion.2 = (f32[4096]{0:T(1024)S(1)}, f32[4096]{0:T(1024)S(1)}) fusion(f32[96]{0:T(128)} %param.17, s32[4096]{0:T(1024)S(1)} %get-tuple-element.58, f32[96]{0:T(128)} %param.16, s32[4096]{0:T(1024)S(1)} %get-tuple-element.59), kind=kLoop, calls=%fused_computation.28 | loop fusion | flops 2351104 | bytes 66304 | tf_op jit(solution)/shard_map/reduce_sum | solution.py:28
  2.6 1.3 %fusion.45 = (bf16[1,4096]{1,0:T(2,128)(2,1)S(1)}, f32[1,4096]{1,0:T(1,128)S(1)}) fusion(f32[1,4096]{1,0:T(1,128)S(1)} %bitcast.82, f32[2,4096]{1,0:T(2,128)} %param.11), kind=kLoop, calls=%fused_computation.127 | loop fusion | flops 28672 | bytes 73728 | tf_op jit(solution)/shard_map/convert_element_type | solution.py:36
  3.9 0.8 reduce-precision_convert_fusion.3
  4.8 0.7 fusion.46
  5.6 0.7 stack.47
  6.3 0.8 iota_compare_fusion.16
  7.1 0.5 broadcast.435
  7.6 1.4 %reduce.11 = s32[4096]{0:T(1024)S(1)} reduce(s32[4096,1]{0,1:T(1,128)} %param.14, s32[]{:T(128)} %broadcast.435), dimensions={1}, to_apply=%param.14.reduce_sub_computation.3 | reduce | bytes 32772 | tf_op args[3]
  9.3 0.4 fusion.18
  9.9 0.3 broadcast_select_fusion
  10.3 0.9 fusion.7
  11.3 19.6 %all_to_all.20 = f32[4,32,256]{2,0,1:T(4,128)S(1)} all-to-all(f32[4,32,256]{2,0,1:T(4,128)S(1)} %copy.30), channel_id=1, replica_groups=mesh['ta'=32,'pb'=16] {'ta'}, dimensions={1} | all-to-all | bytes 262144 | tf_op jit(solution)/shard_map/all_to_all | solution.py:149
  31.5 0.6 select_reduce_fusion
  32.1 0.6 select_reduce_fusion.1
  33.3 2.1 %fusion.2 = f32[384,96]{0,1:T(8,128)S(1)} fusion(s32[8192]{0:T(1024)S(1)} %get-tuple-element.47, bf16[8192]{0:T(1024)(128)(2,1)S(1)} %convert_element_type.119, s32[8192]{0:T(1024)S(1)} %get-tuple-element.49), kind=kOutput, calls=%fused_computation.4 | convolution fusion | flops 611057664 | bytes 229376 | tf_op jit(solution)/shard_map/dot_general | solution.py:60
  35.6 21.4 %all_to_all.21 = f32[16,32,96]{2,1,0:T(8,128)S(1)} all-to-all(f32[16,32,96]{2,1,0:T(8,128)S(1)} %bitcast.60), channel_id=1, replica_groups=mesh['ta'=32,'pb'=16] {'pb'}, dimensions={0} | all-to-all | bytes 393216 | tf_op jit(solution)/shard_map/all_to_all | solution.py:68
  57.0 14.4 %all_to_all.22 = f32[16,32,96]{2,1,0:T(8,128)S(1)} all-to-all(f32[16,32,96]{2,1,0:T(8,128)S(1)} %broadcast_in_dim.90), channel_id=1, replica_groups=mesh['ta'=32,'pb'=16] {'pb'}, dimensions={0} | all-to-all | bytes 393216 | tf_op jit(solution)/shard_map/all_to_all | solution.py:69
  71.9 2.5 %collective-permute-start = (f32[104,96]{1,0:T(8,128)S(1)}, f32[104,96]{1,0:T(8,128)S(1)}, u32[]{:S(2)}, u32[]{:S(2)}) collective-permute-start(f32[104,96]{1,0:T(8,128)S(1)} %select_maximum_fusion.1), channel_id=1, source_target_pairs={{0,16},{16,32},{32,48},{48,64},{64,80},{80,96},{96,112},{112,128},... | collective-permute-start | bytes 119816 | tf_op jit(solution)/shard_map/ppermute | solution.py:23
  74.4 5.7 %collective-permute-start.1 = (f32[96,96]{1,0:T(8,128)S(1)}, f32[96,96]{1,0:T(8,128)S(1)}, u32[]{:S(2)}, u32[]{:S(2)}) collective-permute-start(f32[96,96]{1,0:T(8,128)S(1)} %bitcast.84), channel_id=1, source_target_pairs={{16,0},{32,16},{48,32},{64,48},{80,64},{96,80},{112,96},{128,112},... | collective-permute-start | bytes 110600 | tf_op jit(solution)/shard_map/ppermute | solution.py:23
  80.1 2.8 %fusion.1 = f32[192,8192]{1,0:T(8,128)S(1)} fusion(s32[8192]{0:T(1024)S(1)} %get-tuple-element.47, bf16[384,96]{1,0:T(8,128)(2,1)S(1)} %get-tuple-element.35, bf16[384,96]{1,0:T(8,128)(2,1)S(1)} %get-tuple-element.34), kind=kOutput, calls=%fused_computation.3 | convolution fusion | flops 1211400192 | bytes 6471680 | tf_op jit(solution)/shard_map/dot_general | solution.py:212
  83.3 1.5 %fusion.6 = f32[192,8192]{1,0:T(8,128)S(1)} fusion(s32[8192]{0:T(1024)S(1)} %get-tuple-element.18, bf16[192,96]{1,0:T(8,128)(2,1)S(1)} %get-tuple-element.44, bf16[192,96]{1,0:T(8,128)(2,1)S(1)} %get-tuple-element.43), kind=kOutput, calls=%fused_computation.8 | convolution fusion | flops 605700096 | bytes 6397952 | tf_op jit(solution)/shard_map/dot_general | solution.py:212
  84.8 1.4 %fusion.9 = (f32[8192]{0:T(1024)S(1)}, f32[8192]{0:T(1024)S(1)}) fusion(f32[192,8192]{1,0:T(8,128)S(1)} %fusion.6, s32[8192]{0:T(1024)S(1)} %get-tuple-element.49, f32[192,8192]{1,0:T(8,128)S(1)} %fusion.1), kind=kLoop, calls=%fused_computation.13 | loop fusion | flops 5488640 | bytes 12681216 | tf_op jit(solution)/shard_map/reduce_sum | solution.py:214
  86.2 0.3 sine_multiply_fusion
  86.8 0.6 broadcast_in_dim.140
  87.4 3.5 %all-to-all-start.3 = ((f32[16,2,4]{2,1,0:T(2,128)}), f32[16,2,4]{2,1,0:T(2,128)S(1)}, u32[]{:S(2)}, u32[]{:S(2)}) async-start(f32[16,2,4]{2,1,0:T(2,128)} %broadcast_in_dim.140), calls=%async_computation.3 | async-start | bytes 32768 | tf_op jit(solution)/shard_map/all_to_all | solution.py:76
  91.0 7.5 %all-to-all-done.3 = f32[16,2,4]{2,1,0:T(2,128)S(1)} async-done(((f32[16,2,4]{2,1,0:T(2,128)}), f32[16,2,4]{2,1,0:T(2,128)S(1)}, u32[]{:S(2)}, u32[]{:S(2)}) %all-to-all-start.3) | async-done | bytes 544 | tf_op jit(solution)/shard_map/all_to_all | solution.py:76
  98.7 1.9 %collective-permute-start.2 = (f32[2,1]{1,0:T(2,128)S(1)}, f32[2,1]{1,0:T(2,128)S(1)}, u32[]{:S(2)}, u32[]{:S(2)}) collective-permute-start(f32[2,1]{1,0:T(2,128)S(1)} %slice.180), channel_id=1, source_target_pairs={{0,16},{16,32},{32,48},{48,64},{64,80},{80,96},{96,112},{112,128},... | collective-permute-start | bytes 32 | tf_op jit(solution)/shard_map/ppermute | solution.py:23
  100.9 2.2 %add_select_fusion.4 = (f32[1,8192]{1,0:T(1,128)S(1)}, f32[1,8192]{1,0:T(1,128)S(1)}) fusion(pred[1,8192]{1,0:T(4,128)(4,1)S(1)} %bitcast.68, f32[1,8192]{1,0:T(1,128)S(1)} %bitcast.64, f32[1,8192]{1,0:T(1,128)S(1)} %bitcast.81, f32[1,8192]{1,0:T(1,128)S(1)} %bitcast.79, f32[1,8192]{1,0:T(1,128)S(1)} %bitcast.78, f32[1,8192]{1,0:T(1,128)S(1)} %bitcast.73, ...), kind=kLoop, calls=%fused_computation.98 | loop fusion | flops 147456 | bytes 335872 | tf_op jit(solution)/shard_map/jit(_where)/select_n | solution.py:247
  103.1 0.7 pad_maximum_fusion.2
  103.8 2.5 %collective-permute-done.2 = f32[2,1]{1,0:T(2,128)S(1)} collective-permute-done((f32[2,1]{1,0:T(2,128)S(1)}, f32[2,1]{1,0:T(2,128)S(1)}, u32[]{:S(2)}, u32[]{:S(2)}) %collective-permute-start.2) | collective-permute-done | bytes 40 | tf_op jit(solution)/shard_map/ppermute | solution.py:23
  106.3 0.6 pad_maximum_fusion.5
  (64 shorter events, 3.8 us)
Async XLA Ops:
  10.2 21.3 %copy-start.2 = (f32[96]{0:T(128)S(1)}, f32[96]{0:T(128)}, u32[]{:S(2)}) copy-start(f32[96]{0:T(128)} %param.19) | copy-start | bytes 1156
  10.2 21.9 %copy-start.3 = (f32[96]{0:T(128)S(1)}, f32[96]{0:T(128)}, u32[]{:S(2)}) copy-start(f32[96]{0:T(128)} %param.18) | copy-start | bytes 1156
  35.4 36.0 %copy-start = (f32[96,96]{1,0:T(8,128)S(1)}, f32[96,96]{1,0:T(8,128)}, u32[]{:S(2)}) copy-start(f32[96,96]{1,0:T(8,128)} %param.20) | copy-start | bytes 110596
  35.4 36.0 %copy-start.1 = (f32[96,96]{1,0:T(8,128)S(1)}, f32[96,96]{1,0:T(8,128)}, u32[]{:S(2)}) copy-start(f32[96,96]{1,0:T(8,128)} %param.21) | copy-start | bytes 110596
  71.9 11.3 %collective-permute-start = (f32[104,96]{1,0:T(8,128)S(1)}, f32[104,96]{1,0:T(8,128)S(1)}, u32[]{:S(2)}, u32[]{:S(2)}) collective-permute-start(f32[104,96]{1,0:T(8,128)S(1)} %select_maximum_fusion.1), channel_id=1, source_target_pairs={{0,16},{16,32},{32,48},{48,64},{64,80},{80,96},{96,112},{112,128},... | collective-permute-start | bytes 119816 | tf_op jit(solution)/shard_map/ppermute | solution.py:23
  74.4 8.8 %collective-permute-start.1 = (f32[96,96]{1,0:T(8,128)S(1)}, f32[96,96]{1,0:T(8,128)S(1)}, u32[]{:S(2)}, u32[]{:S(2)}) collective-permute-start(f32[96,96]{1,0:T(8,128)S(1)} %bitcast.84), channel_id=1, source_target_pairs={{16,0},{32,16},{48,32},{64,48},{80,64},{96,80},{112,96},{128,112},... | collective-permute-start | bytes 110600 | tf_op jit(solution)/shard_map/ppermute | solution.py:23
  87.4 11.1 %all-to-all-start.3 = ((f32[16,2,4]{2,1,0:T(2,128)}), f32[16,2,4]{2,1,0:T(2,128)S(1)}, u32[]{:S(2)}, u32[]{:S(2)}) async-start(f32[16,2,4]{2,1,0:T(2,128)} %broadcast_in_dim.140), calls=%async_computation.3 | async-start | bytes 32768 | tf_op jit(solution)/shard_map/all_to_all | solution.py:76
  98.7 7.6 %collective-permute-start.2 = (f32[2,1]{1,0:T(2,128)S(1)}, f32[2,1]{1,0:T(2,128)S(1)}, u32[]{:S(2)}, u32[]{:S(2)}) collective-permute-start(f32[2,1]{1,0:T(2,128)S(1)} %slice.180), channel_id=1, source_target_pairs={{0,16},{16,32},{32,48},{48,64},{64,80},{80,96},{96,112},{112,128},... | collective-permute-start | bytes 32 | tf_op jit(solution)/shard_map/ppermute | solution.py:23

commit v7 on v5

--- a/solution.py
+++ b/solution.py
@@ -183,13 +183,17 @@
         return cosine, sine_part, sums
 
     cosine0, sine0, sums0 = local_bunching(got_phase)
-    sums_row = jnp.pad(sums0.reshape(1, 2 * SL_DEV), ((0, 7), (0, grid_y - 2 * SL_DEV)))
-    stacked = jnp.concatenate([partial, sums_row])
-    chunk_rows = -(-stacked.shape[0] // (splits * 8)) * 8
-    stacked = jnp.pad(stacked, ((0, chunk_rows * splits - stacked.shape[0]), (0, 0)))
+    lanes = -(-(grid_y + 2 * SL_DEV) // 128) * 128
+    chunk_rows = -(-density_rows // (splits * 8)) * 8
+    side = jnp.pad(
+        sums0.reshape(1, 2 * SL_DEV),
+        ((0, chunk_rows * splits - 1), (0, lanes - grid_y - 2 * SL_DEV)),
+    )
+    stacked = jnp.pad(partial, ((0, chunk_rows * splits - density_rows), (0, 0)))
+    stacked = jnp.concatenate([stacked, side], axis=1)
     summed = pb_sum(stacked, "pb")
-    density = summed[:density_rows].reshape(SL_DEV, grid_x, grid_y)
-    bunching0 = summed[density_rows, : 2 * SL_DEV].reshape(2, SL_DEV)
+    density = summed[:density_rows, :grid_y].reshape(SL_DEV, grid_x, grid_y)
+    bunching0 = summed[0, grid_y : grid_y + 2 * SL_DEV].reshape(2, SL_DEV)
 
     couple = 1.0 / math.sqrt(splits * PS_DEV)
     radiation0 = couple * bunching0

time: 106 us -> 103 us (0.972)
  blocking collectives: 55.3 us -> 52.7 us
    all_to_all x1, blocking collectives: 14.4 us -> 13 us  [pb_sum(): lax.all_to_all(jnp.broadcast_to(mine[None], chunks.shape), axis, 0, 0, ti...]
    all_to_all x1, blocking collectives: 21.4 us -> 20.1 us  [pb_sum(): mine = jnp.sum(lax.all_to_all(chunks, axis, 0, 0, tiled=True), axis=0)]
where the time goes in v7:
time: 103 us
  blocking collectives  52.7 us (51%)
  other arithmetic  15.5 us (15%)
  starting transfers between devices  13.5 us (13%)
  waiting for transfers between devices  9.94 us (10%)
  matrix products  8.03 us (8%)
  local copies, waits for them, and re-layouts  2.07 us (2%)
    all_to_all x1, blocking collectives, pb_sum(): mine = jnp.sum(lax.all_to_all(chunks, axis, 0, 0, tiled=True), axis=0)  20.1 us
    all_to_all x1, blocking collectives, body(): lax.all_to_all(send.reshape(value_count, groups, capacity), 'ta', split_a...  19.6 us
    all_to_all x1, blocking collectives, pb_sum(): lax.all_to_all(jnp.broadcast_to(mine[None], chunks.shape), axis, 0, 0, ti...  13 us
    ppermute x3, starting transfers between devices, shifted(): lax.ppermute(value, axis, [(source, source + steps) for source in range(l...  10 us
    all_to_all x1, waiting for transfers between devices, pb_sum_small(): return jnp.sum(lax.all_to_all(spread, axis, 0, 0, tiled=True), axis=0)  7.44 us
    dot_general x2, matrix products, pick(): picked = jnp.dot(table_parts, pick_row, preferred_element_type=jnp.float32)  4.35 us
    all_to_all x1, starting transfers between devices, pb_sum_small(): return jnp.sum(lax.all_to_all(spread, axis, 0, 0, tiled=True), axis=0)  3.49 us
    ppermute x3, waiting for transfers between devices, shifted(): lax.ppermute(value, axis, [(source, source + steps) for source in range(l...  2.49 us
  transfers between devices with their start and end apart: 4, of which 2 were waited for; matrix products, arithmetic and copies ran while one was open for 6% of the time, Pallas kernels for 0%

profile of v7, /device:TPU:8, one launch (start us, length us, event | category | flops | bytes accessed | tf_op | source)
XLA Modules:
  0.0 102.7 jit_solution(4695270807809175871)
XLA Ops:
  0.6 0.7 stack.47
  1.3 0.8 iota_compare_fusion.16
  2.1 0.5 broadcast.438
  2.6 1.4 %reduce.11 = s32[4096]{0:T(1024)S(1)} reduce(s32[4096,1]{0,1:T(1,128)} %param.14, s32[]{:T(128)} %broadcast.438), dimensions={1}, to_apply=%param.14.reduce_sub_computation.3 | reduce | bytes 32772 | tf_op args[3]
  4.4 0.4 fusion.23
  4.7 0.8 add_select_fusion.5
  5.5 1.2 %select_reduce_fusion.2 = (f32[4096]{0:T(1024)S(1)}, f32[4096]{0:T(1024)S(1)}) fusion(f32[96]{0:T(128)} %param.17, s32[4096]{0:T(1024)S(1)} %get-tuple-element.50, f32[96]{0:T(128)} %param.16, s32[4096]{0:T(1024)S(1)} %get-tuple-element.52), kind=kLoop, calls=%fused_computation.32 | loop fusion | flops 2351104 | bytes 66304 | tf_op jit(solution)/shard_map/reduce_sum | solution.py:28
  6.7 1.3 %multiply_add_fusion.4 = (f32[1,4096]{1,0:T(1,128)S(1)}, f32[1,4096]{1,0:T(1,128)S(1)}) fusion(f32[2,4096]{1,0:T(2,128)} %param.11, f32[1,4096]{1,0:T(1,128)S(1)} %bitcast.81), kind=kLoop, calls=%fused_computation.128 | loop fusion | flops 16384 | bytes 81920 | tf_op jit(solution)/shard_map/add | solution.py:118
  8.1 0.3 broadcast_select_fusion.2
  8.5 1.2 %fusion.7 = f32[384,256]{1,0:T(8,128)S(1)} fusion(bf16[128,4096]{1,0:T(8,128)(2,1)S(1)} %bitcast.58, bf16[128,4096]{1,0:T(8,128)(2,1)S(1)} %bitcast.57, bf16[128,4096]{1,0:T(8,128)(2,1)S(1)} %bitcast.56, s32[4096]{0:T(1024)S(1)} %bitcast.84), kind=kOutput, calls=%fused_computation.10 | convolution fusion | flops 815792128 | bytes 3555328 | tf_op jit(solution)/shard_map/dot_general | solution.py:144
  9.8 19.6 %all_to_all.20 = f32[4,32,256]{2,0,1:T(4,128)S(1)} all-to-all(f32[4,32,256]{2,0,1:T(4,128)S(1)} %copy.30), channel_id=1, replica_groups=mesh['ta'=32,'pb'=16] {'ta'}, dimensions={1} | all-to-all | bytes 262144 | tf_op jit(solution)/shard_map/all_to_all | solution.py:147
  30.1 0.6 select_reduce_fusion
  30.6 0.6 select_reduce_fusion.1
  31.8 2.1 %fusion.2 = f32[384,96]{0,1:T(8,128)S(1)} fusion(s32[8192]{0:T(1024)S(1)} %get-tuple-element.47, bf16[8192]{0:T(1024)(128)(2,1)S(1)} %convert_element_type.104, s32[8192]{0:T(1024)S(1)} %get-tuple-element.49), kind=kOutput, calls=%fused_computation.4 | convolution fusion | flops 611057664 | bytes 229376 | tf_op jit(solution)/shard_map/dot_general | solution.py:60
  34.0 20.1 %all_to_all.21 = f32[16,24,128]{2,1,0:T(8,128)S(1)} all-to-all(f32[16,24,128]{2,1,0:T(8,128)S(1)} %bitcast.63), channel_id=1, replica_groups=mesh['ta'=32,'pb'=16] {'pb'}, dimensions={0} | all-to-all | bytes 393216 | tf_op jit(solution)/shard_map/all_to_all | solution.py:68
  54.2 13.0 %all_to_all.22 = f32[16,24,128]{2,1,0:T(8,128)S(1)} all-to-all(f32[16,24,128]{2,1,0:T(8,128)S(1)} %broadcast_in_dim.163), channel_id=1, replica_groups=mesh['ta'=32,'pb'=16] {'pb'}, dimensions={0} | all-to-all | bytes 393216 | tf_op jit(solution)/shard_map/all_to_all | solution.py:69
  67.7 2.5 %collective-permute-start = (f32[104,96]{1,0:T(8,128)S(1)}, f32[104,96]{1,0:T(8,128)S(1)}, u32[]{:S(2)}, u32[]{:S(2)}) collective-permute-start(f32[104,96]{1,0:T(8,128)S(1)} %select_maximum_fusion.1), channel_id=1, source_target_pairs={{0,16},{16,32},{32,48},{48,64},{64,80},{80,96},{96,112},{112,128},... | collective-permute-start | bytes 119816 | tf_op jit(solution)/shard_map/ppermute | solution.py:23
  70.2 5.7 %collective-permute-start.1 = (f32[96,96]{1,0:T(8,128)S(1)}, f32[96,96]{1,0:T(8,128)S(1)}, u32[]{:S(2)}, u32[]{:S(2)}) collective-permute-start(f32[96,96]{1,0:T(8,128)S(1)} %get-tuple-element.27), channel_id=1, source_target_pairs={{16,0},{32,16},{48,32},{64,48},{80,64},{96,80},{112,96},{128,112},... | collective-permute-start | bytes 110600 | tf_op jit(solution)/shard_map/ppermute | solution.py:23
  76.0 2.8 %fusion.1 = f32[192,8192]{1,0:T(8,128)S(1)} fusion(s32[8192]{0:T(1024)S(1)} %get-tuple-element.47, bf16[384,96]{1,0:T(8,128)(2,1)S(1)} %get-tuple-element.25, bf16[384,96]{1,0:T(8,128)(2,1)S(1)} %get-tuple-element.24), kind=kOutput, calls=%fused_computation.3 | convolution fusion | flops 1211400192 | bytes 6471680 | tf_op jit(solution)/shard_map/dot_general | solution.py:214
  78.8 0.2 select_reduce_fusion.9
  79.1 1.5 %fusion.6 = f32[192,8192]{1,0:T(8,128)S(1)} fusion(s32[8192]{0:T(1024)S(1)} %get-tuple-element.18, bf16[192,96]{1,0:T(8,128)(2,1)S(1)} %get-tuple-element.41, bf16[192,96]{1,0:T(8,128)(2,1)S(1)} %get-tuple-element.40), kind=kOutput, calls=%fused_computation.8 | convolution fusion | flops 605700096 | bytes 6397952 | tf_op jit(solution)/shard_map/dot_general | solution.py:214
  80.6 1.4 %fusion.9 = (f32[8192]{0:T(1024)S(1)}, f32[8192]{0:T(1024)S(1)}) fusion(f32[192,8192]{1,0:T(8,128)S(1)} %fusion.6, s32[8192]{0:T(1024)S(1)} %get-tuple-element.49, f32[192,8192]{1,0:T(8,128)S(1)} %fusion.1), kind=kLoop, calls=%fused_computation.13 | loop fusion | flops 5488640 | bytes 12681216 | tf_op jit(solution)/shard_map/reduce_sum | solution.py:216
  82.0 0.3 sine_multiply_fusion
  82.7 0.6 broadcast_in_dim.164
  83.3 3.5 %all-to-all-start.3 = ((f32[16,2,4]{2,1,0:T(2,128)}), f32[16,2,4]{2,1,0:T(2,128)S(1)}, u32[]{:S(2)}, u32[]{:S(2)}) async-start(f32[16,2,4]{2,1,0:T(2,128)} %broadcast_in_dim.164), calls=%async_computation.3 | async-start | bytes 32768 | tf_op jit(solution)/shard_map/all_to_all | solution.py:76
  86.9 7.4 %all-to-all-done.3 = f32[16,2,4]{2,1,0:T(2,128)S(1)} async-done(((f32[16,2,4]{2,1,0:T(2,128)}), f32[16,2,4]{2,1,0:T(2,128)S(1)}, u32[]{:S(2)}, u32[]{:S(2)}) %all-to-all-start.3) | async-done | bytes 544 | tf_op jit(solution)/shard_map/all_to_all | solution.py:76
  94.5 1.9 %collective-permute-start.2 = (f32[2,1]{1,0:T(2,128)S(1)}, f32[2,1]{1,0:T(2,128)S(1)}, u32[]{:S(2)}, u32[]{:S(2)}) collective-permute-start(f32[2,1]{1,0:T(2,128)S(1)} %slice.143), channel_id=1, source_target_pairs={{0,16},{16,32},{32,48},{48,64},{64,80},{80,96},{96,112},{112,128},... | collective-permute-start | bytes 32 | tf_op jit(solution)/shard_map/ppermute | solution.py:23
  96.4 0.2 select_reduce_fusion.5
  96.7 2.2 %add_select_fusion.4 = (f32[1,8192]{1,0:T(1,128)S(1)}, f32[1,8192]{1,0:T(1,128)S(1)}) fusion(pred[1,8192]{1,0:T(4,128)(4,1)S(1)} %bitcast.67, f32[1,8192]{1,0:T(1,128)S(1)} %bitcast.62, f32[1,8192]{1,0:T(1,128)S(1)} %bitcast.79, f32[1,8192]{1,0:T(1,128)S(1)} %bitcast.77, f32[1,8192]{1,0:T(1,128)S(1)} %bitcast.76, f32[1,8192]{1,0:T(1,128)S(1)} %bitcast.72, ...), kind=kLoop, calls=%fused_computation.103 | loop fusion | flops 147456 | bytes 335872 | tf_op jit(solution)/shard_map/jit(_where)/select_n | solution.py:249
  98.9 0.7 pad_maximum_fusion.2
  99.6 2.5 %collective-permute-done.2 = f32[2,1]{1,0:T(2,128)S(1)} collective-permute-done((f32[2,1]{1,0:T(2,128)S(1)}, f32[2,1]{1,0:T(2,128)S(1)}, u32[]{:S(2)}, u32[]{:S(2)}) %collective-permute-start.2) | collective-permute-done | bytes 40 | tf_op jit(solution)/shard_map/ppermute | solution.py:23
  102.1 0.6 pad_maximum_fusion.5
  (56 shorter events, 3.2 us)
Async XLA Ops:
  8.5 21.6 %copy-start.2 = (f32[96]{0:T(128)S(1)}, f32[96]{0:T(128)}, u32[]{:S(2)}) copy-start(f32[96]{0:T(128)} %param.19) | copy-start | bytes 1156
  8.5 22.2 %copy-start.3 = (f32[96]{0:T(128)S(1)}, f32[96]{0:T(128)}, u32[]{:S(2)}) copy-start(f32[96]{0:T(128)} %param.18) | copy-start | bytes 1156
  31.8 35.5 %copy-start = (f32[96,96]{1,0:T(8,128)S(1)}, f32[96,96]{1,0:T(8,128)}, u32[]{:S(2)}) copy-start(f32[96,96]{1,0:T(8,128)} %param.20) | copy-start | bytes 110596
  31.8 35.5 %copy-start.1 = (f32[96,96]{1,0:T(8,128)S(1)}, f32[96,96]{1,0:T(8,128)}, u32[]{:S(2)}) copy-start(f32[96,96]{1,0:T(8,128)} %param.21) | copy-start | bytes 110596
  67.7 11.3 %collective-permute-start = (f32[104,96]{1,0:T(8,128)S(1)}, f32[104,96]{1,0:T(8,128)S(1)}, u32[]{:S(2)}, u32[]{:S(2)}) collective-permute-start(f32[104,96]{1,0:T(8,128)S(1)} %select_maximum_fusion.1), channel_id=1, source_target_pairs={{0,16},{16,32},{32,48},{48,64},{64,80},{80,96},{96,112},{112,128},... | collective-permute-start | bytes 119816 | tf_op jit(solution)/shard_map/ppermute | solution.py:23
  70.2 8.8 %collective-permute-start.1 = (f32[96,96]{1,0:T(8,128)S(1)}, f32[96,96]{1,0:T(8,128)S(1)}, u32[]{:S(2)}, u32[]{:S(2)}) collective-permute-start(f32[96,96]{1,0:T(8,128)S(1)} %get-tuple-element.27), channel_id=1, source_target_pairs={{16,0},{32,16},{48,32},{64,48},{80,64},{96,80},{112,96},{128,112},... | collective-permute-start | bytes 110600 | tf_op jit(solution)/shard_map/ppermute | solution.py:23
  83.3 11.1 %all-to-all-start.3 = ((f32[16,2,4]{2,1,0:T(2,128)}), f32[16,2,4]{2,1,0:T(2,128)S(1)}, u32[]{:S(2)}, u32[]{:S(2)}) async-start(f32[16,2,4]{2,1,0:T(2,128)} %broadcast_in_dim.164), calls=%async_computation.3 | async-start | bytes 32768 | tf_op jit(solution)/shard_map/all_to_all | solution.py:76
  94.5 7.6 %collective-permute-start.2 = (f32[2,1]{1,0:T(2,128)S(1)}, f32[2,1]{1,0:T(2,128)S(1)}, u32[]{:S(2)}, u32[]{:S(2)}) collective-permute-start(f32[2,1]{1,0:T(2,128)S(1)} %slice.143), channel_id=1, source_target_pairs={{0,16},{16,32},{32,48},{48,64},{64,80},{80,96},{96,112},{112,128},... | collective-permute-start | bytes 32 | tf_op jit(solution)/shard_map/ppermute | solution.py:23

commit v8 on v7

--- a/solution.py
+++ b/solution.py
@@ -117,7 +117,7 @@
     )
     phases = particles[0] + DISPERSION * energy
     destination = target_group.reshape(1, per_device)
-    to_group = destination == jnp.arange(groups, dtype=jnp.int32)[:, None]
+    to_group = lax.optimization_barrier(destination == jnp.arange(groups, dtype=jnp.int32)[:, None])
     arrival = arrival_slots(to_group)
 
     values = jnp.stack(

time: 103 us -> 101 us (0.981)
  other arithmetic: 15.5 us -> 14.1 us
    unnamed x2 -> x1, other arithmetic: 1.41 us -> 0.01 us
where the time goes in v8:
time: 101 us
  blocking collectives  52.7 us (52%)
  other arithmetic  14.1 us (14%)
  starting transfers between devices  13.5 us (13%)
  waiting for transfers between devices  9.94 us (10%)
  matrix products  8.01 us (8%)
  local copies, waits for them, and re-layouts  1.62 us (2%)
    all_to_all x1, blocking collectives, pb_sum(): mine = jnp.sum(lax.all_to_all(chunks, axis, 0, 0, tiled=True), axis=0)  20.1 us
    all_to_all x1, blocking collectives, body(): lax.all_to_all(send.reshape(value_count, groups, capacity), 'ta', split_a...  19.6 us
    all_to_all x1, blocking collectives, pb_sum(): lax.all_to_all(jnp.broadcast_to(mine[None], chunks.shape), axis, 0, 0, ti...  13 us
    ppermute x3, starting transfers between devices, shifted(): lax.ppermute(value, axis, [(source, source + steps) for source in range(l...  10 us
    all_to_all x1, waiting for transfers between devices, pb_sum_small(): return jnp.sum(lax.all_to_all(spread, axis, 0, 0, tiled=True), axis=0)  7.44 us
    dot_general x2, matrix products, pick(): picked = jnp.dot(table_parts, pick_row, preferred_element_type=jnp.float32)  4.35 us
    all_to_all x1, starting transfers between devices, pb_sum_small(): return jnp.sum(lax.all_to_all(spread, axis, 0, 0, tiled=True), axis=0)  3.49 us
    ppermute x3, waiting for transfers between devices, shifted(): lax.ppermute(value, axis, [(source, source + steps) for source in range(l...  2.49 us
  transfers between devices with their start and end apart: 4, of which 2 were waited for; matrix products, arithmetic and copies ran while one was open for 6% of the time, Pallas kernels for 0%

profile of v8, /device:TPU:8, one launch (start us, length us, event | category | flops | bytes accessed | tf_op | source)
XLA Modules:
  0.0 100.9 jit_solution(4396010089819699827)
XLA Ops:
  0.6 0.7 stack.47
  1.3 0.8 iota_compare_fusion.14
  2.5 0.3 fusion.23
  2.9 0.8 add_select_fusion.5
  3.6 1.2 %select_reduce_fusion.2 = (f32[4096]{0:T(1024)S(1)}, f32[4096]{0:T(1024)S(1)}) fusion(f32[96]{0:T(128)} %param.17, s32[4096]{0:T(1024)S(1)} %get-tuple-element.50, f32[96]{0:T(128)} %param.16, s32[4096]{0:T(1024)S(1)} %get-tuple-element.52), kind=kLoop, calls=%fused_computation.32 | loop fusion | flops 2351104 | bytes 66304 | tf_op jit(solution)/shard_map/reduce_sum | solution.py:28
  4.9 1.3 %multiply_add_fusion.4 = (f32[1,4096]{1,0:T(1,128)S(1)}, f32[1,4096]{1,0:T(1,128)S(1)}) fusion(f32[2,4096]{1,0:T(2,128)} %param.11, f32[1,4096]{1,0:T(1,128)S(1)} %bitcast.86), kind=kLoop, calls=%fused_computation.125 | loop fusion | flops 16384 | bytes 81920 | tf_op jit(solution)/shard_map/add | solution.py:118
  6.3 0.3 broadcast_select_fusion.2
  6.6 1.2 %fusion.7 = f32[384,256]{1,0:T(8,128)S(1)} fusion(bf16[128,4096]{1,0:T(8,128)(2,1)S(1)} %bitcast.61, bf16[128,4096]{1,0:T(8,128)(2,1)S(1)} %bitcast.60, bf16[128,4096]{1,0:T(8,128)(2,1)S(1)} %bitcast.59, s32[4096]{0:T(1024)S(1)} %bitcast.89), kind=kOutput, calls=%fused_computation.10 | convolution fusion | flops 815792128 | bytes 3555328 | tf_op jit(solution)/shard_map/dot_general | solution.py:144
  8.0 19.6 %all_to_all.20 = f32[4,32,256]{2,0,1:T(4,128)S(1)} all-to-all(f32[4,32,256]{2,0,1:T(4,128)S(1)} %copy.30), channel_id=1, replica_groups=mesh['ta'=32,'pb'=16] {'ta'}, dimensions={1} | all-to-all | bytes 262144 | tf_op jit(solution)/shard_map/all_to_all | solution.py:147
  28.2 0.6 select_reduce_fusion
  28.8 0.6 select_reduce_fusion.1
  29.6 0.2 select_reduce_fusion.11
  29.9 2.1 %fusion.2 = f32[384,96]{0,1:T(8,128)S(1)} fusion(s32[8192]{0:T(1024)S(1)} %get-tuple-element.47, bf16[8192]{0:T(1024)(128)(2,1)S(1)} %convert_element_type.104, s32[8192]{0:T(1024)S(1)} %get-tuple-element.49), kind=kOutput, calls=%fused_computation.4 | convolution fusion | flops 611057664 | bytes 229376 | tf_op jit(solution)/shard_map/dot_general | solution.py:60
  32.2 20.1 %all_to_all.21 = f32[16,24,128]{2,1,0:T(8,128)S(1)} all-to-all(f32[16,24,128]{2,1,0:T(8,128)S(1)} %bitcast.66), channel_id=1, replica_groups=mesh['ta'=32,'pb'=16] {'pb'}, dimensions={0} | all-to-all | bytes 393216 | tf_op jit(solution)/shard_map/all_to_all | solution.py:68
  52.3 13.0 %all_to_all.22 = f32[16,24,128]{2,1,0:T(8,128)S(1)} all-to-all(f32[16,24,128]{2,1,0:T(8,128)S(1)} %broadcast_in_dim.163), channel_id=1, replica_groups=mesh['ta'=32,'pb'=16] {'pb'}, dimensions={0} | all-to-all | bytes 393216 | tf_op jit(solution)/shard_map/all_to_all | solution.py:69
  65.9 2.5 %collective-permute-start = (f32[104,96]{1,0:T(8,128)S(1)}, f32[104,96]{1,0:T(8,128)S(1)}, u32[]{:S(2)}, u32[]{:S(2)}) collective-permute-start(f32[104,96]{1,0:T(8,128)S(1)} %select_maximum_fusion.1), channel_id=1, source_target_pairs={{0,16},{16,32},{32,48},{48,64},{64,80},{80,96},{96,112},{112,128},... | collective-permute-start | bytes 119816 | tf_op jit(solution)/shard_map/ppermute | solution.py:23
  68.4 5.7 %collective-permute-start.1 = (f32[96,96]{1,0:T(8,128)S(1)}, f32[96,96]{1,0:T(8,128)S(1)}, u32[]{:S(2)}, u32[]{:S(2)}) collective-permute-start(f32[96,96]{1,0:T(8,128)S(1)} %get-tuple-element.27), channel_id=1, source_target_pairs={{16,0},{32,16},{48,32},{64,48},{80,64},{96,80},{112,96},{128,112},... | collective-permute-start | bytes 110600 | tf_op jit(solution)/shard_map/ppermute | solution.py:23
  74.1 2.8 %fusion.1 = f32[192,8192]{1,0:T(8,128)S(1)} fusion(s32[8192]{0:T(1024)S(1)} %get-tuple-element.47, bf16[384,96]{1,0:T(8,128)(2,1)S(1)} %get-tuple-element.25, bf16[384,96]{1,0:T(8,128)(2,1)S(1)} %get-tuple-element.24), kind=kOutput, calls=%fused_computation.3 | convolution fusion | flops 1211400192 | bytes 6471680 | tf_op jit(solution)/shard_map/dot_general | solution.py:214
  76.9 0.2 select_reduce_fusion.9
  77.3 1.5 %fusion.6 = f32[192,8192]{1,0:T(8,128)S(1)} fusion(s32[8192]{0:T(1024)S(1)} %get-tuple-element.18, bf16[192,96]{1,0:T(8,128)(2,1)S(1)} %get-tuple-element.41, bf16[192,96]{1,0:T(8,128)(2,1)S(1)} %get-tuple-element.40), kind=kOutput, calls=%fused_computation.8 | convolution fusion | flops 605700096 | bytes 6397952 | tf_op jit(solution)/shard_map/dot_general | solution.py:214
  78.8 1.4 %fusion.9 = (f32[8192]{0:T(1024)S(1)}, f32[8192]{0:T(1024)S(1)}) fusion(f32[192,8192]{1,0:T(8,128)S(1)} %fusion.6, s32[8192]{0:T(1024)S(1)} %get-tuple-element.49, f32[192,8192]{1,0:T(8,128)S(1)} %fusion.1), kind=kLoop, calls=%fused_computation.13 | loop fusion | flops 5488640 | bytes 12681216 | tf_op jit(solution)/shard_map/reduce_sum | solution.py:216
  80.2 0.3 sine_multiply_fusion
  80.6 0.2 select_reduce_fusion.7
  80.8 0.6 broadcast_in_dim.164
  81.4 3.5 %all-to-all-start.3 = ((f32[16,2,4]{2,1,0:T(2,128)}), f32[16,2,4]{2,1,0:T(2,128)S(1)}, u32[]{:S(2)}, u32[]{:S(2)}) async-start(f32[16,2,4]{2,1,0:T(2,128)} %broadcast_in_dim.164), calls=%async_computation.3 | async-start | bytes 32768 | tf_op jit(solution)/shard_map/all_to_all | solution.py:76
  85.0 7.4 %all-to-all-done.3 = f32[16,2,4]{2,1,0:T(2,128)S(1)} async-done(((f32[16,2,4]{2,1,0:T(2,128)}), f32[16,2,4]{2,1,0:T(2,128)S(1)}, u32[]{:S(2)}, u32[]{:S(2)}) %all-to-all-start.3) | async-done | bytes 544 | tf_op jit(solution)/shard_map/all_to_all | solution.py:76
  92.6 1.9 %collective-permute-start.2 = (f32[2,1]{1,0:T(2,128)S(1)}, f32[2,1]{1,0:T(2,128)S(1)}, u32[]{:S(2)}, u32[]{:S(2)}) collective-permute-start(f32[2,1]{1,0:T(2,128)S(1)} %slice.143), channel_id=1, source_target_pairs={{0,16},{16,32},{32,48},{48,64},{64,80},{80,96},{96,112},{112,128},... | collective-permute-start | bytes 32 | tf_op jit(solution)/shard_map/ppermute | solution.py:23
  94.6 0.2 select_reduce_fusion.5
  94.8 2.2 %add_select_fusion.4 = (f32[1,8192]{1,0:T(1,128)S(1)}, f32[1,8192]{1,0:T(1,128)S(1)}) fusion(pred[1,8192]{1,0:T(4,128)(4,1)S(1)} %bitcast.72, f32[1,8192]{1,0:T(1,128)S(1)} %bitcast.65, f32[1,8192]{1,0:T(1,128)S(1)} %bitcast.84, f32[1,8192]{1,0:T(1,128)S(1)} %bitcast.82, f32[1,8192]{1,0:T(1,128)S(1)} %bitcast.81, f32[1,8192]{1,0:T(1,128)S(1)} %bitcast.77, ...), kind=kLoop, calls=%fused_computation.100 | loop fusion | flops 147456 | bytes 335872 | tf_op jit(solution)/shard_map/jit(_where)/select_n | solution.py:249
  97.0 0.7 pad_maximum_fusion.2
  97.7 2.5 %collective-permute-done.2 = f32[2,1]{1,0:T(2,128)S(1)} collective-permute-done((f32[2,1]{1,0:T(2,128)S(1)}, f32[2,1]{1,0:T(2,128)S(1)}, u32[]{:S(2)}, u32[]{:S(2)}) %collective-permute-start.2) | collective-permute-done | bytes 40 | tf_op jit(solution)/shard_map/ppermute | solution.py:23
  100.2 0.6 pad_maximum_fusion.5
  (54 shorter events, 2.8 us)
Async XLA Ops:
  6.6 21.6 %copy-start.2 = (f32[96]{0:T(128)S(1)}, f32[96]{0:T(128)}, u32[]{:S(2)}) copy-start(f32[96]{0:T(128)} %param.19) | copy-start | bytes 1156
  6.6 22.2 %copy-start.3 = (f32[96]{0:T(128)S(1)}, f32[96]{0:T(128)}, u32[]{:S(2)}) copy-start(f32[96]{0:T(128)} %param.18) | copy-start | bytes 1156
  29.9 35.5 %copy-start = (f32[96,96]{1,0:T(8,128)S(1)}, f32[96,96]{1,0:T(8,128)}, u32[]{:S(2)}) copy-start(f32[96,96]{1,0:T(8,128)} %param.20) | copy-start | bytes 110596
  29.9 35.5 %copy-start.1 = (f32[96,96]{1,0:T(8,128)S(1)}, f32[96,96]{1,0:T(8,128)}, u32[]{:S(2)}) copy-start(f32[96,96]{1,0:T(8,128)} %param.21) | copy-start | bytes 110596
  65.9 11.3 %collective-permute-start = (f32[104,96]{1,0:T(8,128)S(1)}, f32[104,96]{1,0:T(8,128)S(1)}, u32[]{:S(2)}, u32[]{:S(2)}) collective-permute-start(f32[104,96]{1,0:T(8,128)S(1)} %select_maximum_fusion.1), channel_id=1, source_target_pairs={{0,16},{16,32},{32,48},{48,64},{64,80},{80,96},{96,112},{112,128},... | collective-permute-start | bytes 119816 | tf_op jit(solution)/shard_map/ppermute | solution.py:23
  68.4 8.8 %collective-permute-start.1 = (f32[96,96]{1,0:T(8,128)S(1)}, f32[96,96]{1,0:T(8,128)S(1)}, u32[]{:S(2)}, u32[]{:S(2)}) collective-permute-start(f32[96,96]{1,0:T(8,128)S(1)} %get-tuple-element.27), channel_id=1, source_target_pairs={{16,0},{32,16},{48,32},{64,48},{80,64},{96,80},{112,96},{128,112},... | collective-permute-start | bytes 110600 | tf_op jit(solution)/shard_map/ppermute | solution.py:23
  81.4 11.1 %all-to-all-start.3 = ((f32[16,2,4]{2,1,0:T(2,128)}), f32[16,2,4]{2,1,0:T(2,128)S(1)}, u32[]{:S(2)}, u32[]{:S(2)}) async-start(f32[16,2,4]{2,1,0:T(2,128)} %broadcast_in_dim.164), calls=%async_computation.3 | async-start | bytes 32768 | tf_op jit(solution)/shard_map/all_to_all | solution.py:76
  92.6 7.6 %collective-permute-start.2 = (f32[2,1]{1,0:T(2,128)S(1)}, f32[2,1]{1,0:T(2,128)S(1)}, u32[]{:S(2)}, u32[]{:S(2)}) collective-permute-start(f32[2,1]{1,0:T(2,128)S(1)} %slice.143), channel_id=1, source_target_pairs={{0,16},{16,32},{32,48},{48,64},{64,80},{80,96},{96,112},{112,128},... | collective-permute-start | bytes 32 | tf_op jit(solution)/shard_map/ppermute | solution.py:23

commit v9 on v8

--- a/solution.py
+++ b/solution.py
@@ -24,8 +24,12 @@
 
 
 def lookup(values_table, positions):
-    matches = positions[None, :] == jnp.arange(values_table.shape[0], dtype=jnp.int32)[:, None]
-    return jnp.sum(jnp.where(matches, values_table[:, None], 0.0), axis=0)
+    matches = (
+        positions[None, :] == jnp.arange(values_table.shape[0], dtype=jnp.int32)[:, None]
+    ).astype(jnp.bfloat16)
+    table_parts = jnp.stack(split3(values_table))
+    picked = jnp.dot(table_parts, matches, preferred_element_type=jnp.float32)
+    return (picked[0] + picked[1]) + picked[2]
 
 
 def split3(x):

time: 101 us -> 107 us (1.059)
  blocking collectives: 52.7 us -> 33.1 us
  waiting for transfers between devices: 9.94 us -> 20.6 us
  starting transfers between devices: 13.5 us -> 23.7 us
  other arithmetic: 14.1 us -> 16 us
  matrix products: 8.01 us -> 9.89 us
    all_to_all x1 -> x0, blocking collectives: 19.6 us -> none  [body(): lax.all_to_all(send.reshape(value_count, groups, capacity), 'ta', split_a...]
    all_to_all x0 -> x1, starting transfers between devices: none -> 10.2 us  [body(): lax.all_to_all(send.reshape(value_count, groups, capacity), 'ta', split_a...]
    all_to_all x0 -> x1, waiting for transfers between devices: none -> 9.6 us  [body(): lax.all_to_all(send.reshape(value_count, groups, capacity), 'ta', split_a...]
    mul x2, other arithmetic: 0.4 us -> 2.93 us  [local_bunching(): -weighted * sine_part]
    reduce_sum x3 -> x0, other arithmetic: 2.34 us -> none  [lookup(): return jnp.sum(jnp.where(matches, values_table[:, None], 0.0), axis=0)]
    dot_general x0 -> x4, matrix products: none -> 1.86 us  [lookup(): picked = jnp.dot(table_parts, matches, preferred_element_type=jnp.float32)]
    mul x2, other arithmetic: 0.25 us -> 1.73 us  [local_bunching(): weighted * cosine]
    another operation x0 -> x4, other arithmetic: none -> 1.34 us  [lookup(): table_parts = jnp.stack(split3(values_table))]
  transfers between devices with their start and end apart: 4 -> 5, of which waited for: 2 -> 3; matrix products, arithmetic and copies ran while one was open for 6% -> 5% of each run, Pallas kernels for 0% -> 0%
where the time goes in v9:
time: 107 us
  blocking collectives  33.1 us (31%)
  starting transfers between devices  23.7 us (22%)
  waiting for transfers between devices  20.6 us (19%)
  other arithmetic  16 us (15%)
  matrix products  9.89 us (9%)
  local copies, waits for them, and re-layouts  2.37 us (2%)
    all_to_all x1, blocking collectives, pb_sum(): mine = jnp.sum(lax.all_to_all(chunks, axis, 0, 0, tiled=True), axis=0)  20.1 us
    all_to_all x1, blocking collectives, pb_sum(): lax.all_to_all(jnp.broadcast_to(mine[None], chunks.shape), axis, 0, 0, ti...  13 us
    all_to_all x1, starting transfers between devices, body(): lax.all_to_all(send.reshape(value_count, groups, capacity), 'ta', split_a...  10.2 us
    ppermute x3, starting transfers between devices, shifted(): lax.ppermute(value, axis, [(source, source + steps) for source in range(l...  10 us
    all_to_all x1, waiting for transfers between devices, body(): lax.all_to_all(send.reshape(value_count, groups, capacity), 'ta', split_a...  9.6 us
    all_to_all x1, waiting for transfers between devices, pb_sum_small(): return jnp.sum(lax.all_to_all(spread, axis, 0, 0, tiled=True), axis=0)  7.44 us
    dot_general x2, matrix products, pick(): picked = jnp.dot(table_parts, pick_row, preferred_element_type=jnp.float32)  4.35 us
    ppermute x3, waiting for transfers between devices, shifted(): lax.ppermute(value, axis, [(source, source + steps) for source in range(l...  3.57 us
  transfers between devices with their start and end apart: 5, of which 3 were waited for; matrix products, arithmetic and copies ran while one was open for 5% of the time, Pallas kernels for 0%

profile of v9, /device:TPU:8, one launch (start us, length us, event | category | flops | bytes accessed | tf_op | source)
XLA Modules:
  0.0 106.6 jit_solution(334271753904629650)
XLA Ops:
  0.6 0.7 fusion.78
  1.3 0.7 fusion.82
  2.0 0.7 stack.111
  2.7 0.8 iota_compare_fusion.18
  4.2 0.8 add_select_fusion.5
  5.7 1.3 %multiply_add_fusion.4 = (f32[1,4096]{1,0:T(1,128)S(1)}, f32[1,4096]{1,0:T(1,128)S(1)}) fusion(f32[2,4096]{1,0:T(2,128)} %param.11, f32[3,4096]{1,0:T(4,128)S(1)} %fusion.27, f32[3,4096]{1,0:T(4,128)S(1)} %fusion.26), kind=kLoop, calls=%fused_computation.138 | loop fusion | flops 36864 | bytes 163840 | tf_op jit(solution)/shard_map/add | solution.py:122
  7.5 1.2 %fusion.7 = f32[384,256]{1,0:T(8,128)S(1)} fusion(bf16[128,4096]{1,0:T(8,128)(2,1)S(1)} %bitcast.91, bf16[128,4096]{1,0:T(8,128)(2,1)S(1)} %bitcast.90, bf16[128,4096]{1,0:T(8,128)(2,1)S(1)} %bitcast.89, s32[4096]{0:T(1024)S(1)} %bitcast.116), kind=kOutput, calls=%fused_computation.10 | convolution fusion | flops 815792128 | bytes 3555328 | tf_op jit(solution)/shard_map/dot_general | solution.py:148
  8.7 0.7 copy.30
  9.5 10.2 %all-to-all-start = ((f32[4,32,256]{2,0,1:T(4,128)}), f32[4,32,256]{2,0,1:T(4,128)S(1)}, u32[]{:S(2)}, u32[]{:S(2)}) async-start(f32[4,32,256]{2,0,1:T(4,128)} %copy.30), calls=%async_computation | async-start | bytes 262144 | tf_op jit(solution)/shard_map/all_to_all | solution.py:151
  19.7 9.6 %all-to-all-done = f32[4,32,256]{2,0,1:T(4,128)S(1)} async-done(((f32[4,32,256]{2,0,1:T(4,128)}), f32[4,32,256]{2,0,1:T(4,128)S(1)}, u32[]{:S(2)}, u32[]{:S(2)}) %all-to-all-start) | async-done | bytes 131104 | tf_op jit(solution)/shard_map/all_to_all | solution.py:151
  29.9 0.6 fusion.20
  30.4 0.6 fusion.21
  31.1 1.0 negate_multiply_fusion.1
  32.1 0.9 fusion.56
  33.3 2.1 %fusion.2 = f32[384,96]{0,1:T(8,128)S(1)} fusion(s32[8192]{0:T(1024)S(1)} %get-tuple-element.44, bf16[8192]{0:T(1024)(128)(2,1)S(1)} %bitcast.117, s32[8192]{0:T(1024)S(1)} %get-tuple-element.46), kind=kOutput, calls=%fused_computation.4 | convolution fusion | flops 611057664 | bytes 229376 | tf_op jit(solution)/shard_map/dot_general | solution.py:64
  35.5 20.1 %all_to_all.20 = f32[16,24,128]{2,1,0:T(8,128)S(1)} all-to-all(f32[16,24,128]{2,1,0:T(8,128)S(1)} %bitcast.92), channel_id=1, replica_groups=mesh['ta'=32,'pb'=16] {'pb'}, dimensions={0} | all-to-all | bytes 393216 | tf_op jit(solution)/shard_map/all_to_all | solution.py:72
  55.7 13.0 %all_to_all.21 = f32[16,24,128]{2,1,0:T(8,128)S(1)} all-to-all(f32[16,24,128]{2,1,0:T(8,128)S(1)} %broadcast_in_dim.70), channel_id=1, replica_groups=mesh['ta'=32,'pb'=16] {'pb'}, dimensions={0} | all-to-all | bytes 393216 | tf_op jit(solution)/shard_map/all_to_all | solution.py:73
  69.2 2.5 %collective-permute-start = (f32[104,96]{1,0:T(8,128)S(1)}, f32[104,96]{1,0:T(8,128)S(1)}, u32[]{:S(2)}, u32[]{:S(2)}) collective-permute-start(f32[104,96]{1,0:T(8,128)S(1)} %select_maximum_fusion.1), channel_id=1, source_target_pairs={{0,16},{16,32},{32,48},{48,64},{64,80},{80,96},{96,112},{112,128},... | collective-permute-start | bytes 119816 | tf_op jit(solution)/shard_map/ppermute | solution.py:23
  71.7 5.7 %collective-permute-start.1 = (f32[96,96]{1,0:T(8,128)S(1)}, f32[96,96]{1,0:T(8,128)S(1)}, u32[]{:S(2)}, u32[]{:S(2)}) collective-permute-start(f32[96,96]{1,0:T(8,128)S(1)} %get-tuple-element.26), channel_id=1, source_target_pairs={{16,0},{32,16},{48,32},{64,48},{80,64},{96,80},{112,96},{128,112},... | collective-permute-start | bytes 110600 | tf_op jit(solution)/shard_map/ppermute | solution.py:23
  77.4 2.8 %fusion.1 = f32[192,8192]{1,0:T(8,128)S(1)} fusion(s32[8192]{0:T(1024)S(1)} %get-tuple-element.44, bf16[384,96]{1,0:T(8,128)(2,1)S(1)} %get-tuple-element.24, bf16[384,96]{1,0:T(8,128)(2,1)S(1)} %get-tuple-element.23), kind=kOutput, calls=%fused_computation.3 | convolution fusion | flops 1211400192 | bytes 6471680 | tf_op jit(solution)/shard_map/dot_general | solution.py:218
  80.6 1.5 %fusion.6 = f32[192,8192]{1,0:T(8,128)S(1)} fusion(s32[8192]{0:T(1024)S(1)} %get-tuple-element.16, bf16[192,96]{1,0:T(8,128)(2,1)S(1)} %get-tuple-element.38, bf16[192,96]{1,0:T(8,128)(2,1)S(1)} %get-tuple-element.37), kind=kOutput, calls=%fused_computation.8 | convolution fusion | flops 605700096 | bytes 6397952 | tf_op jit(solution)/shard_map/dot_general | solution.py:218
  82.1 1.4 %fusion.9 = (f32[8192]{0:T(1024)S(1)}, f32[8192]{0:T(1024)S(1)}) fusion(f32[192,8192]{1,0:T(8,128)S(1)} %fusion.6, s32[8192]{0:T(1024)S(1)} %get-tuple-element.46, f32[192,8192]{1,0:T(8,128)S(1)} %fusion.1), kind=kLoop, calls=%fused_computation.13 | loop fusion | flops 5488640 | bytes 12681216 | tf_op jit(solution)/shard_map/reduce_sum | solution.py:220
  83.5 1.9 %negate_multiply_fusion = (f32[1,8192]{1,0:T(1,128)S(1)}, f32[1,8192]{1,0:T(1,128)S(1)}) fusion(f32[1,8192]{1,0:T(1,128)S(1)} %get-tuple-element.19, f32[1,8192]{1,0:T(1,128)S(1)} %bitcast.86, f32[1,8192]{1,0:T(1,128)S(1)} %bitcast.102, f32[1,8192]{1,0:T(1,128)S(1)} %bitcast.101, f32[1,8192]{1,0:T(1,128)S(1)} %get-tuple-element.20, ...), kind=kLoop, calls=%fused_computation.124 | loop fusion | flops 106496 | bytes 294912 | tf_op jit(solution)/shard_map/mul | solution.py:184
  85.5 0.9 fusion.57
  86.6 0.6 broadcast_in_dim.72
  87.2 3.5 %all-to-all-start.3 = ((f32[16,2,4]{2,1,0:T(2,128)}), f32[16,2,4]{2,1,0:T(2,128)S(1)}, u32[]{:S(2)}, u32[]{:S(2)}) async-start(f32[16,2,4]{2,1,0:T(2,128)} %broadcast_in_dim.72), calls=%async_computation.3 | async-start | bytes 32768 | tf_op jit(solution)/shard_map/all_to_all | solution.py:80
  90.8 7.4 %all-to-all-done.3 = f32[16,2,4]{2,1,0:T(2,128)S(1)} async-done(((f32[16,2,4]{2,1,0:T(2,128)}), f32[16,2,4]{2,1,0:T(2,128)S(1)}, u32[]{:S(2)}, u32[]{:S(2)}) %all-to-all-start.3) | async-done | bytes 544 | tf_op jit(solution)/shard_map/all_to_all | solution.py:80
  98.4 1.9 %collective-permute-start.2 = (f32[2,1]{1,0:T(2,128)S(1)}, f32[2,1]{1,0:T(2,128)S(1)}, u32[]{:S(2)}, u32[]{:S(2)}) collective-permute-start(f32[2,1]{1,0:T(2,128)S(1)} %slice.191), channel_id=1, source_target_pairs={{0,16},{16,32},{32,48},{48,64},{64,80},{80,96},{96,112},{112,128},... | collective-permute-start | bytes 32 | tf_op jit(solution)/shard_map/ppermute | solution.py:23
  100.6 1.1 %compare_select_fusion.1 = (f32[1,8192]{1,0:T(1,128)S(1)}, f32[1,8192]{1,0:T(1,128)S(1)}) fusion(f32[1,8192]{1,0:T(1,128)S(1)} %bitcast.97, f32[1,8192]{1,0:T(1,128)S(1)} %bitcast.88, f32[1,8192]{1,0:T(1,128)S(1)} %get-tuple-element.15, f32[1,8192]{1,0:T(1,128)S(1)} %bitcast.110, f32[1,8192]{1,0:T(1,128)S(1)} %bitcast.109, f32[1,8192]{1,0:T(1,128)S(1)} %get-tuple-element.20), kind=kLoop, calls=%fused_computation.94 | loop fusion | flops 106496 | bytes 262144 | tf_op jit(solution)/shard_map/jit(_where)/select_n | solution.py:253
  101.7 0.7 pad_maximum_fusion.2
  102.4 3.6 %collective-permute-done.2 = f32[2,1]{1,0:T(2,128)S(1)} collective-permute-done((f32[2,1]{1,0:T(2,128)S(1)}, f32[2,1]{1,0:T(2,128)S(1)}, u32[]{:S(2)}, u32[]{:S(2)}) %collective-permute-start.2) | collective-permute-done | bytes 40 | tf_op jit(solution)/shard_map/ppermute | solution.py:23
  106.0 0.6 pad_maximum_fusion.5
  (61 shorter events, 4.7 us)
Async XLA Ops:
  7.4 12.2 %copy-start.2 = (f32[96]{0:T(128)S(1)}, f32[96]{0:T(128)}, u32[]{:S(2)}) copy-start(f32[96]{0:T(128)} %param.18) | copy-start | bytes 1156
  7.5 12.2 %copy-start.3 = (f32[96]{0:T(128)S(1)}, f32[96]{0:T(128)}, u32[]{:S(2)}) copy-start(f32[96]{0:T(128)} %param.19) | copy-start | bytes 1156
  9.5 19.8 %all-to-all-start = ((f32[4,32,256]{2,0,1:T(4,128)}), f32[4,32,256]{2,0,1:T(4,128)S(1)}, u32[]{:S(2)}, u32[]{:S(2)}) async-start(f32[4,32,256]{2,0,1:T(4,128)} %copy.30), calls=%async_computation | async-start | bytes 262144 | tf_op jit(solution)/shard_map/all_to_all | solution.py:151
  33.3 35.5 %copy-start = (f32[96,96]{1,0:T(8,128)S(1)}, f32[96,96]{1,0:T(8,128)}, u32[]{:S(2)}) copy-start(f32[96,96]{1,0:T(8,128)} %param.20) | copy-start | bytes 110596
  33.3 35.5 %copy-start.1 = (f32[96,96]{1,0:T(8,128)S(1)}, f32[96,96]{1,0:T(8,128)}, u32[]{:S(2)}) copy-start(f32[96,96]{1,0:T(8,128)} %param.21) | copy-start | bytes 110596
  69.2 11.3 %collective-permute-start = (f32[104,96]{1,0:T(8,128)S(1)}, f32[104,96]{1,0:T(8,128)S(1)}, u32[]{:S(2)}, u32[]{:S(2)}) collective-permute-start(f32[104,96]{1,0:T(8,128)S(1)} %select_maximum_fusion.1), channel_id=1, source_target_pairs={{0,16},{16,32},{32,48},{48,64},{64,80},{80,96},{96,112},{112,128},... | collective-permute-start | bytes 119816 | tf_op jit(solution)/shard_map/ppermute | solution.py:23
  71.7 8.8 %collective-permute-start.1 = (f32[96,96]{1,0:T(8,128)S(1)}, f32[96,96]{1,0:T(8,128)S(1)}, u32[]{:S(2)}, u32[]{:S(2)}) collective-permute-start(f32[96,96]{1,0:T(8,128)S(1)} %get-tuple-element.26), channel_id=1, source_target_pairs={{16,0},{32,16},{48,32},{64,48},{80,64},{96,80},{112,96},{128,112},... | collective-permute-start | bytes 110600 | tf_op jit(solution)/shard_map/ppermute | solution.py:23
  87.2 11.1 %all-to-all-start.3 = ((f32[16,2,4]{2,1,0:T(2,128)}), f32[16,2,4]{2,1,0:T(2,128)S(1)}, u32[]{:S(2)}, u32[]{:S(2)}) async-start(f32[16,2,4]{2,1,0:T(2,128)} %broadcast_in_dim.72), calls=%async_computation.3 | async-start | bytes 32768 | tf_op jit(solution)/shard_map/all_to_all | solution.py:80
  98.4 7.6 %collective-permute-start.2 = (f32[2,1]{1,0:T(2,128)S(1)}, f32[2,1]{1,0:T(2,128)S(1)}, u32[]{:S(2)}, u32[]{:S(2)}) collective-permute-start(f32[2,1]{1,0:T(2,128)S(1)} %slice.191), channel_id=1, source_target_pairs={{0,16},{16,32},{32,48},{48,64},{64,80},{80,96},{96,112},{112,128},... | collective-permute-start | bytes 32 | tf_op jit(solution)/shard_map/ppermute | solution.py:23

commit v10 on v8

--- a/solution.py
+++ b/solution.py
@@ -234,6 +234,7 @@
             radiation = radiation + radiation0
         else:
             cosine, sine_part, local_sums = local_bunching(got_phase)
+            cosine, sine_part = lax.optimization_barrier((cosine, sine_part))
             bunching = pb_sum_small(local_sums, "pb")
             radiation = radiation + couple * bunching
         real_here = jnp.sum(select * radiation[0][:, None], axis=0)

time: 101 us -> 101 us (level)
  other arithmetic: 14.1 us -> 11.8 us
  waiting for transfers between devices: 9.94 us -> 12.1 us
    ppermute x3, waiting for transfers between devices: 2.49 us -> 4.68 us  [shifted(): lax.ppermute(value, axis, [(source, source + steps) for source in range(l...]
    select_n x1, other arithmetic: 2.16 us -> 0.03 us  [body(): jnp.where(filled, got_phase, 0.0)]
  transfers between devices with their start and end apart: 4 -> 4, of which waited for: 2 -> 2; matrix products, arithmetic and copies ran while one was open for 6% -> 4% of each run, Pallas kernels for 0% -> 0%
where the time goes in v10:
time: 101 us
  blocking collectives  52.7 us (52%)
  starting transfers between devices  13.5 us (13%)
  waiting for transfers between devices  12.1 us (12%)
  other arithmetic  11.8 us (12%)
  matrix products  8.01 us (8%)
  local copies, waits for them, and re-layouts  1.62 us (2%)
    all_to_all x1, blocking collectives, pb_sum(): mine = jnp.sum(lax.all_to_all(chunks, axis, 0, 0, tiled=True), axis=0)  20.1 us
    all_to_all x1, blocking collectives, body(): lax.all_to_all(send.reshape(value_count, groups, capacity), 'ta', split_a...  19.6 us
    all_to_all x1, blocking collectives, pb_sum(): lax.all_to_all(jnp.broadcast_to(mine[None], chunks.shape), axis, 0, 0, ti...  13 us
    ppermute x3, starting transfers between devices, shifted(): lax.ppermute(value, axis, [(source, source + steps) for source in range(l...  10 us
    all_to_all x1, waiting for transfers between devices, pb_sum_small(): return jnp.sum(lax.all_to_all(spread, axis, 0, 0, tiled=True), axis=0)  7.44 us
    ppermute x3, waiting for transfers between devices, shifted(): lax.ppermute(value, axis, [(source, source + steps) for source in range(l...  4.68 us
    dot_general x2, matrix products, pick(): picked = jnp.dot(table_parts, pick_row, preferred_element_type=jnp.float32)  4.35 us
    all_to_all x1, starting transfers between devices, pb_sum_small(): return jnp.sum(lax.all_to_all(spread, axis, 0, 0, tiled=True), axis=0)  3.49 us
  transfers between devices with their start and end apart: 4, of which 2 were waited for; matrix products, arithmetic and copies ran while one was open for 4% of the time, Pallas kernels for 0%

profile of v10, /device:TPU:8, one launch (start us, length us, event | category | flops | bytes accessed | tf_op | source)
XLA Modules:
  0.0 100.8 jit_solution(8584152620361288989)
XLA Ops:
  0.6 0.7 stack.53
  1.3 0.8 iota_compare_fusion.14
  2.5 0.3 fusion.23
  2.9 0.8 add_select_fusion.5
  3.6 1.2 %select_reduce_fusion.2 = (f32[4096]{0:T(1024)S(1)}, f32[4096]{0:T(1024)S(1)}) fusion(f32[96]{0:T(128)} %param.17, s32[4096]{0:T(1024)S(1)} %get-tuple-element.55, f32[96]{0:T(128)} %param.16, s32[4096]{0:T(1024)S(1)} %get-tuple-element.57), kind=kLoop, calls=%fused_computation.32 | loop fusion | flops 2351104 | bytes 66304 | tf_op jit(solution)/shard_map/reduce_sum | solution.py:28
  4.9 1.3 %multiply_add_fusion.4 = (f32[1,4096]{1,0:T(1,128)S(1)}, f32[1,4096]{1,0:T(1,128)S(1)}) fusion(f32[2,4096]{1,0:T(2,128)} %param.11, f32[1,4096]{1,0:T(1,128)S(1)} %bitcast.72), kind=kLoop, calls=%fused_computation.124 | loop fusion | flops 16384 | bytes 81920 | tf_op jit(solution)/shard_map/add | solution.py:118
  6.3 0.3 broadcast_select_fusion.2
  6.6 1.2 %fusion.7 = f32[384,256]{1,0:T(8,128)S(1)} fusion(bf16[128,4096]{1,0:T(8,128)(2,1)S(1)} %bitcast.54, bf16[128,4096]{1,0:T(8,128)(2,1)S(1)} %bitcast.53, bf16[128,4096]{1,0:T(8,128)(2,1)S(1)} %bitcast.52, s32[4096]{0:T(1024)S(1)} %bitcast.75), kind=kOutput, calls=%fused_computation.10 | convolution fusion | flops 815792128 | bytes 3555328 | tf_op jit(solution)/shard_map/dot_general | solution.py:144
  8.0 19.6 %all_to_all.20 = f32[4,32,256]{2,0,1:T(4,128)S(1)} all-to-all(f32[4,32,256]{2,0,1:T(4,128)S(1)} %copy.30), channel_id=1, replica_groups=mesh['ta'=32,'pb'=16] {'ta'}, dimensions={1} | all-to-all | bytes 262144 | tf_op jit(solution)/shard_map/all_to_all | solution.py:147
  28.2 0.6 select_reduce_fusion
  28.7 0.6 select_reduce_fusion.1
  29.6 0.2 select_reduce_fusion.11
  29.9 2.1 %fusion.2 = f32[384,96]{0,1:T(8,128)S(1)} fusion(s32[8192]{0:T(1024)S(1)} %get-tuple-element.52, bf16[8192]{0:T(1024)(128)(2,1)S(1)} %convert_element_type.104, s32[8192]{0:T(1024)S(1)} %get-tuple-element.54), kind=kOutput, calls=%fused_computation.4 | convolution fusion | flops 611057664 | bytes 229376 | tf_op jit(solution)/shard_map/dot_general | solution.py:60
  32.1 20.1 %all_to_all.21 = f32[16,24,128]{2,1,0:T(8,128)S(1)} all-to-all(f32[16,24,128]{2,1,0:T(8,128)S(1)} %bitcast.55), channel_id=1, replica_groups=mesh['ta'=32,'pb'=16] {'pb'}, dimensions={0} | all-to-all | bytes 393216 | tf_op jit(solution)/shard_map/all_to_all | solution.py:68
  52.3 13.0 %all_to_all.22 = f32[16,24,128]{2,1,0:T(8,128)S(1)} all-to-all(f32[16,24,128]{2,1,0:T(8,128)S(1)} %broadcast_in_dim.163), channel_id=1, replica_groups=mesh['ta'=32,'pb'=16] {'pb'}, dimensions={0} | all-to-all | bytes 393216 | tf_op jit(solution)/shard_map/all_to_all | solution.py:69
  65.6 0.2 slice_reduce_fusion
  65.8 2.5 %collective-permute-start = (f32[104,96]{1,0:T(8,128)S(1)}, f32[104,96]{1,0:T(8,128)S(1)}, u32[]{:S(2)}, u32[]{:S(2)}) collective-permute-start(f32[104,96]{1,0:T(8,128)S(1)} %select_maximum_fusion.1), channel_id=1, source_target_pairs={{0,16},{16,32},{32,48},{48,64},{64,80},{80,96},{96,112},{112,128},... | collective-permute-start | bytes 119816 | tf_op jit(solution)/shard_map/ppermute | solution.py:23
  68.3 5.7 %collective-permute-start.1 = (f32[96,96]{1,0:T(8,128)S(1)}, f32[96,96]{1,0:T(8,128)S(1)}, u32[]{:S(2)}, u32[]{:S(2)}) collective-permute-start(f32[96,96]{1,0:T(8,128)S(1)} %get-tuple-element.31), channel_id=1, source_target_pairs={{16,0},{32,16},{48,32},{64,48},{80,64},{96,80},{112,96},{128,112},... | collective-permute-start | bytes 110600 | tf_op jit(solution)/shard_map/ppermute | solution.py:23
  74.1 2.8 %fusion.1 = f32[192,8192]{1,0:T(8,128)S(1)} fusion(s32[8192]{0:T(1024)S(1)} %get-tuple-element.52, bf16[384,96]{1,0:T(8,128)(2,1)S(1)} %get-tuple-element.29, bf16[384,96]{1,0:T(8,128)(2,1)S(1)} %get-tuple-element.28), kind=kOutput, calls=%fused_computation.3 | convolution fusion | flops 1211400192 | bytes 6471680 | tf_op jit(solution)/shard_map/dot_general | solution.py:214
  76.9 0.2 select_reduce_fusion.9
  77.2 1.5 %fusion.6 = f32[192,8192]{1,0:T(8,128)S(1)} fusion(s32[8192]{0:T(1024)S(1)} %get-tuple-element.22, bf16[192,96]{1,0:T(8,128)(2,1)S(1)} %get-tuple-element.43, bf16[192,96]{1,0:T(8,128)(2,1)S(1)} %get-tuple-element.42), kind=kOutput, calls=%fused_computation.8 | convolution fusion | flops 605700096 | bytes 6397952 | tf_op jit(solution)/shard_map/dot_general | solution.py:214
  78.7 1.4 %fusion.9 = (f32[8192]{0:T(1024)S(1)}, f32[8192]{0:T(1024)S(1)}) fusion(f32[192,8192]{1,0:T(8,128)S(1)} %fusion.6, s32[8192]{0:T(1024)S(1)} %get-tuple-element.54, f32[192,8192]{1,0:T(8,128)S(1)} %fusion.1), kind=kLoop, calls=%fused_computation.13 | loop fusion | flops 5488640 | bytes 12681216 | tf_op jit(solution)/shard_map/reduce_sum | solution.py:216
  80.1 0.3 multiply_sine_fusion
  80.5 0.2 select_reduce_fusion.7
  80.8 0.6 broadcast_in_dim.164
  81.4 3.5 %all-to-all-start.3 = ((f32[16,2,4]{2,1,0:T(2,128)}), f32[16,2,4]{2,1,0:T(2,128)S(1)}, u32[]{:S(2)}, u32[]{:S(2)}) async-start(f32[16,2,4]{2,1,0:T(2,128)} %broadcast_in_dim.164), calls=%async_computation.3 | async-start | bytes 32768 | tf_op jit(solution)/shard_map/all_to_all | solution.py:76
  85.0 7.4 %all-to-all-done.3 = f32[16,2,4]{2,1,0:T(2,128)S(1)} async-done(((f32[16,2,4]{2,1,0:T(2,128)}), f32[16,2,4]{2,1,0:T(2,128)S(1)}, u32[]{:S(2)}, u32[]{:S(2)}) %all-to-all-start.3) | async-done | bytes 544 | tf_op jit(solution)/shard_map/all_to_all | solution.py:76
  92.6 1.9 %collective-permute-start.2 = (f32[2,1]{1,0:T(2,128)S(1)}, f32[2,1]{1,0:T(2,128)S(1)}, u32[]{:S(2)}, u32[]{:S(2)}) collective-permute-start(f32[2,1]{1,0:T(2,128)S(1)} %slice.143), channel_id=1, source_target_pairs={{0,16},{16,32},{32,48},{48,64},{64,80},{80,96},{96,112},{112,128},... | collective-permute-start | bytes 32 | tf_op jit(solution)/shard_map/ppermute | solution.py:23
  94.5 0.2 select_reduce_fusion.5
  94.8 0.7 pad_maximum_fusion.2
  95.5 4.7 %collective-permute-done.2 = f32[2,1]{1,0:T(2,128)S(1)} collective-permute-done((f32[2,1]{1,0:T(2,128)S(1)}, f32[2,1]{1,0:T(2,128)S(1)}, u32[]{:S(2)}, u32[]{:S(2)}) %collective-permute-start.2) | collective-permute-done | bytes 40 | tf_op jit(solution)/shard_map/ppermute | solution.py:23
  100.2 0.6 pad_maximum_fusion.5
  (54 shorter events, 2.6 us)
Async XLA Ops:
  6.6 21.6 %copy-start.2 = (f32[96]{0:T(128)S(1)}, f32[96]{0:T(128)}, u32[]{:S(2)}) copy-start(f32[96]{0:T(128)} %param.19) | copy-start | bytes 1156
  6.6 22.1 %copy-start.3 = (f32[96]{0:T(128)S(1)}, f32[96]{0:T(128)}, u32[]{:S(2)}) copy-start(f32[96]{0:T(128)} %param.18) | copy-start | bytes 1156
  29.9 35.5 %copy-start = (f32[96,96]{1,0:T(8,128)S(1)}, f32[96,96]{1,0:T(8,128)}, u32[]{:S(2)}) copy-start(f32[96,96]{1,0:T(8,128)} %param.20) | copy-start | bytes 110596
  29.9 35.5 %copy-start.1 = (f32[96,96]{1,0:T(8,128)S(1)}, f32[96,96]{1,0:T(8,128)}, u32[]{:S(2)}) copy-start(f32[96,96]{1,0:T(8,128)} %param.21) | copy-start | bytes 110596
  65.8 11.3 %collective-permute-start = (f32[104,96]{1,0:T(8,128)S(1)}, f32[104,96]{1,0:T(8,128)S(1)}, u32[]{:S(2)}, u32[]{:S(2)}) collective-permute-start(f32[104,96]{1,0:T(8,128)S(1)} %select_maximum_fusion.1), channel_id=1, source_target_pairs={{0,16},{16,32},{32,48},{48,64},{64,80},{80,96},{96,112},{112,128},... | collective-permute-start | bytes 119816 | tf_op jit(solution)/shard_map/ppermute | solution.py:23
  68.3 8.8 %collective-permute-start.1 = (f32[96,96]{1,0:T(8,128)S(1)}, f32[96,96]{1,0:T(8,128)S(1)}, u32[]{:S(2)}, u32[]{:S(2)}) collective-permute-start(f32[96,96]{1,0:T(8,128)S(1)} %get-tuple-element.31), channel_id=1, source_target_pairs={{16,0},{32,16},{48,32},{64,48},{80,64},{96,80},{112,96},{128,112},... | collective-permute-start | bytes 110600 | tf_op jit(solution)/shard_map/ppermute | solution.py:23
  81.4 11.1 %all-to-all-start.3 = ((f32[16,2,4]{2,1,0:T(2,128)}), f32[16,2,4]{2,1,0:T(2,128)S(1)}, u32[]{:S(2)}, u32[]{:S(2)}) async-start(f32[16,2,4]{2,1,0:T(2,128)} %broadcast_in_dim.164), calls=%async_computation.3 | async-start | bytes 32768 | tf_op jit(solution)/shard_map/all_to_all | solution.py:76
  92.6 7.6 %collective-permute-start.2 = (f32[2,1]{1,0:T(2,128)S(1)}, f32[2,1]{1,0:T(2,128)S(1)}, u32[]{:S(2)}, u32[]{:S(2)}) collective-permute-start(f32[2,1]{1,0:T(2,128)S(1)} %slice.143), channel_id=1, source_target_pairs={{0,16},{16,32},{32,48},{48,64},{64,80},{80,96},{96,112},{112,128},... | collective-permute-start | bytes 32 | tf_op jit(solution)/shard_map/ppermute | solution.py:23

commit v11 on v10

--- a/solution.py
+++ b/solution.py
@@ -197,8 +197,8 @@
 
     couple = 1.0 / math.sqrt(splits * PS_DEV)
     radiation0 = couple * bunching0
-    last_row = jnp.pad(radiation0[:, -1:].reshape(1, 2), ((0, 7), (0, grid_y - 2)))
-    halo_below = shifted(jnp.concatenate([density[SL_DEV - 1], last_row]), "ta", 1)
+    last_lanes = jnp.pad(radiation0[:, -1:].reshape(1, 2), ((0, grid_x - 1), (0, lanes - grid_y - 2)))
+    halo_below = shifted(jnp.concatenate([density[SL_DEV - 1], last_lanes], axis=1), "ta", 1)
     above = shifted(density[0], "ta", -1)
     empty = jnp.zeros((1, grid_x, grid_y), jnp.float32)
     force_map = stencil(jnp.concatenate([empty, density, empty]), along_coeff, across_coeff)
@@ -217,7 +217,7 @@
 
     pick_col = jnp.arange(grid_y, dtype=jnp.int32)[:, None] == got_y[None, :]
     force_here = pick(force_map.reshape(SL_DEV * grid_x, grid_y), row_key, SL_DEV * grid_x)
-    below_density = halo_below[:grid_x]
+    below_density = halo_below[:, :grid_y]
     halo_force = jnp.concatenate([-along_coeff * below_density, along_coeff * above]).reshape(
         2 * grid_x, grid_y
     )
@@ -242,7 +242,7 @@
         kicked = kicked + KICK_GAIN * profile * (real_here * cosine - imag_here * sine_part)
         got_phase = got_phase + SLIP_GAIN * kicked
         if period == 0:
-            incoming = halo_below[grid_x, :2].reshape(2, 1)
+            incoming = halo_below[0, grid_y : grid_y + 2].reshape(2, 1)
         else:
             incoming = shifted(radiation[:, -1:], "ta", 1)
         radiation = jnp.concatenate([incoming, radiation[:, :-1]], axis=1)

time: 101 us -> 102 us (level)
  no operation moved by 1% of the time
where the time goes in v11:
time: 102 us; the launch traced here: 101 us
  blocking collectives  52.7 us (52%)
  starting transfers between devices  13.5 us (13%)
  waiting for transfers between devices  12.1 us (12%)
  other arithmetic  11.9 us (12%)
  matrix products  8.01 us (8%)
  local copies, waits for them, and re-layouts  1.7 us (2%)
    all_to_all x1, blocking collectives, pb_sum(): mine = jnp.sum(lax.all_to_all(chunks, axis, 0, 0, tiled=True), axis=0)  20.1 us
    all_to_all x1, blocking collectives, body(): lax.all_to_all(send.reshape(value_count, groups, capacity), 'ta', split_a...  19.6 us
    all_to_all x1, blocking collectives, pb_sum(): lax.all_to_all(jnp.broadcast_to(mine[None], chunks.shape), axis, 0, 0, ti...  13 us
    ppermute x3, starting transfers between devices, shifted(): lax.ppermute(value, axis, [(source, source + steps) for source in range(l...  10 us
    all_to_all x1, waiting for transfers between devices, pb_sum_small(): return jnp.sum(lax.all_to_all(spread, axis, 0, 0, tiled=True), axis=0)  7.38 us
    ppermute x3, waiting for transfers between devices, shifted(): lax.ppermute(value, axis, [(source, source + steps) for source in range(l...  4.68 us
    dot_general x2, matrix products, pick(): picked = jnp.dot(table_parts, pick_row, preferred_element_type=jnp.float32)  4.35 us
    all_to_all x1, starting transfers between devices, pb_sum_small(): return jnp.sum(lax.all_to_all(spread, axis, 0, 0, tiled=True), axis=0)  3.49 us
  transfers between devices with their start and end apart: 4, of which 2 were waited for; matrix products, arithmetic and copies ran while one was open for 4% of the time, Pallas kernels for 0%

profile of v11, /device:TPU:8, one launch (start us, length us, event | category | flops | bytes accessed | tf_op | source)
XLA Modules:
  0.0 100.9 jit_solution(17120956328455231142)
XLA Ops:
  0.6 0.7 stack.53
  1.3 0.8 iota_compare_fusion.14
  2.5 0.3 fusion.23
  2.9 0.8 add_select_fusion.5
  3.6 1.2 %select_reduce_fusion.2 = (f32[4096]{0:T(1024)S(1)}, f32[4096]{0:T(1024)S(1)}) fusion(f32[96]{0:T(128)} %param.17, s32[4096]{0:T(1024)S(1)} %get-tuple-element.55, f32[96]{0:T(128)} %param.16, s32[4096]{0:T(1024)S(1)} %get-tuple-element.57), kind=kLoop, calls=%fused_computation.32 | loop fusion | flops 2351104 | bytes 66304 | tf_op jit(solution)/shard_map/reduce_sum | solution.py:28
  4.9 1.3 %multiply_add_fusion.4 = (f32[1,4096]{1,0:T(1,128)S(1)}, f32[1,4096]{1,0:T(1,128)S(1)}) fusion(f32[2,4096]{1,0:T(2,128)} %param.11, f32[1,4096]{1,0:T(1,128)S(1)} %bitcast.72), kind=kLoop, calls=%fused_computation.124 | loop fusion | flops 16384 | bytes 81920 | tf_op jit(solution)/shard_map/add | solution.py:118
  6.3 0.3 broadcast_select_fusion.2
  6.6 1.2 %fusion.7 = f32[384,256]{1,0:T(8,128)S(1)} fusion(bf16[128,4096]{1,0:T(8,128)(2,1)S(1)} %bitcast.54, bf16[128,4096]{1,0:T(8,128)(2,1)S(1)} %bitcast.53, bf16[128,4096]{1,0:T(8,128)(2,1)S(1)} %bitcast.52, s32[4096]{0:T(1024)S(1)} %bitcast.75), kind=kOutput, calls=%fused_computation.10 | convolution fusion | flops 815792128 | bytes 3555328 | tf_op jit(solution)/shard_map/dot_general | solution.py:144
  8.0 19.6 %all_to_all.20 = f32[4,32,256]{2,0,1:T(4,128)S(1)} all-to-all(f32[4,32,256]{2,0,1:T(4,128)S(1)} %copy.30), channel_id=1, replica_groups=mesh['ta'=32,'pb'=16] {'ta'}, dimensions={1} | all-to-all | bytes 262144 | tf_op jit(solution)/shard_map/all_to_all | solution.py:147
  28.2 0.6 select_reduce_fusion
  28.7 0.6 select_reduce_fusion.1
  29.6 0.2 select_reduce_fusion.11
  29.9 2.1 %fusion.2 = f32[384,96]{0,1:T(8,128)S(1)} fusion(s32[8192]{0:T(1024)S(1)} %get-tuple-element.52, bf16[8192]{0:T(1024)(128)(2,1)S(1)} %convert_element_type.104, s32[8192]{0:T(1024)S(1)} %get-tuple-element.54), kind=kOutput, calls=%fused_computation.4 | convolution fusion | flops 611057664 | bytes 229376 | tf_op jit(solution)/shard_map/dot_general | solution.py:60
  32.1 20.1 %all_to_all.21 = f32[16,24,128]{2,1,0:T(8,128)S(1)} all-to-all(f32[16,24,128]{2,1,0:T(8,128)S(1)} %bitcast.55), channel_id=1, replica_groups=mesh['ta'=32,'pb'=16] {'pb'}, dimensions={0} | all-to-all | bytes 393216 | tf_op jit(solution)/shard_map/all_to_all | solution.py:68
  52.3 13.0 %all_to_all.22 = f32[16,24,128]{2,1,0:T(8,128)S(1)} all-to-all(f32[16,24,128]{2,1,0:T(8,128)S(1)} %broadcast_in_dim.163), channel_id=1, replica_groups=mesh['ta'=32,'pb'=16] {'pb'}, dimensions={0} | all-to-all | bytes 393216 | tf_op jit(solution)/shard_map/all_to_all | solution.py:69
  65.6 0.2 slice_reduce_fusion
  65.9 2.5 %collective-permute-start = (f32[96,128]{1,0:T(8,128)S(1)}, f32[96,128]{1,0:T(8,128)S(1)}, u32[]{:S(2)}, u32[]{:S(2)}) collective-permute-start(f32[96,128]{1,0:T(8,128)S(1)} %select_maximum_fusion.1), channel_id=1, source_target_pairs={{0,16},{16,32},{32,48},{48,64},{64,80},{80,96},{96,112},{112,128},... | collective-permute-start | bytes 147464 | tf_op jit(solution)/shard_map/ppermute | solution.py:23
  68.4 5.7 %collective-permute-start.1 = (f32[96,96]{1,0:T(8,128)S(1)}, f32[96,96]{1,0:T(8,128)S(1)}, u32[]{:S(2)}, u32[]{:S(2)}) collective-permute-start(f32[96,96]{1,0:T(8,128)S(1)} %get-tuple-element.31), channel_id=1, source_target_pairs={{16,0},{32,16},{48,32},{64,48},{80,64},{96,80},{112,96},{128,112},... | collective-permute-start | bytes 110600 | tf_op jit(solution)/shard_map/ppermute | solution.py:23
  74.1 2.8 %fusion.1 = f32[192,8192]{1,0:T(8,128)S(1)} fusion(s32[8192]{0:T(1024)S(1)} %get-tuple-element.52, bf16[384,96]{1,0:T(8,128)(2,1)S(1)} %get-tuple-element.29, bf16[384,96]{1,0:T(8,128)(2,1)S(1)} %get-tuple-element.28), kind=kOutput, calls=%fused_computation.3 | convolution fusion | flops 1211400192 | bytes 6471680 | tf_op jit(solution)/shard_map/dot_general | solution.py:214
  77.0 0.2 select_reduce_fusion.9
  77.3 1.5 %fusion.6 = f32[192,8192]{1,0:T(8,128)S(1)} fusion(s32[8192]{0:T(1024)S(1)} %get-tuple-element.22, bf16[192,96]{1,0:T(8,128)(2,1)S(1)} %get-tuple-element.43, bf16[192,96]{1,0:T(8,128)(2,1)S(1)} %get-tuple-element.42), kind=kOutput, calls=%fused_computation.8 | convolution fusion | flops 605700096 | bytes 6397952 | tf_op jit(solution)/shard_map/dot_general | solution.py:214
  78.8 1.4 %fusion.9 = (f32[8192]{0:T(1024)S(1)}, f32[8192]{0:T(1024)S(1)}) fusion(f32[192,8192]{1,0:T(8,128)S(1)} %fusion.6, s32[8192]{0:T(1024)S(1)} %get-tuple-element.54, f32[192,8192]{1,0:T(8,128)S(1)} %fusion.1), kind=kLoop, calls=%fused_computation.13 | loop fusion | flops 5488640 | bytes 12681216 | tf_op jit(solution)/shard_map/reduce_sum | solution.py:216
  80.2 0.3 multiply_sine_fusion
  80.6 0.2 select_reduce_fusion.7
  80.8 0.6 broadcast_in_dim.164
  81.4 3.5 %all-to-all-start.3 = ((f32[16,2,4]{2,1,0:T(2,128)}), f32[16,2,4]{2,1,0:T(2,128)S(1)}, u32[]{:S(2)}, u32[]{:S(2)}) async-start(f32[16,2,4]{2,1,0:T(2,128)} %broadcast_in_dim.164), calls=%async_computation.3 | async-start | bytes 32768 | tf_op jit(solution)/shard_map/all_to_all | solution.py:76
  85.1 7.4 %all-to-all-done.3 = f32[16,2,4]{2,1,0:T(2,128)S(1)} async-done(((f32[16,2,4]{2,1,0:T(2,128)}), f32[16,2,4]{2,1,0:T(2,128)S(1)}, u32[]{:S(2)}, u32[]{:S(2)}) %all-to-all-start.3) | async-done | bytes 544 | tf_op jit(solution)/shard_map/all_to_all | solution.py:76
  92.7 1.9 %collective-permute-start.2 = (f32[2,1]{1,0:T(2,128)S(1)}, f32[2,1]{1,0:T(2,128)S(1)}, u32[]{:S(2)}, u32[]{:S(2)}) collective-permute-start(f32[2,1]{1,0:T(2,128)S(1)} %slice.143), channel_id=1, source_target_pairs={{0,16},{16,32},{32,48},{48,64},{64,80},{80,96},{96,112},{112,128},... | collective-permute-start | bytes 32 | tf_op jit(solution)/shard_map/ppermute | solution.py:23
  94.6 0.2 select_reduce_fusion.5
  94.9 0.7 pad_maximum_fusion.2
  95.6 4.7 %collective-permute-done.2 = f32[2,1]{1,0:T(2,128)S(1)} collective-permute-done((f32[2,1]{1,0:T(2,128)S(1)}, f32[2,1]{1,0:T(2,128)S(1)}, u32[]{:S(2)}, u32[]{:S(2)}) %collective-permute-start.2) | collective-permute-done | bytes 40 | tf_op jit(solution)/shard_map/ppermute | solution.py:23
  100.2 0.6 pad_maximum_fusion.5
  (54 shorter events, 2.7 us)
Async XLA Ops:
  6.6 21.6 %copy-start.2 = (f32[96]{0:T(128)S(1)}, f32[96]{0:T(128)}, u32[]{:S(2)}) copy-start(f32[96]{0:T(128)} %param.19) | copy-start | bytes 1156
  6.6 22.1 %copy-start.3 = (f32[96]{0:T(128)S(1)}, f32[96]{0:T(128)}, u32[]{:S(2)}) copy-start(f32[96]{0:T(128)} %param.18) | copy-start | bytes 1156
  29.9 35.5 %copy-start = (f32[96,96]{1,0:T(8,128)S(1)}, f32[96,96]{1,0:T(8,128)}, u32[]{:S(2)}) copy-start(f32[96,96]{1,0:T(8,128)} %param.20) | copy-start | bytes 110596
  29.9 35.5 %copy-start.1 = (f32[96,96]{1,0:T(8,128)S(1)}, f32[96,96]{1,0:T(8,128)}, u32[]{:S(2)}) copy-start(f32[96,96]{1,0:T(8,128)} %param.21) | copy-start | bytes 110596
  65.9 11.3 %collective-permute-start = (f32[96,128]{1,0:T(8,128)S(1)}, f32[96,128]{1,0:T(8,128)S(1)}, u32[]{:S(2)}, u32[]{:S(2)}) collective-permute-start(f32[96,128]{1,0:T(8,128)S(1)} %select_maximum_fusion.1), channel_id=1, source_target_pairs={{0,16},{16,32},{32,48},{48,64},{64,80},{80,96},{96,112},{112,128},... | collective-permute-start | bytes 147464 | tf_op jit(solution)/shard_map/ppermute | solution.py:23
  68.4 8.8 %collective-permute-start.1 = (f32[96,96]{1,0:T(8,128)S(1)}, f32[96,96]{1,0:T(8,128)S(1)}, u32[]{:S(2)}, u32[]{:S(2)}) collective-permute-start(f32[96,96]{1,0:T(8,128)S(1)} %get-tuple-element.31), channel_id=1, source_target_pairs={{16,0},{32,16},{48,32},{64,48},{80,64},{96,80},{112,96},{128,112},... | collective-permute-start | bytes 110600 | tf_op jit(solution)/shard_map/ppermute | solution.py:23
  81.4 11.1 %all-to-all-start.3 = ((f32[16,2,4]{2,1,0:T(2,128)}), f32[16,2,4]{2,1,0:T(2,128)S(1)}, u32[]{:S(2)}, u32[]{:S(2)}) async-start(f32[16,2,4]{2,1,0:T(2,128)} %broadcast_in_dim.164), calls=%async_computation.3 | async-start | bytes 32768 | tf_op jit(solution)/shard_map/all_to_all | solution.py:76
  92.7 7.6 %collective-permute-start.2 = (f32[2,1]{1,0:T(2,128)S(1)}, f32[2,1]{1,0:T(2,128)S(1)}, u32[]{:S(2)}, u32[]{:S(2)}) collective-permute-start(f32[2,1]{1,0:T(2,128)S(1)} %slice.143), channel_id=1, source_target_pairs={{0,16},{16,32},{32,48},{48,64},{64,80},{80,96},{96,112},{112,128},... | collective-permute-start | bytes 32 | tf_op jit(solution)/shard_map/ppermute | solution.py:23

commit v12 on v10

--- a/solution.py
+++ b/solution.py
@@ -203,14 +203,15 @@
     empty = jnp.zeros((1, grid_x, grid_y), jnp.float32)
     force_map = stencil(jnp.concatenate([empty, density, empty]), along_coeff, across_coeff)
 
-    def pick(table, key, key_count):
+    def pick(table, key, key_count, early=False):
         table_hi = lax.reduce_precision(table, exponent_bits=8, mantissa_bits=7)
         table_parts = jnp.concatenate(
             [table_hi.astype(jnp.bfloat16), (table - table_hi).astype(jnp.bfloat16)], axis=1
         ).T
-        pick_row = (jnp.arange(key_count, dtype=jnp.int32)[:, None] == key[None, :]).astype(
-            jnp.bfloat16
-        )
+        pick_row = jnp.arange(key_count, dtype=jnp.int32)[:, None] == key[None, :]
+        if early:
+            pick_row = lax.optimization_barrier(pick_row)
+        pick_row = pick_row.astype(jnp.bfloat16)
         picked = jnp.dot(table_parts, pick_row, preferred_element_type=jnp.float32)
         picked = picked[:grid_y] + picked[grid_y:]
         return jnp.sum(jnp.where(pick_col, picked, 0.0), axis=0)
@@ -224,7 +225,7 @@
     halo_key = jnp.where(
         got_slice == 0, got_x, jnp.where(got_slice == SL_DEV - 1, got_x + grid_x, -1)
     )
-    halo_here = pick(halo_force, halo_key, 2 * grid_x)
+    halo_here = pick(halo_force, halo_key, 2 * grid_x, early=True)
     kicked = got_energy + (force_here + halo_here)
 
     radiation = jnp.zeros((2, SL_DEV), jnp.float32)

time: 101 us -> 103 us (1.020)
  blocking collectives: 52.7 us -> 39.7 us
  waiting for transfers between devices: 12.1 us -> 23.9 us
  starting transfers between devices: 13.5 us -> 14.9 us
    all_to_all x1 -> x0, blocking collectives: 13 us -> none  [pb_sum(): lax.all_to_all(jnp.broadcast_to(mine[None], chunks.shape), axis, 0, 0, ti...]
    all_to_all x0 -> x1, waiting for transfers between devices: none -> 9.15 us  [pb_sum(): lax.all_to_all(jnp.broadcast_to(mine[None], chunks.shape), axis, 0, 0, ti...]
    all_to_all x0 -> x1, starting transfers between devices: none -> 3.52 us  [pb_sum(): lax.all_to_all(jnp.broadcast_to(mine[None], chunks.shape), axis, 0, 0, ti...]
    ppermute x3, waiting for transfers between devices: 4.68 us -> 7.31 us  [shifted(): lax.ppermute(value, axis, [(source, source + steps) for source in range(l...]
    ppermute x3, starting transfers between devices: 10 us -> 7.92 us  [shifted(): lax.ppermute(value, axis, [(source, source + steps) for source in range(l...]
  transfers between devices with their start and end apart: 4 -> 5, of which waited for: 2 -> 4; matrix products, arithmetic and copies ran while one was open for 4% -> 5% of each run, Pallas kernels for 0% -> 0%
where the time goes in v12:
time: 103 us; the launch traced here: 102 us
  blocking collectives  39.7 us (39%)
  waiting for transfers between devices  23.9 us (23%)
  starting transfers between devices  14.9 us (14%)
  other arithmetic  12.7 us (12%)
  matrix products  7.58 us (7%)
  local copies, waits for them, and re-layouts  2.3 us (2%)
    all_to_all x1, blocking collectives, pb_sum(): mine = jnp.sum(lax.all_to_all(chunks, axis, 0, 0, tiled=True), axis=0)  20.1 us
    all_to_all x1, blocking collectives, body(): lax.all_to_all(send.reshape(value_count, groups, capacity), 'ta', split_a...  19.6 us
    all_to_all x1, waiting for transfers between devices, pb_sum(): lax.all_to_all(jnp.broadcast_to(mine[None], chunks.shape), axis, 0, 0, ti...  9.15 us
    ppermute x3, starting transfers between devices, shifted(): lax.ppermute(value, axis, [(source, source + steps) for source in range(l...  7.92 us
    all_to_all x1, waiting for transfers between devices, pb_sum_small(): return jnp.sum(lax.all_to_all(spread, axis, 0, 0, tiled=True), axis=0)  7.44 us
    ppermute x3, waiting for transfers between devices, shifted(): lax.ppermute(value, axis, [(source, source + steps) for source in range(l...  7.31 us
    dot_general x2, matrix products, pick(): picked = jnp.dot(table_parts, pick_row, preferred_element_type=jnp.float32)  3.93 us
    all_to_all x1, starting transfers between devices, pb_sum(): lax.all_to_all(jnp.broadcast_to(mine[None], chunks.shape), axis, 0, 0, ti...  3.52 us
  transfers between devices with their start and end apart: 5, of which 4 were waited for; matrix products, arithmetic and copies ran while one was open for 5% of the time, Pallas kernels for 0%

profile of v12, /device:TPU:8, one launch (start us, length us, event | category | flops | bytes accessed | tf_op | source)
XLA Modules:
  0.0 102.1 jit_solution(4915737201294815379)
XLA Ops:
  0.6 0.7 stack.53
  1.3 0.8 iota_compare_fusion.13
  2.5 0.3 fusion.21
  2.9 0.8 add_select_fusion.5
  3.6 1.2 %select_reduce_fusion.2 = (f32[4096]{0:T(1024)S(1)}, f32[4096]{0:T(1024)S(1)}) fusion(f32[96]{0:T(128)} %param.17, s32[4096]{0:T(1024)S(1)} %get-tuple-element.55, f32[96]{0:T(128)} %param.16, s32[4096]{0:T(1024)S(1)} %get-tuple-element.57), kind=kLoop, calls=%fused_computation.30 | loop fusion | flops 2351104 | bytes 66304 | tf_op jit(solution)/shard_map/reduce_sum | solution.py:28
  4.9 1.3 %multiply_add_fusion.4 = (f32[1,4096]{1,0:T(1,128)S(1)}, f32[1,4096]{1,0:T(1,128)S(1)}) fusion(f32[2,4096]{1,0:T(2,128)} %param.11, f32[1,4096]{1,0:T(1,128)S(1)} %bitcast.73), kind=kLoop, calls=%fused_computation.123 | loop fusion | flops 16384 | bytes 81920 | tf_op jit(solution)/shard_map/add | solution.py:118
  6.3 0.3 broadcast_select_fusion.2
  6.6 1.2 %fusion.6 = f32[384,256]{1,0:T(8,128)S(1)} fusion(bf16[128,4096]{1,0:T(8,128)(2,1)S(1)} %bitcast.55, bf16[128,4096]{1,0:T(8,128)(2,1)S(1)} %bitcast.54, bf16[128,4096]{1,0:T(8,128)(2,1)S(1)} %bitcast.53, s32[4096]{0:T(1024)S(1)} %bitcast.76), kind=kOutput, calls=%fused_computation.9 | convolution fusion | flops 815792128 | bytes 3555328 | tf_op jit(solution)/shard_map/dot_general | solution.py:144
  8.0 19.6 %all_to_all.20 = f32[4,32,256]{2,0,1:T(4,128)S(1)} all-to-all(f32[4,32,256]{2,0,1:T(4,128)S(1)} %copy.30), channel_id=1, replica_groups=mesh['ta'=32,'pb'=16] {'ta'}, dimensions={1} | all-to-all | bytes 262144 | tf_op jit(solution)/shard_map/all_to_all | solution.py:147
  28.2 0.6 select_reduce_fusion.1
  28.7 0.6 select_reduce_fusion
  29.9 2.1 %fusion.2 = f32[384,96]{0,1:T(8,128)S(1)} fusion(s32[8192]{0:T(1024)S(1)} %get-tuple-element.52, bf16[8192]{0:T(1024)(128)(2,1)S(1)} %convert_element_type.104, s32[8192]{0:T(1024)S(1)} %get-tuple-element.54), kind=kOutput, calls=%fused_computation.4 | convolution fusion | flops 611057664 | bytes 229376 | tf_op jit(solution)/shard_map/dot_general | solution.py:60
  32.1 20.1 %all_to_all.21 = f32[16,24,128]{2,1,0:T(8,128)S(1)} all-to-all(f32[16,24,128]{2,1,0:T(8,128)S(1)} %bitcast.56), channel_id=1, replica_groups=mesh['ta'=32,'pb'=16] {'pb'}, dimensions={0} | all-to-all | bytes 393216 | tf_op jit(solution)/shard_map/all_to_all | solution.py:68
  52.3 0.7 broadcast_in_dim.163
  53.0 3.5 %all-to-all-start.2 = ((f32[16,24,128]{2,1,0:T(8,128)}), f32[16,24,128]{2,1,0:T(8,128)S(1)}, u32[]{:S(2)}, u32[]{:S(2)}) async-start(f32[16,24,128]{2,1,0:T(8,128)} %broadcast_in_dim.163), calls=%async_computation.2 | async-start | bytes 393216 | tf_op jit(solution)/shard_map/all_to_all | solution.py:69
  56.5 0.8 iota_compare_fusion.3
  57.3 9.1 %all-to-all-done.2 = f32[16,24,128]{2,1,0:T(8,128)S(1)} async-done(((f32[16,24,128]{2,1,0:T(8,128)}), f32[16,24,128]{2,1,0:T(8,128)S(1)}, u32[]{:S(2)}, u32[]{:S(2)}) %all-to-all-start.2) | async-done | bytes 196640 | tf_op jit(solution)/shard_map/all_to_all | solution.py:69
  66.9 3.8 %collective-permute-start.1 = (f32[96,96]{1,0:T(8,128)S(1)}, f32[96,96]{1,0:T(8,128)S(1)}, u32[]{:S(2)}, u32[]{:S(2)}) collective-permute-start(f32[96,96]{1,0:T(8,128)S(1)} %get-tuple-element.31), channel_id=1, source_target_pairs={{16,0},{32,16},{48,32},{64,48},{80,64},{96,80},{112,96},{128,112},... | collective-permute-start | bytes 110600 | tf_op jit(solution)/shard_map/ppermute | solution.py:23
  70.8 2.2 %collective-permute-start = (f32[104,96]{1,0:T(8,128)S(1)}, f32[104,96]{1,0:T(8,128)S(1)}, u32[]{:S(2)}, u32[]{:S(2)}) collective-permute-start(f32[104,96]{1,0:T(8,128)S(1)} %select_maximum_fusion.1), channel_id=1, source_target_pairs={{0,16},{16,32},{32,48},{48,64},{64,80},{80,96},{96,112},{112,128},... | collective-permute-start | bytes 119816 | tf_op jit(solution)/shard_map/ppermute | solution.py:23
  73.2 2.8 %fusion.1 = f32[192,8192]{1,0:T(8,128)S(1)} fusion(s32[8192]{0:T(1024)S(1)} %get-tuple-element.52, bf16[384,96]{1,0:T(8,128)(2,1)S(1)} %get-tuple-element.29, bf16[384,96]{1,0:T(8,128)(2,1)S(1)} %get-tuple-element.28), kind=kOutput, calls=%fused_computation.3 | convolution fusion | flops 1211400192 | bytes 6471680 | tf_op jit(solution)/shard_map/dot_general | solution.py:215
  76.3 2.6 %collective-permute-done = f32[104,96]{1,0:T(8,128)S(1)} collective-permute-done((f32[104,96]{1,0:T(8,128)S(1)}, f32[104,96]{1,0:T(8,128)S(1)}, u32[]{:S(2)}, u32[]{:S(2)}) %collective-permute-start) | collective-permute-done | bytes 39968 | tf_op jit(solution)/shard_map/ppermute | solution.py:23
  78.9 1.1 %fusion.37 = f32[192,8192]{1,0:T(8,128)S(1)} fusion(pred[192,8192]{1,0:T(32,128)(4,1)S(1)} %iota_compare_fusion.3, bf16[192,96]{1,0:T(8,128)(2,1)S(1)} %get-tuple-element.43, bf16[192,96]{1,0:T(8,128)(2,1)S(1)} %get-tuple-element.42), kind=kOutput, calls=%fused_computation.80 | convolution fusion | flops 604127232 | bytes 7938048 | tf_op jit(solution)/shard_map/dot_general | solution.py:215
  80.0 1.4 %fusion.8 = (f32[8192]{0:T(1024)S(1)}, f32[8192]{0:T(1024)S(1)}) fusion(f32[192,8192]{1,0:T(8,128)S(1)} %fusion.37, s32[8192]{0:T(1024)S(1)} %get-tuple-element.54, f32[192,8192]{1,0:T(8,128)S(1)} %fusion.1), kind=kLoop, calls=%fused_computation.12 | loop fusion | flops 5488640 | bytes 12681216 | tf_op jit(solution)/shard_map/reduce_sum | solution.py:217
  81.4 0.3 multiply_sine_fusion
  82.1 0.6 broadcast_in_dim.164
  82.7 3.5 %all-to-all-start.3 = ((f32[16,2,4]{2,1,0:T(2,128)}), f32[16,2,4]{2,1,0:T(2,128)S(1)}, u32[]{:S(2)}, u32[]{:S(2)}) async-start(f32[16,2,4]{2,1,0:T(2,128)} %broadcast_in_dim.164), calls=%async_computation.3 | async-start | bytes 32768 | tf_op jit(solution)/shard_map/all_to_all | solution.py:76
  86.3 7.4 %all-to-all-done.3 = f32[16,2,4]{2,1,0:T(2,128)S(1)} async-done(((f32[16,2,4]{2,1,0:T(2,128)}), f32[16,2,4]{2,1,0:T(2,128)S(1)}, u32[]{:S(2)}, u32[]{:S(2)}) %all-to-all-start.3) | async-done | bytes 544 | tf_op jit(solution)/shard_map/all_to_all | solution.py:76
  93.9 1.9 %collective-permute-start.2 = (f32[2,1]{1,0:T(2,128)S(1)}, f32[2,1]{1,0:T(2,128)S(1)}, u32[]{:S(2)}, u32[]{:S(2)}) collective-permute-start(f32[2,1]{1,0:T(2,128)S(1)} %slice.143), channel_id=1, source_target_pairs={{0,16},{16,32},{32,48},{48,64},{64,80},{80,96},{96,112},{112,128},... | collective-permute-start | bytes 32 | tf_op jit(solution)/shard_map/ppermute | solution.py:23
  95.8 0.2 select_reduce_fusion.5
  96.1 0.7 pad_maximum_fusion.2
  96.8 4.7 %collective-permute-done.2 = f32[2,1]{1,0:T(2,128)S(1)} collective-permute-done((f32[2,1]{1,0:T(2,128)S(1)}, f32[2,1]{1,0:T(2,128)S(1)}, u32[]{:S(2)}, u32[]{:S(2)}) %collective-permute-start.2) | collective-permute-done | bytes 40 | tf_op jit(solution)/shard_map/ppermute | solution.py:23
  101.5 0.6 pad_maximum_fusion.5
  (56 shorter events, 3.4 us)
Async XLA Ops:
  6.6 21.6 %copy-start.2 = (f32[96]{0:T(128)S(1)}, f32[96]{0:T(128)}, u32[]{:S(2)}) copy-start(f32[96]{0:T(128)} %param.18) | copy-start | bytes 1156
  6.6 22.1 %copy-start.3 = (f32[96]{0:T(128)S(1)}, f32[96]{0:T(128)}, u32[]{:S(2)}) copy-start(f32[96]{0:T(128)} %param.19) | copy-start | bytes 1156
  32.0 41.0 %copy-start = (f32[96,96]{1,0:T(8,128)S(1)}, f32[96,96]{1,0:T(8,128)}, u32[]{:S(2)}) copy-start(f32[96,96]{1,0:T(8,128)} %param.20) | copy-start | bytes 110596
  32.0 41.0 %copy-start.1 = (f32[96,96]{1,0:T(8,128)S(1)}, f32[96,96]{1,0:T(8,128)}, u32[]{:S(2)}) copy-start(f32[96,96]{1,0:T(8,128)} %param.21) | copy-start | bytes 110596
  53.0 13.5 %all-to-all-start.2 = ((f32[16,24,128]{2,1,0:T(8,128)}), f32[16,24,128]{2,1,0:T(8,128)S(1)}, u32[]{:S(2)}, u32[]{:S(2)}) async-start(f32[16,24,128]{2,1,0:T(8,128)} %broadcast_in_dim.163), calls=%async_computation.2 | async-start | bytes 393216 | tf_op jit(solution)/shard_map/all_to_all | solution.py:69
  66.9 9.4 %collective-permute-start.1 = (f32[96,96]{1,0:T(8,128)S(1)}, f32[96,96]{1,0:T(8,128)S(1)}, u32[]{:S(2)}, u32[]{:S(2)}) collective-permute-start(f32[96,96]{1,0:T(8,128)S(1)} %get-tuple-element.31), channel_id=1, source_target_pairs={{16,0},{32,16},{48,32},{64,48},{80,64},{96,80},{112,96},{128,112},... | collective-permute-start | bytes 110600 | tf_op jit(solution)/shard_map/ppermute | solution.py:23
  70.8 8.1 %collective-permute-start = (f32[104,96]{1,0:T(8,128)S(1)}, f32[104,96]{1,0:T(8,128)S(1)}, u32[]{:S(2)}, u32[]{:S(2)}) collective-permute-start(f32[104,96]{1,0:T(8,128)S(1)} %select_maximum_fusion.1), channel_id=1, source_target_pairs={{0,16},{16,32},{32,48},{48,64},{64,80},{80,96},{96,112},{112,128},... | collective-permute-start | bytes 119816 | tf_op jit(solution)/shard_map/ppermute | solution.py:23
  82.7 11.1 %all-to-all-start.3 = ((f32[16,2,4]{2,1,0:T(2,128)}), f32[16,2,4]{2,1,0:T(2,128)S(1)}, u32[]{:S(2)}, u32[]{:S(2)}) async-start(f32[16,2,4]{2,1,0:T(2,128)} %broadcast_in_dim.164), calls=%async_computation.3 | async-start | bytes 32768 | tf_op jit(solution)/shard_map/all_to_all | solution.py:76
  93.9 7.6 %collective-permute-start.2 = (f32[2,1]{1,0:T(2,128)S(1)}, f32[2,1]{1,0:T(2,128)S(1)}, u32[]{:S(2)}, u32[]{:S(2)}) collective-permute-start(f32[2,1]{1,0:T(2,128)S(1)} %slice.143), channel_id=1, source_target_pairs={{0,16},{16,32},{32,48},{48,64},{64,80},{80,96},{96,112},{112,128},... | collective-permute-start | bytes 32 | tf_op jit(solution)/shard_map/ppermute | solution.py:23

commit v13 on v10

--- a/solution.py
+++ b/solution.py
@@ -121,15 +121,14 @@
     arrival = arrival_slots(to_group)
 
     values = jnp.stack(
-        [
-            phases,
-            energy,
-            weights.astype(jnp.float32),
-            (target_slice * cell_count + cell_index).astype(jnp.float32),
-        ]
-    )
-    value_count = values.shape[0]
-    parts = split3(values)
+        [phases, energy, (target_slice * cell_count + cell_index).astype(jnp.float32)]
+    )
+    weight_row = weights[None]
+    parts = [
+        jnp.concatenate([part, weight_row if k == 0 else jnp.zeros_like(weight_row)])
+        for k, part in enumerate(split3(values))
+    ]
+    value_count = parts[0].shape[0]
     left = jnp.concatenate(
         [
             jnp.where(to_group[None], part[:, None, :], jnp.zeros((), jnp.bfloat16)).reshape(
@@ -150,8 +149,8 @@
 
     got_phase = got[0]
     got_energy = got[1]
-    arrived_weight = got[2]
-    combined = got[3].astype(jnp.int32)
+    arrived_weight = got[3]
+    combined = got[2].astype(jnp.int32)
     got_slice = combined // cell_count
     got_cell = combined % cell_count
     got_x = got_cell // grid_y

time: 101 us -> 102 us (level)
  no operation moved by 1% of the time
where the time goes in v13:
time: 102 us; the launch traced here: 101 us
  blocking collectives  52.7 us (52%)
  starting transfers between devices  13.5 us (13%)
  waiting for transfers between devices  12.1 us (12%)
  other arithmetic  11.2 us (11%)
  matrix products  8.03 us (8%)
  local copies, waits for them, and re-layouts  2.37 us (2%)
    all_to_all x1, blocking collectives, pb_sum(): mine = jnp.sum(lax.all_to_all(chunks, axis, 0, 0, tiled=True), axis=0)  20.1 us
    all_to_all x1, blocking collectives, body(): lax.all_to_all(send.reshape(value_count, groups, capacity), 'ta', split_a...  19.6 us
    all_to_all x1, blocking collectives, pb_sum(): lax.all_to_all(jnp.broadcast_to(mine[None], chunks.shape), axis, 0, 0, ti...  13 us
    ppermute x3, starting transfers between devices, shifted(): lax.ppermute(value, axis, [(source, source + steps) for source in range(l...  10 us
    all_to_all x1, waiting for transfers between devices, pb_sum_small(): return jnp.sum(lax.all_to_all(spread, axis, 0, 0, tiled=True), axis=0)  7.44 us
    ppermute x3, waiting for transfers between devices, shifted(): lax.ppermute(value, axis, [(source, source + steps) for source in range(l...  4.68 us
    dot_general x2, matrix products, pick(): picked = jnp.dot(table_parts, pick_row, preferred_element_type=jnp.float32)  4.35 us
    all_to_all x1, starting transfers between devices, pb_sum_small(): return jnp.sum(lax.all_to_all(spread, axis, 0, 0, tiled=True), axis=0)  3.49 us
  transfers between devices with their start and end apart: 4, of which 2 were waited for; matrix products, arithmetic and copies ran while one was open for 4% of the time, Pallas kernels for 0%

profile of v13, /device:TPU:8, one launch (start us, length us, event | category | flops | bytes accessed | tf_op | source)
XLA Modules:
  0.0 100.9 jit_solution(11670521179023124352)
XLA Ops:
  0.6 0.8 add_select_fusion.5
  1.4 1.2 %select_reduce_fusion.2 = (f32[4096]{0:T(1024)S(1)}, f32[4096]{0:T(1024)S(1)}) fusion(f32[96]{0:T(128)} %param.17, s32[4096]{0:T(1024)S(1)} %get-tuple-element.55, f32[96]{0:T(128)} %param.16, s32[4096]{0:T(1024)S(1)} %get-tuple-element.57), kind=kLoop, calls=%fused_computation.32 | loop fusion | flops 2351104 | bytes 66304 | tf_op jit(solution)/shard_map/reduce_sum | solution.py:28
  2.6 1.3 %multiply_add_fusion.4 = (f32[1,4096]{1,0:T(1,128)S(1)}, f32[1,4096]{1,0:T(1,128)S(1)}) fusion(f32[2,4096]{1,0:T(2,128)} %param.11, f32[1,4096]{1,0:T(1,128)S(1)} %bitcast.71), kind=kLoop, calls=%fused_computation.125 | loop fusion | flops 16384 | bytes 81920 | tf_op jit(solution)/shard_map/add | solution.py:118
  4.1 0.7 broadcast_in_dim.157
  4.8 0.8 iota_compare_fusion.14
  6.0 0.4 fusion.23
  6.4 0.3 broadcast_select_fusion.2
  6.7 1.2 %fusion.7 = f32[384,256]{1,0:T(8,128)S(1)} fusion(bf16[128,4096]{1,0:T(8,128)(2,1)S(1)} %bitcast.53, bf16[128,4096]{1,0:T(8,128)(2,1)S(1)} %bitcast.52, bf16[128,4096]{1,0:T(8,128)(2,1)S(1)} %bitcast.51, s32[4096]{0:T(1024)S(1)} %bitcast.73), kind=kOutput, calls=%fused_computation.10 | convolution fusion | flops 815792128 | bytes 3555328 | tf_op jit(solution)/shard_map/dot_general | solution.py:143
  8.1 19.6 %all_to_all.20 = f32[4,32,256]{2,0,1:T(4,128)S(1)} all-to-all(f32[4,32,256]{2,0,1:T(4,128)S(1)} %copy.30), channel_id=1, replica_groups=mesh['ta'=32,'pb'=16] {'ta'}, dimensions={1} | all-to-all | bytes 262144 | tf_op jit(solution)/shard_map/all_to_all | solution.py:146
  28.3 0.6 select_reduce_fusion
  28.8 0.6 select_reduce_fusion.1
  29.7 0.2 select_reduce_fusion.11
  30.0 2.1 %fusion.2 = f32[384,96]{0,1:T(8,128)S(1)} fusion(s32[8192]{0:T(1024)S(1)} %get-tuple-element.52, bf16[8192]{0:T(1024)(128)(2,1)S(1)} %convert_element_type.91, s32[8192]{0:T(1024)S(1)} %get-tuple-element.54), kind=kOutput, calls=%fused_computation.4 | convolution fusion | flops 611057664 | bytes 229376 | tf_op jit(solution)/shard_map/dot_general | solution.py:60
  32.2 20.1 %all_to_all.21 = f32[16,24,128]{2,1,0:T(8,128)S(1)} all-to-all(f32[16,24,128]{2,1,0:T(8,128)S(1)} %bitcast.54), channel_id=1, replica_groups=mesh['ta'=32,'pb'=16] {'pb'}, dimensions={0} | all-to-all | bytes 393216 | tf_op jit(solution)/shard_map/all_to_all | solution.py:68
  52.4 13.0 %all_to_all.22 = f32[16,24,128]{2,1,0:T(8,128)S(1)} all-to-all(f32[16,24,128]{2,1,0:T(8,128)S(1)} %broadcast_in_dim.167), channel_id=1, replica_groups=mesh['ta'=32,'pb'=16] {'pb'}, dimensions={0} | all-to-all | bytes 393216 | tf_op jit(solution)/shard_map/all_to_all | solution.py:69
  65.7 0.2 slice_reduce_fusion
  65.9 2.5 %collective-permute-start = (f32[104,96]{1,0:T(8,128)S(1)}, f32[104,96]{1,0:T(8,128)S(1)}, u32[]{:S(2)}, u32[]{:S(2)}) collective-permute-start(f32[104,96]{1,0:T(8,128)S(1)} %select_maximum_fusion.1), channel_id=1, source_target_pairs={{0,16},{16,32},{32,48},{48,64},{64,80},{80,96},{96,112},{112,128},... | collective-permute-start | bytes 119816 | tf_op jit(solution)/shard_map/ppermute | solution.py:23
  68.4 5.7 %collective-permute-start.1 = (f32[96,96]{1,0:T(8,128)S(1)}, f32[96,96]{1,0:T(8,128)S(1)}, u32[]{:S(2)}, u32[]{:S(2)}) collective-permute-start(f32[96,96]{1,0:T(8,128)S(1)} %get-tuple-element.31), channel_id=1, source_target_pairs={{16,0},{32,16},{48,32},{64,48},{80,64},{96,80},{112,96},{128,112},... | collective-permute-start | bytes 110600 | tf_op jit(solution)/shard_map/ppermute | solution.py:23
  74.2 2.8 %fusion.1 = f32[192,8192]{1,0:T(8,128)S(1)} fusion(s32[8192]{0:T(1024)S(1)} %get-tuple-element.52, bf16[384,96]{1,0:T(8,128)(2,1)S(1)} %get-tuple-element.29, bf16[384,96]{1,0:T(8,128)(2,1)S(1)} %get-tuple-element.28), kind=kOutput, calls=%fused_computation.3 | convolution fusion | flops 1211400192 | bytes 6471680 | tf_op jit(solution)/shard_map/dot_general | solution.py:213
  77.0 0.2 select_reduce_fusion.9
  77.3 1.5 %fusion.6 = f32[192,8192]{1,0:T(8,128)S(1)} fusion(s32[8192]{0:T(1024)S(1)} %get-tuple-element.22, bf16[192,96]{1,0:T(8,128)(2,1)S(1)} %get-tuple-element.43, bf16[192,96]{1,0:T(8,128)(2,1)S(1)} %get-tuple-element.42), kind=kOutput, calls=%fused_computation.8 | convolution fusion | flops 605700096 | bytes 6397952 | tf_op jit(solution)/shard_map/dot_general | solution.py:213
  78.8 1.4 %fusion.9 = (f32[8192]{0:T(1024)S(1)}, f32[8192]{0:T(1024)S(1)}) fusion(f32[192,8192]{1,0:T(8,128)S(1)} %fusion.6, s32[8192]{0:T(1024)S(1)} %get-tuple-element.54, f32[192,8192]{1,0:T(8,128)S(1)} %fusion.1), kind=kLoop, calls=%fused_computation.13 | loop fusion | flops 5488640 | bytes 12681216 | tf_op jit(solution)/shard_map/reduce_sum | solution.py:215
  80.2 0.3 multiply_sine_fusion
  80.6 0.2 select_reduce_fusion.7
  80.9 0.6 broadcast_in_dim.168
  81.5 3.5 %all-to-all-start.3 = ((f32[16,2,4]{2,1,0:T(2,128)}), f32[16,2,4]{2,1,0:T(2,128)S(1)}, u32[]{:S(2)}, u32[]{:S(2)}) async-start(f32[16,2,4]{2,1,0:T(2,128)} %broadcast_in_dim.168), calls=%async_computation.3 | async-start | bytes 32768 | tf_op jit(solution)/shard_map/all_to_all | solution.py:76
  85.1 7.4 %all-to-all-done.3 = f32[16,2,4]{2,1,0:T(2,128)S(1)} async-done(((f32[16,2,4]{2,1,0:T(2,128)}), f32[16,2,4]{2,1,0:T(2,128)S(1)}, u32[]{:S(2)}, u32[]{:S(2)}) %all-to-all-start.3) | async-done | bytes 544 | tf_op jit(solution)/shard_map/all_to_all | solution.py:76
  92.7 1.9 %collective-permute-start.2 = (f32[2,1]{1,0:T(2,128)S(1)}, f32[2,1]{1,0:T(2,128)S(1)}, u32[]{:S(2)}, u32[]{:S(2)}) collective-permute-start(f32[2,1]{1,0:T(2,128)S(1)} %slice.143), channel_id=1, source_target_pairs={{0,16},{16,32},{32,48},{48,64},{64,80},{80,96},{96,112},{112,128},... | collective-permute-start | bytes 32 | tf_op jit(solution)/shard_map/ppermute | solution.py:23
  94.6 0.2 select_reduce_fusion.5
  94.9 0.7 pad_maximum_fusion.2
  95.6 4.7 %collective-permute-done.2 = f32[2,1]{1,0:T(2,128)S(1)} collective-permute-done((f32[2,1]{1,0:T(2,128)S(1)}, f32[2,1]{1,0:T(2,128)S(1)}, u32[]{:S(2)}, u32[]{:S(2)}) %collective-permute-start.2) | collective-permute-done | bytes 40 | tf_op jit(solution)/shard_map/ppermute | solution.py:23
  100.3 0.6 pad_maximum_fusion.6
  (57 shorter events, 2.7 us)
Async XLA Ops:
  6.7 21.5 %copy-start.2 = (f32[96]{0:T(128)S(1)}, f32[96]{0:T(128)}, u32[]{:S(2)}) copy-start(f32[96]{0:T(128)} %param.19) | copy-start | bytes 1156
  6.7 22.1 %copy-start.3 = (f32[96]{0:T(128)S(1)}, f32[96]{0:T(128)}, u32[]{:S(2)}) copy-start(f32[96]{0:T(128)} %param.18) | copy-start | bytes 1156
  30.0 35.5 %copy-start = (f32[96,96]{1,0:T(8,128)S(1)}, f32[96,96]{1,0:T(8,128)}, u32[]{:S(2)}) copy-start(f32[96,96]{1,0:T(8,128)} %param.20) | copy-start | bytes 110596
  30.0 35.5 %copy-start.1 = (f32[96,96]{1,0:T(8,128)S(1)}, f32[96,96]{1,0:T(8,128)}, u32[]{:S(2)}) copy-start(f32[96,96]{1,0:T(8,128)} %param.21) | copy-start | bytes 110596
  65.9 11.3 %collective-permute-start = (f32[104,96]{1,0:T(8,128)S(1)}, f32[104,96]{1,0:T(8,128)S(1)}, u32[]{:S(2)}, u32[]{:S(2)}) collective-permute-start(f32[104,96]{1,0:T(8,128)S(1)} %select_maximum_fusion.1), channel_id=1, source_target_pairs={{0,16},{16,32},{32,48},{48,64},{64,80},{80,96},{96,112},{112,128},... | collective-permute-start | bytes 119816 | tf_op jit(solution)/shard_map/ppermute | solution.py:23
  68.4 8.8 %collective-permute-start.1 = (f32[96,96]{1,0:T(8,128)S(1)}, f32[96,96]{1,0:T(8,128)S(1)}, u32[]{:S(2)}, u32[]{:S(2)}) collective-permute-start(f32[96,96]{1,0:T(8,128)S(1)} %get-tuple-element.31), channel_id=1, source_target_pairs={{16,0},{32,16},{48,32},{64,48},{80,64},{96,80},{112,96},{128,112},... | collective-permute-start | bytes 110600 | tf_op jit(solution)/shard_map/ppermute | solution.py:23
  81.5 11.1 %all-to-all-start.3 = ((f32[16,2,4]{2,1,0:T(2,128)}), f32[16,2,4]{2,1,0:T(2,128)S(1)}, u32[]{:S(2)}, u32[]{:S(2)}) async-start(f32[16,2,4]{2,1,0:T(2,128)} %broadcast_in_dim.168), calls=%async_computation.3 | async-start | bytes 32768 | tf_op jit(solution)/shard_map/all_to_all | solution.py:76
  92.7 7.6 %collective-permute-start.2 = (f32[2,1]{1,0:T(2,128)S(1)}, f32[2,1]{1,0:T(2,128)S(1)}, u32[]{:S(2)}, u32[]{:S(2)}) collective-permute-start(f32[2,1]{1,0:T(2,128)S(1)} %slice.143), channel_id=1, source_target_pairs={{0,16},{16,32},{32,48},{48,64},{64,80},{80,96},{96,112},{112,128},... | collective-permute-start | bytes 32 | tf_op jit(solution)/shard_map/ppermute | solution.py:23

commit v14 on v10

--- a/solution.py
+++ b/solution.py
@@ -233,9 +233,18 @@
             cosine, sine_part = cosine0, sine0
             radiation = radiation + radiation0
         else:
-            cosine, sine_part, local_sums = local_bunching(got_phase)
+            harmonic_phase = HARM * got_phase
+            cosine = jnp.cos(harmonic_phase)
+            sine_part = jnp.sin(harmonic_phase)
             cosine, sine_part = lax.optimization_barrier((cosine, sine_part))
-            bunching = pb_sum_small(local_sums, "pb")
+            terms = jnp.stack([weighted * cosine, -weighted * sine_part])
+            spread = jnp.einsum(
+                "kcn,jn->kcj",
+                jnp.broadcast_to(terms[None], (splits,) + terms.shape),
+                select,
+                precision=lax.Precision.HIGHEST,
+            )
+            bunching = jnp.sum(lax.all_to_all(spread, "pb", 0, 0, tiled=True), axis=0)
             radiation = radiation + couple * bunching
         real_here = jnp.sum(select * radiation[0][:, None], axis=0)
         imag_here = jnp.sum(select * radiation[1][:, None], axis=0)

time: 101 us -> 103 us (1.020)
  matrix products: 8.01 us -> 9.94 us
    dot_general x0 -> x1, matrix products: none -> 1.92 us  [body(): jnp.einsum('kcn,jn->kcj', jnp.broadcast_to(terms[None], (splits,) + terms...]
where the time goes in v14:
time: 103 us
  blocking collectives  52.7 us (51%)
  starting transfers between devices  13.5 us (13%)
  waiting for transfers between devices  12.1 us (12%)
  other arithmetic  11.7 us (11%)
  matrix products  9.94 us (10%)
  local copies, waits for them, and re-layouts  1.73 us (2%)
    all_to_all x1, blocking collectives, pb_sum(): mine = jnp.sum(lax.all_to_all(chunks, axis, 0, 0, tiled=True), axis=0)  20.1 us
    all_to_all x1, blocking collectives, body(): lax.all_to_all(send.reshape(value_count, groups, capacity), 'ta', split_a...  19.6 us
    all_to_all x1, blocking collectives, pb_sum(): lax.all_to_all(jnp.broadcast_to(mine[None], chunks.shape), axis, 0, 0, ti...  13 us
    ppermute x3, starting transfers between devices, shifted(): lax.ppermute(value, axis, [(source, source + steps) for source in range(l...  10 us
    all_to_all x1, waiting for transfers between devices, body(): bunching = jnp.sum(lax.all_to_all(spread, 'pb', 0, 0, tiled=True), axis=0)  7.44 us
    ppermute x3, waiting for transfers between devices, shifted(): lax.ppermute(value, axis, [(source, source + steps) for source in range(l...  4.68 us
    dot_general x2, matrix products, pick(): picked = jnp.dot(table_parts, pick_row, preferred_element_type=jnp.float32)  4.35 us
    all_to_all x1, starting transfers between devices, body(): bunching = jnp.sum(lax.all_to_all(spread, 'pb', 0, 0, tiled=True), axis=0)  3.49 us
  transfers between devices with their start and end apart: 4, of which 2 were waited for; matrix products, arithmetic and copies ran while one was open for 4% of the time, Pallas kernels for 0%

profile of v14, /device:TPU:8, one launch (start us, length us, event | category | flops | bytes accessed | tf_op | source)
XLA Modules:
  0.0 102.7 jit_solution(13010086701427127488)
XLA Ops:
  0.6 0.7 stack.53
  1.3 0.8 iota_compare_fusion.14
  2.5 0.3 fusion.23
  2.9 0.8 add_select_fusion.5
  3.6 1.2 %select_reduce_fusion.2 = (f32[4096]{0:T(1024)S(1)}, f32[4096]{0:T(1024)S(1)}) fusion(f32[96]{0:T(128)} %param.17, s32[4096]{0:T(1024)S(1)} %get-tuple-element.51, f32[96]{0:T(128)} %param.16, s32[4096]{0:T(1024)S(1)} %get-tuple-element.53), kind=kLoop, calls=%fused_computation.32 | loop fusion | flops 2351104 | bytes 66304 | tf_op jit(solution)/shard_map/reduce_sum | solution.py:28
  4.9 1.3 %multiply_add_fusion.4 = (f32[1,4096]{1,0:T(1,128)S(1)}, f32[1,4096]{1,0:T(1,128)S(1)}) fusion(f32[2,4096]{1,0:T(2,128)} %param.11, f32[1,4096]{1,0:T(1,128)S(1)} %bitcast.79), kind=kLoop, calls=%fused_computation.127 | loop fusion | flops 16384 | bytes 81920 | tf_op jit(solution)/shard_map/add | solution.py:118
  6.3 0.3 broadcast_select_fusion.2
  6.6 1.2 %fusion.7 = f32[384,256]{1,0:T(8,128)S(1)} fusion(bf16[128,4096]{1,0:T(8,128)(2,1)S(1)} %bitcast.62, bf16[128,4096]{1,0:T(8,128)(2,1)S(1)} %bitcast.61, bf16[128,4096]{1,0:T(8,128)(2,1)S(1)} %bitcast.60, s32[4096]{0:T(1024)S(1)} %bitcast.82), kind=kOutput, calls=%fused_computation.10 | convolution fusion | flops 815792128 | bytes 3555328 | tf_op jit(solution)/shard_map/dot_general | solution.py:144
  8.0 19.6 %all_to_all.20 = f32[4,32,256]{2,0,1:T(4,128)S(1)} all-to-all(f32[4,32,256]{2,0,1:T(4,128)S(1)} %copy.28), channel_id=1, replica_groups=mesh['ta'=32,'pb'=16] {'ta'}, dimensions={1} | all-to-all | bytes 262144 | tf_op jit(solution)/shard_map/all_to_all | solution.py:147
  28.2 0.6 select_reduce_fusion
  28.7 0.6 select_reduce_fusion.1
  29.6 0.2 select_reduce_fusion.9
  29.9 2.1 %fusion.2 = f32[384,96]{0,1:T(8,128)S(1)} fusion(s32[8192]{0:T(1024)S(1)} %get-tuple-element.48, bf16[8192]{0:T(1024)(128)(2,1)S(1)} %convert_element_type.104, s32[8192]{0:T(1024)S(1)} %get-tuple-element.50), kind=kOutput, calls=%fused_computation.4 | convolution fusion | flops 611057664 | bytes 229376 | tf_op jit(solution)/shard_map/dot_general | solution.py:60
  32.1 20.1 %all_to_all.21 = f32[16,24,128]{2,1,0:T(8,128)S(1)} all-to-all(f32[16,24,128]{2,1,0:T(8,128)S(1)} %bitcast.63), channel_id=1, replica_groups=mesh['ta'=32,'pb'=16] {'pb'}, dimensions={0} | all-to-all | bytes 393216 | tf_op jit(solution)/shard_map/all_to_all | solution.py:68
  52.3 13.0 %all_to_all.22 = f32[16,24,128]{2,1,0:T(8,128)S(1)} all-to-all(f32[16,24,128]{2,1,0:T(8,128)S(1)} %broadcast_in_dim.161), channel_id=1, replica_groups=mesh['ta'=32,'pb'=16] {'pb'}, dimensions={0} | all-to-all | bytes 393216 | tf_op jit(solution)/shard_map/all_to_all | solution.py:69
  65.6 0.2 slice_reduce_fusion
  65.8 2.5 %collective-permute-start = (f32[104,96]{1,0:T(8,128)S(1)}, f32[104,96]{1,0:T(8,128)S(1)}, u32[]{:S(2)}, u32[]{:S(2)}) collective-permute-start(f32[104,96]{1,0:T(8,128)S(1)} %select_maximum_fusion.1), channel_id=1, source_target_pairs={{0,16},{16,32},{32,48},{48,64},{64,80},{80,96},{96,112},{112,128},... | collective-permute-start | bytes 119816 | tf_op jit(solution)/shard_map/ppermute | solution.py:23
  68.3 5.7 %collective-permute-start.1 = (f32[96,96]{1,0:T(8,128)S(1)}, f32[96,96]{1,0:T(8,128)S(1)}, u32[]{:S(2)}, u32[]{:S(2)}) collective-permute-start(f32[96,96]{1,0:T(8,128)S(1)} %get-tuple-element.28), channel_id=1, source_target_pairs={{16,0},{32,16},{48,32},{64,48},{80,64},{96,80},{112,96},{128,112},... | collective-permute-start | bytes 110600 | tf_op jit(solution)/shard_map/ppermute | solution.py:23
  74.1 2.8 %fusion.1 = f32[192,8192]{1,0:T(8,128)S(1)} fusion(s32[8192]{0:T(1024)S(1)} %get-tuple-element.48, bf16[384,96]{1,0:T(8,128)(2,1)S(1)} %get-tuple-element.26, bf16[384,96]{1,0:T(8,128)(2,1)S(1)} %get-tuple-element.25), kind=kOutput, calls=%fused_computation.3 | convolution fusion | flops 1211400192 | bytes 6471680 | tf_op jit(solution)/shard_map/dot_general | solution.py:214
  76.9 0.2 select_reduce_fusion.7
  77.2 1.5 %fusion.6 = f32[192,8192]{1,0:T(8,128)S(1)} fusion(s32[8192]{0:T(1024)S(1)} %get-tuple-element.19, bf16[192,96]{1,0:T(8,128)(2,1)S(1)} %get-tuple-element.40, bf16[192,96]{1,0:T(8,128)(2,1)S(1)} %get-tuple-element.39), kind=kOutput, calls=%fused_computation.8 | convolution fusion | flops 605700096 | bytes 6397952 | tf_op jit(solution)/shard_map/dot_general | solution.py:214
  78.7 1.4 %fusion.9 = (f32[8192]{0:T(1024)S(1)}, f32[8192]{0:T(1024)S(1)}) fusion(f32[192,8192]{1,0:T(8,128)S(1)} %fusion.6, s32[8192]{0:T(1024)S(1)} %get-tuple-element.50, f32[192,8192]{1,0:T(8,128)S(1)} %fusion.1), kind=kLoop, calls=%fused_computation.13 | loop fusion | flops 5488640 | bytes 12681216 | tf_op jit(solution)/shard_map/reduce_sum | solution.py:216
  80.1 0.3 multiply_sine_fusion
  80.6 1.9 %fusion.26 = f32[16,2,4]{0,2,1:T(4,128)S(1)} fusion(f32[2,8192]{1,0:T(2,128)S(1)} %pad_maximum_fusion.2, s32[8192]{0:T(1024)S(1)} %get-tuple-element.20), kind=kOutput, calls=%fused_computation.46 | convolution fusion | flops 12615680 | bytes 98816 | tf_op jit(solution)/shard_map/kcn,jn->kcj/dot_general | solution.py:241
  82.5 0.7 copy.32
  83.3 3.5 %all-to-all-start.3 = ((f32[16,2,4]{2,1,0:T(2,128)}), f32[16,2,4]{2,1,0:T(2,128)S(1)}, u32[]{:S(2)}, u32[]{:S(2)}) async-start(f32[16,2,4]{2,1,0:T(2,128)} %copy.32), calls=%async_computation.3 | async-start | bytes 32768 | tf_op jit(solution)/shard_map/all_to_all | solution.py:247
  86.9 7.4 %all-to-all-done.3 = f32[16,2,4]{2,1,0:T(2,128)S(1)} async-done(((f32[16,2,4]{2,1,0:T(2,128)}), f32[16,2,4]{2,1,0:T(2,128)S(1)}, u32[]{:S(2)}, u32[]{:S(2)}) %all-to-all-start.3) | async-done | bytes 544 | tf_op jit(solution)/shard_map/all_to_all | solution.py:247
  94.5 1.9 %collective-permute-start.2 = (f32[2,1]{1,0:T(2,128)S(1)}, f32[2,1]{1,0:T(2,128)S(1)}, u32[]{:S(2)}, u32[]{:S(2)}) collective-permute-start(f32[2,1]{1,0:T(2,128)S(1)} %slice.143), channel_id=1, source_target_pairs={{0,16},{16,32},{32,48},{48,64},{64,80},{80,96},{96,112},{112,128},... | collective-permute-start | bytes 32 | tf_op jit(solution)/shard_map/ppermute | solution.py:23
  96.4 0.2 select_reduce_fusion.5
  96.7 0.7 pad_maximum_fusion.3
  97.4 4.7 %collective-permute-done.2 = f32[2,1]{1,0:T(2,128)S(1)} collective-permute-done((f32[2,1]{1,0:T(2,128)S(1)}, f32[2,1]{1,0:T(2,128)S(1)}, u32[]{:S(2)}, u32[]{:S(2)}) %collective-permute-start.2) | collective-permute-done | bytes 40 | tf_op jit(solution)/shard_map/ppermute | solution.py:23
  102.1 0.6 pad_maximum_fusion.5
  (55 shorter events, 2.6 us)
Async XLA Ops:
  6.6 21.6 %copy-start.2 = (f32[96]{0:T(128)S(1)}, f32[96]{0:T(128)}, u32[]{:S(2)}) copy-start(f32[96]{0:T(128)} %param.19) | copy-start | bytes 1156
  6.6 22.1 %copy-start.3 = (f32[96]{0:T(128)S(1)}, f32[96]{0:T(128)}, u32[]{:S(2)}) copy-start(f32[96]{0:T(128)} %param.18) | copy-start | bytes 1156
  29.9 35.5 %copy-start = (f32[96,96]{1,0:T(8,128)S(1)}, f32[96,96]{1,0:T(8,128)}, u32[]{:S(2)}) copy-start(f32[96,96]{1,0:T(8,128)} %param.20) | copy-start | bytes 110596
  29.9 35.5 %copy-start.1 = (f32[96,96]{1,0:T(8,128)S(1)}, f32[96,96]{1,0:T(8,128)}, u32[]{:S(2)}) copy-start(f32[96,96]{1,0:T(8,128)} %param.21) | copy-start | bytes 110596
  65.8 11.3 %collective-permute-start = (f32[104,96]{1,0:T(8,128)S(1)}, f32[104,96]{1,0:T(8,128)S(1)}, u32[]{:S(2)}, u32[]{:S(2)}) collective-permute-start(f32[104,96]{1,0:T(8,128)S(1)} %select_maximum_fusion.1), channel_id=1, source_target_pairs={{0,16},{16,32},{32,48},{48,64},{64,80},{80,96},{96,112},{112,128},... | collective-permute-start | bytes 119816 | tf_op jit(solution)/shard_map/ppermute | solution.py:23
  68.3 8.8 %collective-permute-start.1 = (f32[96,96]{1,0:T(8,128)S(1)}, f32[96,96]{1,0:T(8,128)S(1)}, u32[]{:S(2)}, u32[]{:S(2)}) collective-permute-start(f32[96,96]{1,0:T(8,128)S(1)} %get-tuple-element.28), channel_id=1, source_target_pairs={{16,0},{32,16},{48,32},{64,48},{80,64},{96,80},{112,96},{128,112},... | collective-permute-start | bytes 110600 | tf_op jit(solution)/shard_map/ppermute | solution.py:23
  83.3 11.1 %all-to-all-start.3 = ((f32[16,2,4]{2,1,0:T(2,128)}), f32[16,2,4]{2,1,0:T(2,128)S(1)}, u32[]{:S(2)}, u32[]{:S(2)}) async-start(f32[16,2,4]{2,1,0:T(2,128)} %copy.32), calls=%async_computation.3 | async-start | bytes 32768 | tf_op jit(solution)/shard_map/all_to_all | solution.py:247
  94.5 7.6 %collective-permute-start.2 = (f32[2,1]{1,0:T(2,128)S(1)}, f32[2,1]{1,0:T(2,128)S(1)}, u32[]{:S(2)}, u32[]{:S(2)}) collective-permute-start(f32[2,1]{1,0:T(2,128)S(1)} %slice.143), channel_id=1, source_target_pairs={{0,16},{16,32},{32,48},{48,64},{64,80},{80,96},{96,112},{112,128},... | collective-permute-start | bytes 32 | tf_op jit(solution)/shard_map/ppermute | solution.py:23

commit v15 on v11

--- a/solution.py
+++ b/solution.py
@@ -199,7 +199,7 @@
     radiation0 = couple * bunching0
     last_lanes = jnp.pad(radiation0[:, -1:].reshape(1, 2), ((0, grid_x - 1), (0, lanes - grid_y - 2)))
     halo_below = shifted(jnp.concatenate([density[SL_DEV - 1], last_lanes], axis=1), "ta", 1)
-    above = shifted(density[0], "ta", -1)
+    above = shifted(jnp.pad(density[0], ((0, 0), (0, lanes - grid_y))), "ta", -1)[:, :grid_y]
     empty = jnp.zeros((1, grid_x, grid_y), jnp.float32)
     force_map = stencil(jnp.concatenate([empty, density, empty]), along_coeff, across_coeff)
 

time: 102 us -> 102 us (level)
  no operation moved by 1% of the time
where the time goes in v15:
time: 102 us; the launch traced here: 101 us
  blocking collectives  52.7 us (52%)
  starting transfers between devices  13.5 us (13%)
  waiting for transfers between devices  12.1 us (12%)
  other arithmetic  11.9 us (12%)
  matrix products  8.02 us (8%)
  local copies, waits for them, and re-layouts  1.7 us (2%)
    all_to_all x1, blocking collectives, pb_sum(): mine = jnp.sum(lax.all_to_all(chunks, axis, 0, 0, tiled=True), axis=0)  20.1 us
    all_to_all x1, blocking collectives, body(): lax.all_to_all(send.reshape(value_count, groups, capacity), 'ta', split_a...  19.6 us
    all_to_all x1, blocking collectives, pb_sum(): lax.all_to_all(jnp.broadcast_to(mine[None], chunks.shape), axis, 0, 0, ti...  13 us
    ppermute x3, starting transfers between devices, shifted(): lax.ppermute(value, axis, [(source, source + steps) for source in range(l...  10 us
    all_to_all x1, waiting for transfers between devices, pb_sum_small(): return jnp.sum(lax.all_to_all(spread, axis, 0, 0, tiled=True), axis=0)  7.38 us
    ppermute x3, waiting for transfers between devices, shifted(): lax.ppermute(value, axis, [(source, source + steps) for source in range(l...  4.68 us
    dot_general x2, matrix products, pick(): picked = jnp.dot(table_parts, pick_row, preferred_element_type=jnp.float32)  4.36 us
    all_to_all x1, starting transfers between devices, pb_sum_small(): return jnp.sum(lax.all_to_all(spread, axis, 0, 0, tiled=True), axis=0)  3.49 us
  transfers between devices with their start and end apart: 4, of which 2 were waited for; matrix products, arithmetic and copies ran while one was open for 4% of the time, Pallas kernels for 0%

profile of v15, /device:TPU:8, one launch (start us, length us, event | category | flops | bytes accessed | tf_op | source)
XLA Modules:
  0.0 100.9 jit_solution(1748905234010701138)
XLA Ops:
  0.6 0.7 stack.53
  1.3 0.8 iota_compare_fusion.14
  2.5 0.3 fusion.23
  2.9 0.8 add_select_fusion.5
  3.6 1.2 %select_reduce_fusion.2 = (f32[4096]{0:T(1024)S(1)}, f32[4096]{0:T(1024)S(1)}) fusion(f32[96]{0:T(128)} %param.17, s32[4096]{0:T(1024)S(1)} %get-tuple-element.55, f32[96]{0:T(128)} %param.16, s32[4096]{0:T(1024)S(1)} %get-tuple-element.57), kind=kLoop, calls=%fused_computation.32 | loop fusion | flops 2351104 | bytes 66304 | tf_op jit(solution)/shard_map/reduce_sum | solution.py:28
  4.9 1.3 %multiply_add_fusion.4 = (f32[1,4096]{1,0:T(1,128)S(1)}, f32[1,4096]{1,0:T(1,128)S(1)}) fusion(f32[2,4096]{1,0:T(2,128)} %param.11, f32[1,4096]{1,0:T(1,128)S(1)} %bitcast.72), kind=kLoop, calls=%fused_computation.125 | loop fusion | flops 16384 | bytes 81920 | tf_op jit(solution)/shard_map/add | solution.py:118
  6.3 0.3 broadcast_select_fusion.2
  6.6 1.2 %fusion.7 = f32[384,256]{1,0:T(8,128)S(1)} fusion(bf16[128,4096]{1,0:T(8,128)(2,1)S(1)} %bitcast.54, bf16[128,4096]{1,0:T(8,128)(2,1)S(1)} %bitcast.53, bf16[128,4096]{1,0:T(8,128)(2,1)S(1)} %bitcast.52, s32[4096]{0:T(1024)S(1)} %bitcast.75), kind=kOutput, calls=%fused_computation.10 | convolution fusion | flops 815792128 | bytes 3555328 | tf_op jit(solution)/shard_map/dot_general | solution.py:144
  8.0 19.6 %all_to_all.20 = f32[4,32,256]{2,0,1:T(4,128)S(1)} all-to-all(f32[4,32,256]{2,0,1:T(4,128)S(1)} %copy.30), channel_id=1, replica_groups=mesh['ta'=32,'pb'=16] {'ta'}, dimensions={1} | all-to-all | bytes 262144 | tf_op jit(solution)/shard_map/all_to_all | solution.py:147
  28.2 0.6 select_reduce_fusion
  28.7 0.6 select_reduce_fusion.1
  29.6 0.2 select_reduce_fusion.11
  29.9 2.1 %fusion.2 = f32[384,96]{0,1:T(8,128)S(1)} fusion(s32[8192]{0:T(1024)S(1)} %get-tuple-element.52, bf16[8192]{0:T(1024)(128)(2,1)S(1)} %convert_element_type.106, s32[8192]{0:T(1024)S(1)} %get-tuple-element.54), kind=kOutput, calls=%fused_computation.4 | convolution fusion | flops 611057664 | bytes 229376 | tf_op jit(solution)/shard_map/dot_general | solution.py:60
  32.1 20.1 %all_to_all.21 = f32[16,24,128]{2,1,0:T(8,128)S(1)} all-to-all(f32[16,24,128]{2,1,0:T(8,128)S(1)} %bitcast.55), channel_id=1, replica_groups=mesh['ta'=32,'pb'=16] {'pb'}, dimensions={0} | all-to-all | bytes 393216 | tf_op jit(solution)/shard_map/all_to_all | solution.py:68
  52.3 13.0 %all_to_all.22 = f32[16,24,128]{2,1,0:T(8,128)S(1)} all-to-all(f32[16,24,128]{2,1,0:T(8,128)S(1)} %broadcast_in_dim.163), channel_id=1, replica_groups=mesh['ta'=32,'pb'=16] {'pb'}, dimensions={0} | all-to-all | bytes 393216 | tf_op jit(solution)/shard_map/all_to_all | solution.py:69
  65.6 0.2 slice_reduce_fusion
  65.9 2.5 %collective-permute-start = (f32[96,128]{1,0:T(8,128)S(1)}, f32[96,128]{1,0:T(8,128)S(1)}, u32[]{:S(2)}, u32[]{:S(2)}) collective-permute-start(f32[96,128]{1,0:T(8,128)S(1)} %select_maximum_fusion.1), channel_id=1, source_target_pairs={{0,16},{16,32},{32,48},{48,64},{64,80},{80,96},{96,112},{112,128},... | collective-permute-start | bytes 147464 | tf_op jit(solution)/shard_map/ppermute | solution.py:23
  68.4 5.7 %collective-permute-start.1 = (f32[96,128]{1,0:T(8,128)S(1)}, f32[96,128]{1,0:T(8,128)S(1)}, u32[]{:S(2)}, u32[]{:S(2)}) collective-permute-start(f32[96,128]{1,0:T(8,128)S(1)} %pad.26), channel_id=1, source_target_pairs={{16,0},{32,16},{48,32},{64,48},{80,64},{96,80},{112,96},{128,112},... | collective-permute-start | bytes 147464 | tf_op jit(solution)/shard_map/ppermute | solution.py:23
  74.1 2.8 %fusion.1 = f32[192,8192]{1,0:T(8,128)S(1)} fusion(s32[8192]{0:T(1024)S(1)} %get-tuple-element.52, bf16[384,96]{1,0:T(8,128)(2,1)S(1)} %get-tuple-element.29, bf16[384,96]{1,0:T(8,128)(2,1)S(1)} %get-tuple-element.28), kind=kOutput, calls=%fused_computation.3 | convolution fusion | flops 1211400192 | bytes 6471680 | tf_op jit(solution)/shard_map/dot_general | solution.py:214
  77.0 0.2 select_reduce_fusion.9
  77.3 1.5 %fusion.6 = f32[192,8192]{1,0:T(8,128)S(1)} fusion(s32[8192]{0:T(1024)S(1)} %get-tuple-element.22, bf16[192,96]{1,0:T(8,128)(2,1)S(1)} %get-tuple-element.43, bf16[192,96]{1,0:T(8,128)(2,1)S(1)} %get-tuple-element.42), kind=kOutput, calls=%fused_computation.8 | convolution fusion | flops 605700096 | bytes 6397952 | tf_op jit(solution)/shard_map/dot_general | solution.py:214
  78.8 1.4 %fusion.9 = (f32[8192]{0:T(1024)S(1)}, f32[8192]{0:T(1024)S(1)}) fusion(f32[192,8192]{1,0:T(8,128)S(1)} %fusion.6, s32[8192]{0:T(1024)S(1)} %get-tuple-element.54, f32[192,8192]{1,0:T(8,128)S(1)} %fusion.1), kind=kLoop, calls=%fused_computation.13 | loop fusion | flops 5488640 | bytes 12681216 | tf_op jit(solution)/shard_map/reduce_sum | solution.py:216
  80.2 0.3 multiply_sine_fusion
  80.6 0.2 select_reduce_fusion.7
  80.8 0.6 broadcast_in_dim.164
  81.5 3.5 %all-to-all-start.3 = ((f32[16,2,4]{2,1,0:T(2,128)}), f32[16,2,4]{2,1,0:T(2,128)S(1)}, u32[]{:S(2)}, u32[]{:S(2)}) async-start(f32[16,2,4]{2,1,0:T(2,128)} %broadcast_in_dim.164), calls=%async_computation.3 | async-start | bytes 32768 | tf_op jit(solution)/shard_map/all_to_all | solution.py:76
  85.1 7.4 %all-to-all-done.3 = f32[16,2,4]{2,1,0:T(2,128)S(1)} async-done(((f32[16,2,4]{2,1,0:T(2,128)}), f32[16,2,4]{2,1,0:T(2,128)S(1)}, u32[]{:S(2)}, u32[]{:S(2)}) %all-to-all-start.3) | async-done | bytes 544 | tf_op jit(solution)/shard_map/all_to_all | solution.py:76
  92.7 1.9 %collective-permute-start.2 = (f32[2,1]{1,0:T(2,128)S(1)}, f32[2,1]{1,0:T(2,128)S(1)}, u32[]{:S(2)}, u32[]{:S(2)}) collective-permute-start(f32[2,1]{1,0:T(2,128)S(1)} %slice.147), channel_id=1, source_target_pairs={{0,16},{16,32},{32,48},{48,64},{64,80},{80,96},{96,112},{112,128},... | collective-permute-start | bytes 32 | tf_op jit(solution)/shard_map/ppermute | solution.py:23
  94.6 0.2 select_reduce_fusion.5
  94.9 0.7 pad_maximum_fusion.2
  95.6 4.7 %collective-permute-done.2 = f32[2,1]{1,0:T(2,128)S(1)} collective-permute-done((f32[2,1]{1,0:T(2,128)S(1)}, f32[2,1]{1,0:T(2,128)S(1)}, u32[]{:S(2)}, u32[]{:S(2)}) %collective-permute-start.2) | collective-permute-done | bytes 40 | tf_op jit(solution)/shard_map/ppermute | solution.py:23
  100.3 0.6 pad_maximum_fusion.5
  (55 shorter events, 2.7 us)
Async XLA Ops:
  6.6 21.6 %copy-start.2 = (f32[96]{0:T(128)S(1)}, f32[96]{0:T(128)}, u32[]{:S(2)}) copy-start(f32[96]{0:T(128)} %param.19) | copy-start | bytes 1156
  6.6 22.1 %copy-start.3 = (f32[96]{0:T(128)S(1)}, f32[96]{0:T(128)}, u32[]{:S(2)}) copy-start(f32[96]{0:T(128)} %param.18) | copy-start | bytes 1156
  29.9 35.5 %copy-start = (f32[96,96]{1,0:T(8,128)S(1)}, f32[96,96]{1,0:T(8,128)}, u32[]{:S(2)}) copy-start(f32[96,96]{1,0:T(8,128)} %param.20) | copy-start | bytes 110596
  29.9 35.5 %copy-start.1 = (f32[96,96]{1,0:T(8,128)S(1)}, f32[96,96]{1,0:T(8,128)}, u32[]{:S(2)}) copy-start(f32[96,96]{1,0:T(8,128)} %param.21) | copy-start | bytes 110596
  65.9 11.3 %collective-permute-start = (f32[96,128]{1,0:T(8,128)S(1)}, f32[96,128]{1,0:T(8,128)S(1)}, u32[]{:S(2)}, u32[]{:S(2)}) collective-permute-start(f32[96,128]{1,0:T(8,128)S(1)} %select_maximum_fusion.1), channel_id=1, source_target_pairs={{0,16},{16,32},{32,48},{48,64},{64,80},{80,96},{96,112},{112,128},... | collective-permute-start | bytes 147464 | tf_op jit(solution)/shard_map/ppermute | solution.py:23
  68.4 8.8 %collective-permute-start.1 = (f32[96,128]{1,0:T(8,128)S(1)}, f32[96,128]{1,0:T(8,128)S(1)}, u32[]{:S(2)}, u32[]{:S(2)}) collective-permute-start(f32[96,128]{1,0:T(8,128)S(1)} %pad.26), channel_id=1, source_target_pairs={{16,0},{32,16},{48,32},{64,48},{80,64},{96,80},{112,96},{128,112},... | collective-permute-start | bytes 147464 | tf_op jit(solution)/shard_map/ppermute | solution.py:23
  81.5 11.1 %all-to-all-start.3 = ((f32[16,2,4]{2,1,0:T(2,128)}), f32[16,2,4]{2,1,0:T(2,128)S(1)}, u32[]{:S(2)}, u32[]{:S(2)}) async-start(f32[16,2,4]{2,1,0:T(2,128)} %broadcast_in_dim.164), calls=%async_computation.3 | async-start | bytes 32768 | tf_op jit(solution)/shard_map/all_to_all | solution.py:76
  92.7 7.6 %collective-permute-start.2 = (f32[2,1]{1,0:T(2,128)S(1)}, f32[2,1]{1,0:T(2,128)S(1)}, u32[]{:S(2)}, u32[]{:S(2)}) collective-permute-start(f32[2,1]{1,0:T(2,128)S(1)} %slice.147), channel_id=1, source_target_pairs={{0,16},{16,32},{32,48},{48,64},{64,80},{80,96},{96,112},{112,128},... | collective-permute-start | bytes 32 | tf_op jit(solution)/shard_map/ppermute | solution.py:23
